TPU v7x, 512 devices: a whole 4x8x8 slice. The times are simulated.
512 devices in a mesh: seq: 32 (over x, z_lo, core), tp: 16 (over y, z_hi).
Axes of the slice: x: 4, y: 8, z: 8 (z_hi: 2, z_lo: 4; z = z_hi * 4 + z_lo), core: 2. Of those that a mesh axis runs over, the one named last changes fastest.
Arguments:
- q_in: bfloat16 [16384, 4096], P('seq', 'tp'), may hold values from -40 to 40
- k_in: bfloat16 [16384, 4096], P('seq', 'tp'), may hold values from -40 to 40
- v_in: bfloat16 [16384, 4096], P('seq', 'tp'), may hold values from -6 to 6
- q_gain: float32 [4096], P('tp'), may hold values from 0.1 to 1.9
- k_gain: float32 [4096], P('tp'), may hold values from 0.1 to 1.9
- d_out: bfloat16 [16384, 4096], P('seq', 'tp'), may hold values from -6 to 6
- counts: int32 [64], replicated, may hold values from 128 to 256, as said below
- windows: int32 [32], P('tp'), may hold values from 1 to 2
Outputs:
- attn_out: bfloat16 [16384, 4096], P('seq', 'tp')
- grad_q: bfloat16 [16384, 4096], P('seq', 'tp')
- grad_k: bfloat16 [16384, 4096], P('seq', 'tp')
- grad_v: bfloat16 [16384, 4096], P('seq', 'tp')
Inputs may be any that keep to these rules, and one draw needn't show every extreme that they name: `counts`: each count is a multiple of 128; slots at or beyond a frame's count are padding; some frame is full.
All inputs are finite; a program needn't handle non-finite values.
Results may differ from a plain program's by a relative error of at most 0.02.
The roundings to bfloat16 on the way count: a program that leaves them out, or rounds other values in their place, can miss the bound.
Values may be sent and summed in bfloat16 or wider, within the bound.
No kernel may reach another device: no remote copies, remote signals or barrier semaphores. Data moves between devices by JAX's collectives and lax.ppermute only.
A program may use at most 64 MiB of HBM per device.

v0:
```python
import jax
import jax.numpy as jnp
from jax import lax
from jax.sharding import PartitionSpec as P

HD = 128
CAP = 256
F_DEV = 2
WIDTH = 4096


EPS = 1e-06
NEG = -1e30


def shifted(block, axis, distance):
    devices = range(lax.axis_size(axis))
    route = [(i - distance, i) for i in devices if i - distance in devices]
    return lax.ppermute(block, axis, route)


def from_root(x, axis, root):
    mine = lax.axis_index(axis) == root
    return lax.psum(jnp.where(mine, x, jnp.zeros_like(x)), axis)


def stack_offsets(padded, before, count):
    blocks = [padded[before - offset : before - offset + count] for offset in range(before + 1)]
    return jnp.concatenate(blocks, axis=1)


def fold_offsets(grads, before, count, slots):
    result = jnp.zeros((before + count, slots) + grads.shape[2:], jnp.float32)
    for offset in range(before + 1):
        piece = grads[:, offset * slots : (offset + 1) * slots]
        result = result + jnp.pad(piece, ((before - offset, offset), (0, 0), (0, 0)))
    return result


def attend(q_head, g_head, k_set, v_set, visible, row_live):
    factor = HD ** (-0.5)
    scores = jnp.einsum("fqd,fkd->fqk", q_head, k_set, preferred_element_type=jnp.float32) * factor
    scores = jnp.where(visible[:, None, :], scores, NEG)
    row_max = jnp.max(scores, axis=2, keepdims=True)
    row_sum = jnp.sum(jnp.exp(scores - row_max), axis=2, keepdims=True)
    lse = row_max + jnp.log(row_sum)
    prob_wide = jnp.exp(scores - lse)
    prob = prob_wide.astype(jnp.bfloat16)
    out_wide = jnp.einsum("fqk,fkd->fqd", prob, v_set, preferred_element_type=jnp.float32)
    attn = lax.optimization_barrier(
        jnp.where(row_live[:, :, None], out_wide, 0.0).astype(jnp.bfloat16)
    )
    delta = jnp.sum(g_head.astype(jnp.float32) * attn.astype(jnp.float32), axis=2)
    dprob = jnp.einsum("fqd,fkd->fqk", g_head, v_set, preferred_element_type=jnp.float32)
    dscore = (prob_wide * (dprob - delta[:, :, None]) * factor).astype(jnp.bfloat16)
    grad_qh = jnp.einsum("fqk,fkd->fqd", dscore, k_set, preferred_element_type=jnp.float32)
    grad_kh = jnp.einsum("fqk,fqd->fkd", dscore, q_head, preferred_element_type=jnp.float32)
    grad_vh = jnp.einsum("fqk,fqd->fkd", prob, g_head, preferred_element_type=jnp.float32)
    return (attn, lse[:, :, 0], delta, grad_qh, grad_kh, grad_vh)


def on_device(q_in, k_in, v_in, q_gain, k_gain, d_out, counts, windows):
    row_count, local_width = q_in.shape
    local_heads = local_width // HD
    device = lax.axis_index("seq")
    q_float = q_in.astype(jnp.float32)
    k_float = k_in.astype(jnp.float32)
    q_power, k_power = lax.psum(
        (jnp.sum(q_float * q_float, axis=1), jnp.sum(k_float * k_float, axis=1)), "tp"
    )
    q_rinv = lax.rsqrt(q_power / WIDTH + EPS)[:, None]
    k_rinv = lax.rsqrt(k_power / WIDTH + EPS)[:, None]
    q_norm = (q_float * q_rinv * q_gain).astype(jnp.bfloat16)
    k_norm = (k_float * k_rinv * k_gain).astype(jnp.bfloat16)
    padded_counts = jnp.concatenate([jnp.zeros((F_DEV,), jnp.int32), counts])
    near_counts = lax.dynamic_slice_in_dim(padded_counts, device * F_DEV, 2 * F_DEV)
    slot_index = jnp.arange(CAP, dtype=jnp.int32)
    near_live = slot_index[None, :] < near_counts[:, None]
    row_live = near_live[F_DEV:]
    grad_mask = jnp.where(row_live.reshape(row_count)[:, None], d_out, jnp.zeros_like(d_out))
    halo_k, halo_v = shifted((k_norm, v_in), "seq", 1)
    anchor_k, anchor_v = (from_root(k_norm[:CAP], "seq", 0), from_root(v_in[:CAP], "seq", 0))
    k_near = jnp.concatenate([halo_k, k_norm], axis=0).reshape(2 * F_DEV, CAP, local_width)
    v_near = jnp.concatenate([halo_v, v_in], axis=0).reshape(2 * F_DEV, CAP, local_width)
    k_set = jnp.concatenate(
        [
            stack_offsets(k_near, F_DEV, F_DEV),
            jnp.broadcast_to(anchor_k[None], (F_DEV, CAP, local_width)),
        ],
        axis=1,
    )
    v_set = jnp.concatenate(
        [
            stack_offsets(v_near, F_DEV, F_DEV),
            jnp.broadcast_to(anchor_v[None], (F_DEV, CAP, local_width)),
        ],
        axis=1,
    )

    def to_heads(value):
        return value.reshape(value.shape[0], value.shape[1], local_heads, HD).transpose(2, 0, 1, 3)

    def from_heads(value):
        return value.transpose(1, 2, 0, 3).reshape(value.shape[1], value.shape[2], local_heads * HD)

    frame_local = jnp.arange(F_DEV, dtype=jnp.int32)
    offsets = jnp.arange((F_DEV + 1) * CAP, dtype=jnp.int32) // CAP
    live_stack = stack_offsets(near_live[:, :, None], F_DEV, F_DEV)[:, :, 0]
    reach = device * F_DEV + frame_local[:, None] - offsets[None, :] >= 0
    within = offsets[None, None, :] <= windows[:, None, None]
    anchor_ok = device * F_DEV + frame_local[None, :] - windows[:, None] > 0
    anchor_live = slot_index < counts[0]
    visible = jnp.concatenate(
        [(live_stack & reach)[None] & within, anchor_ok[:, :, None] & anchor_live[None, None, :]],
        axis=2,
    )

    def per_head(items):
        q_head, g_head, k_head, v_head, seen = items
        return attend(q_head, g_head, k_head, v_head, seen, row_live)

    q_heads = to_heads(q_norm.reshape(F_DEV, CAP, local_width))
    g_heads = to_heads(grad_mask.reshape(F_DEV, CAP, local_width))
    attn_h, lse_h, delta_h, grad_qh, grad_kh, grad_vh = lax.map(
        per_head, (q_heads, g_heads, to_heads(k_set), to_heads(v_set), visible)
    )
    attn_out = from_heads(attn_h).reshape(row_count, local_width)
    grad_qn = from_heads(grad_qh).reshape(row_count, local_width)
    grad_k_all = from_heads(grad_kh)
    grad_v_all = from_heads(grad_vh)
    split = (F_DEV + 1) * CAP
    grad_k_near = fold_offsets(grad_k_all[:, :split], F_DEV, F_DEV, CAP)
    grad_v_near = fold_offsets(grad_v_all[:, :split], F_DEV, F_DEV, CAP)
    grad_k_anchor = jnp.sum(grad_k_all[:, split:], axis=0)
    grad_v_anchor = jnp.sum(grad_v_all[:, split:], axis=0)
    back_k, back_v = shifted((grad_k_near[:F_DEV], grad_v_near[:F_DEV]), "seq", -1)
    grad_k_own = grad_k_near[F_DEV:] + back_k
    grad_v_own = grad_v_near[F_DEV:] + back_v
    anchor_gk, anchor_gv = lax.psum((grad_k_anchor, grad_v_anchor), "seq")
    first_device = device == 0
    grad_k_own = grad_k_own.at[0].add(jnp.where(first_device, anchor_gk, 0.0))
    grad_v_own = grad_v_own.at[0].add(jnp.where(first_device, anchor_gv, 0.0))
    q_scaled = grad_qn * q_gain
    k_scaled = grad_k_own.reshape(row_count, local_width) * k_gain
    q_dot, k_dot = lax.psum(
        (jnp.sum(q_float * q_scaled, axis=1), jnp.sum(k_float * k_scaled, axis=1)), "tp"
    )
    grad_q = (q_rinv * q_scaled - q_float * q_rinv**3 * q_dot[:, None] / WIDTH).astype(jnp.bfloat16)
    grad_k = (k_rinv * k_scaled - k_float * k_rinv**3 * k_dot[:, None] / WIDTH).astype(jnp.bfloat16)
    grad_v = grad_v_own.reshape(row_count, local_width).astype(jnp.bfloat16)
    return (attn_out, grad_q, grad_k, grad_v)


def solution(mesh):
    return jax.shard_map(
        on_device,
        mesh=mesh,
        in_specs=(
            P("seq", "tp"),
            P("seq", "tp"),
            P("seq", "tp"),
            P("tp"),
            P("tp"),
            P("seq", "tp"),
            P(),
            P("tp"),
        ),
        out_specs=(P("seq", "tp"), P("seq", "tp"), P("seq", "tp"), P("seq", "tp")),
        check_vma=False,
    )
```

profile of v0, /device:TPU:32, one launch (start us, length us, event | category | flops | bytes accessed | tf_op | source)
XLA Modules:
  0.0 733.7 jit_solution(7441168945927711885)
XLA Ops:
  7.3 1.2 fusion.29
  8.5 1.1 fusion.37
  9.6 55.4 %all-reduce.9 = (f32[512]{0:T(512)S(1)}, f32[512]{0:T(512)S(1)}) all-reduce(f32[512]{0:T(512)S(1)} %fusion.29, f32[512]{0:T(512)S(1)} %fusion.37), channel_id=1, replica_groups=mesh['seq'=32,'tp'=16] {'tp'}, use_global_device_ids=true, to_apply=%region_1.0 | all-reduce | flops 1024 | bytes 8192 | tf_op jit(solution)/shard_map/psum | solution.py:68
  64.9 1.1 fusion.39
  66.0 1.3 collective-permute-start
  67.4 4.0 collective-permute-start.1
  75.2 281.3 %all-reduce.16.cloned.1.call-done = (bf16[256,2,128]{2,1,0:T(2,128)(2,1)}, bf16[256,2,128]{2,1,0:T(2,128)(2,1)}) async-done(((bf16[256,2,128]{2,1,0:T(2,128)(2,1)}, bf16[256,2,128]{2,1,0:T(2,128)(2,1)}), (bf16[256,2,128]{2,1,0:T(2,128)(2,1)}, bf16[256,2,128]{2,1,0:T(2,128)(2,1)})) %all-reduce.16.cloned.1.call-update) | async-done | bytes 262160 | tf_op jit(solution)/shard_map/psum | solution.py:24
  359.4 1.6 maximum_bitcast_fusion.1
  361.3 17.1 %while.18 = (s32[]{:T(128)}, bf16[2,2,256,128]{3,2,1,0:T(8,128)(2,1)}, f32[2,2,256,128]{3,2,1,0:T(8,128)}, f32[2,2,1024,128]{3,2,1,0:T(8,128)}, f32[2,2,1024,128...) while((s32[]{:T(128)}, ...), condition=%wide.region_10.11_spmd, body=%wide.region_6.10_spmd.sunk | while | flops 813038592 | bytes 57053992 | solution.py:124
  363.6 1.3 copy-done.6
  372.1 1.3 copy-done.6
  378.3 1.7 copy_bitcast_fusion
  381.9 1.3 collective-permute-start.3
  383.3 1.6 slice_reduce_fusion.1
  385.0 1.2 pad_add_fusion.1
  387.0 1.3 collective-permute-start.2
  388.9 1.2 copy.33
  390.9 1.1 slice_add_fusion
  392.0 277.9 %all-reduce.14.cloned.1.call-done = (f32[256,256]{1,0:T(8,128)}, f32[256,256]{1,0:T(8,128)}) async-done(((f32[256,256]{1,0:T(8,128)}, f32[256,256]{1,0:T(8,128)}), (f32[256,256]{1,0:T(8,128)}, f32[256,256]{1,0:T(8,128)})) %all-reduce.14.cloned.1.call-update) | async-done | bytes 524304 | tf_op jit(solution)/shard_map/psum | solution.py:139
  669.9 1.1 fusion.45
  671.7 1.1 slice_add_fusion.1
  673.1 51.9 %all-reduce.8 = (f32[512]{0:T(512)S(1)}, f32[512]{0:T(512)S(1)}) all-reduce(f32[512]{0:T(512)S(1)} %fusion.36, f32[512]{0:T(512)S(1)} %fusion.44), channel_id=1, replica_groups=mesh['seq'=32,'tp'=16] {'tp'}, use_global_device_ids=true, to_apply=%region_12.13 | all-reduce | flops 1024 | bytes 8192 | tf_op jit(solution)/shard_map/psum | solution.py:145
  725.0 1.0 fusion.43
  725.9 1.0 fusion.35
  (134 shorter events, 26.0 us)
Async XLA Ops:
  7.2 67.3 %copy-start.1 = (bf16[512,256]{1,0:T(8,128)(2,1)S(1)}, bf16[512,256]{1,0:T(8,128)(2,1)}, u32[]{:S(2)}) copy-start(bf16[512,256]{1,0:T(8,128)(2,1)} %param.14) | copy-start | bytes 786436
  7.2 67.6 %copy-start.7 = (bf16[512,256]{1,0:T(8,128)(2,1)S(1)}, bf16[512,256]{1,0:T(8,128)(2,1)}, u32[]{:S(2)}) copy-start(bf16[512,256]{1,0:T(8,128)(2,1)} %param.16) | copy-start | bytes 786436
  7.2 66.7 %copy-start.19 = (s32[64]{0:T(128)S(1)}, s32[64]{0:T(128)}, u32[]{:S(2)}) copy-start(s32[64]{0:T(128)} %param.20) | copy-start | bytes 772
  7.2 66.9 %copy-start.18 = (s32[2]{0:T(128)S(1)}, s32[2]{0:T(128)}, u32[]{:S(2)}) copy-start(s32[2]{0:T(128)} %param.21) | copy-start | bytes 28
  7.2 67.1 %copy-start.13 = (bf16[512,256]{1,0:T(8,128)(2,1)S(1)}, bf16[512,256]{1,0:T(8,128)(2,1)}, u32[]{:S(2)}) copy-start(bf16[512,256]{1,0:T(8,128)(2,1)} %param.19) | copy-start | bytes 786436
  7.2 67.2 %copy-start.17 = (f32[256]{0:T(256)S(1)}, f32[256]{0:T(256)}, u32[]{:S(2)}) copy-start(f32[256]{0:T(256)} %param.17) | copy-start | bytes 3076
  7.2 349.2 %all-reduce.16.cloned.1.call-start = ((), (), s32[]{:S(2)}) async-start(), calls=%async_computation.1 | async-start | bytes 524288 | tf_op jit(solution)/shard_map/psum | solution.py:24
  66.0 291.3 %collective-permute-start = (bf16[512,256]{1,0:T(8,128)(2,1)S(1)}, bf16[512,256]{1,0:T(8,128)(2,1)S(1)}, u32[]{:S(2)}, u32[]{:S(2)}) collective-permute-start(bf16[512,256]{1,0:T(8,128)(2,1)S(1)} %fusion.39), channel_id=1, source_target_pairs={{0,16},{16,32},{32,48},{48,64},{64,80},{80,96},{96,112},{112,128},... | collective-permute-start | bytes 786440 | tf_op jit(solution)/shard_map/ppermute | solution.py:19
  67.4 291.7 %collective-permute-start.1 = (bf16[512,256]{1,0:T(8,128)(2,1)}, bf16[512,256]{1,0:T(8,128)(2,1)S(1)}, u32[]{:S(2)}, u32[]{:S(2)}) collective-permute-start(bf16[512,256]{1,0:T(8,128)(2,1)} %param.16), channel_id=1, source_target_pairs={{0,16},{16,32},{32,48},{48,64},{64,80},{80,96},{96,112},{112,128},... | collective-permute-start | bytes 786440 | tf_op jit(solution)/shard_map/ppermute | solution.py:19
  73.8 596.1 %all-reduce.14.cloned.1.call-start = ((), (), s32[]{:S(2)}) async-start(), calls=%async_computation | async-start | bytes 1048576 | tf_op jit(solution)/shard_map/psum | solution.py:139
  357.4 1.8 copy-start.15
  359.4 1.8 copy-start.8
  359.4 1.8 copy-start.9
  361.3 1.6 copy-start.5
  365.5 1.6 copy-start.2
  365.6 2.0 copy-start.10
  374.2 2.0 copy-start.10
  380.9 2.2 copy-start.4
  381.9 9.0 %collective-permute-start.3 = (f32[2,256,256]{2,1,0:T(8,128)}, f32[2,256,256]{2,1,0:T(8,128)}, u32[]{:S(2)}, u32[]{:S(2)}) collective-permute-start(f32[2,256,256]{2,1,0:T(8,128)} %slice.172), channel_id=1, source_target_pairs={{16,0},{32,16},{48,32},{64,48},{80,64},{96,80},{112,96},{128,112},... | collective-permute-start | bytes 1572872 | tf_op jit(solution)/shard_map/ppermute | solution.py:19
  385.0 3.3 copy-start.12
  387.0 284.6 %collective-permute-start.2 = (f32[2,256,256]{2,1,0:T(8,128)}, f32[2,256,256]{2,1,0:T(8,128)}, u32[]{:S(2)}, u32[]{:S(2)}) collective-permute-start(f32[2,256,256]{2,1,0:T(8,128)} %slice.165), channel_id=1, source_target_pairs={{16,0},{32,16},{48,32},{64,48},{80,64},{96,80},{112,96},{128,112},... | collective-permute-start | bytes 1572872 | tf_op jit(solution)/shard_map/ppermute | solution.py:19
  392.0 280.9 %copy-start = (bf16[512,256]{1,0:T(8,128)(2,1)S(1)}, bf16[512,256]{1,0:T(8,128)(2,1)}, u32[]{:S(2)}) copy-start(bf16[512,256]{1,0:T(8,128)(2,1)} %param.15) | copy-start | bytes 786436
  392.0 280.9 %copy-start.16 = (f32[256]{0:T(256)S(1)}, f32[256]{0:T(256)}, u32[]{:S(2)}) copy-start(f32[256]{0:T(256)} %param.18) | copy-start | bytes 3076
  669.9 2.9 copy-start.14
  (8 other events, 10.2 us)
Sparse Core Ops, SparseCore 0:
  73.9 282.5 all-reduce.15
  385.1 284.7 all-reduce.13
where the time goes:
time: 735 us; the launch traced here: 734 us
  waiting for transfers between devices  559 us (76%)
  blocking collectives  107 us (15%)
  local copies, waits for them, and re-layouts  19.6 us (3%)
  other arithmetic  18.1 us (2%)
  between operations  14.6 us (2%)
  starting transfers between devices  7.98 us (1%)
    psum x1, waiting for transfers between devices, from_root(): return lax.psum(jnp.where(mine, x, jnp.zeros_like(x)), axis)  281 us
    psum x1, waiting for transfers between devices, on_device(): anchor_gk, anchor_gv = lax.psum((grad_k_anchor, grad_v_anchor), 'seq')  278 us
    psum x1, blocking collectives, on_device(): lax.psum((jnp.sum(q_float * q_float, axis=1), jnp.sum(k_float * k_float,...  55.4 us
    psum x1, blocking collectives, on_device(): lax.psum((jnp.sum(q_float * q_scaled, axis=1), jnp.sum(k_float * k_scaled...  51.9 us
  transfers between devices with their start and end apart: 6, of which 2 were waited for; matrix products, arithmetic and copies ran while one was open for 2% of the time, Pallas kernels for 0%

commit v1 on v0

--- a/solution.py
+++ b/solution.py
@@ -19,9 +19,61 @@
     return lax.ppermute(block, axis, route)
 
 
-def from_root(x, axis, root):
-    mine = lax.axis_index(axis) == root
-    return lax.psum(jnp.where(mine, x, jnp.zeros_like(x)), axis)
+def xor_psum(values, axis):
+    n = lax.axis_size(axis)
+    if n & (n - 1):
+        return lax.psum(values, axis)
+    step = 1
+    while step < n:
+        got = lax.ppermute(values, axis, [(i, i ^ step) for i in range(n)])
+        values = jax.tree.map(jnp.add, values, got)
+        step *= 2
+    return values
+
+
+def tree_plan(n):
+    fans, m = [], n
+    if m % 2 == 0 and (m.bit_length() - 1) % 2 == 1 and m & (m - 1) == 0:
+        fans.append(2)
+        m //= 2
+    while m > 1:
+        f = 4 if m % 4 == 0 else next(p for p in range(2, m + 1) if m % p == 0)
+        fans.append(f)
+        m //= f
+    plan, step = [], 1
+    for f in fans:
+        plan.append((step, f))
+        step *= f
+    return plan
+
+
+def tree_bcast(values, axis):
+    n = lax.axis_size(axis)
+    me = lax.axis_index(axis)
+    for step, fan in reversed(tree_plan(n)):
+        span = step * fan
+        got = values
+        for j in range(1, fan):
+            route = [(i, i + j * step) for i in range(0, n, span) if i + j * step < n]
+            arrived = lax.ppermute(values, axis, route)
+            hit = me % span == j * step
+            got = jax.tree.map(lambda a, g: jnp.where(hit, a, g), arrived, got)
+        values = got
+    return values
+
+
+def tree_reduce(values, axis, wire):
+    n = lax.axis_size(axis)
+    for step, fan in tree_plan(n):
+        span = step * fan
+        total = values
+        for j in range(1, fan):
+            route = [(i + j * step, i) for i in range(0, n, span) if i + j * step < n]
+            sent = jax.tree.map(lambda a: a.astype(wire), values)
+            arrived = lax.ppermute(sent, axis, route)
+            total = jax.tree.map(lambda t, a: t + a.astype(t.dtype), total, arrived)
+        values = total
+    return values
 
 
 def stack_offsets(padded, before, count):
@@ -65,7 +117,7 @@
     device = lax.axis_index("seq")
     q_float = q_in.astype(jnp.float32)
     k_float = k_in.astype(jnp.float32)
-    q_power, k_power = lax.psum(
+    q_power, k_power = xor_psum(
         (jnp.sum(q_float * q_float, axis=1), jnp.sum(k_float * k_float, axis=1)), "tp"
     )
     q_rinv = lax.rsqrt(q_power / WIDTH + EPS)[:, None]
@@ -79,7 +131,7 @@
     row_live = near_live[F_DEV:]
     grad_mask = jnp.where(row_live.reshape(row_count)[:, None], d_out, jnp.zeros_like(d_out))
     halo_k, halo_v = shifted((k_norm, v_in), "seq", 1)
-    anchor_k, anchor_v = (from_root(k_norm[:CAP], "seq", 0), from_root(v_in[:CAP], "seq", 0))
+    anchor_k, anchor_v = tree_bcast((k_norm[:CAP], v_in[:CAP]), "seq")
     k_near = jnp.concatenate([halo_k, k_norm], axis=0).reshape(2 * F_DEV, CAP, local_width)
     v_near = jnp.concatenate([halo_v, v_in], axis=0).reshape(2 * F_DEV, CAP, local_width)
     k_set = jnp.concatenate(
@@ -136,15 +188,14 @@
     back_k, back_v = shifted((grad_k_near[:F_DEV], grad_v_near[:F_DEV]), "seq", -1)
     grad_k_own = grad_k_near[F_DEV:] + back_k
     grad_v_own = grad_v_near[F_DEV:] + back_v
-    anchor_gk, anchor_gv = lax.psum((grad_k_anchor, grad_v_anchor), "seq")
+    anchor_gk, anchor_gv = tree_reduce((grad_k_anchor, grad_v_anchor), "seq", jnp.bfloat16)
     first_device = device == 0
     grad_k_own = grad_k_own.at[0].add(jnp.where(first_device, anchor_gk, 0.0))
     grad_v_own = grad_v_own.at[0].add(jnp.where(first_device, anchor_gv, 0.0))
     q_scaled = grad_qn * q_gain
     k_scaled = grad_k_own.reshape(row_count, local_width) * k_gain
-    q_dot, k_dot = lax.psum(
-        (jnp.sum(q_float * q_scaled, axis=1), jnp.sum(k_float * k_scaled, axis=1)), "tp"
-    )
+    q_dot = xor_psum(jnp.sum(q_float * q_scaled, axis=1), "tp")
+    k_dot = xor_psum(jnp.sum(k_float * k_scaled, axis=1), "tp")
     grad_q = (q_rinv * q_scaled - q_float * q_rinv**3 * q_dot[:, None] / WIDTH).astype(jnp.bfloat16)
     grad_k = (k_rinv * k_scaled - k_float * k_rinv**3 * k_dot[:, None] / WIDTH).astype(jnp.bfloat16)
     grad_v = grad_v_own.reshape(row_count, local_width).astype(jnp.bfloat16)

time: 735 us -> 204 us (0.28)
  the two profiles are of different devices: /device:TPU:32 before, /device:TPU:6 now
where the time goes in v1:
time: 204 us; the launch traced here: 202 us
  starting transfers between devices  137 us (67%)
  other arithmetic  21.9 us (11%)
  local copies, waits for them, and re-layouts  17.4 us (9%)
  waiting for transfers between devices  15.6 us (8%)
  matrix products  8.04 us (4%)
    ppermute x16, starting transfers between devices, xor_psum(): got = lax.ppermute(values, axis, [(i, i ^ step) for i in range(n)])  78.8 us
    ppermute x14, starting transfers between devices, tree_reduce(): arrived = lax.ppermute(sent, axis, route)  24.1 us
    ppermute x14, starting transfers between devices, tree_bcast(): arrived = lax.ppermute(values, axis, route)  22.8 us
    ppermute x4, starting transfers between devices, shifted(): return lax.ppermute(block, axis, route)  11.6 us
    ppermute x16, waiting for transfers between devices, xor_psum(): got = lax.ppermute(values, axis, [(i, i ^ step) for i in range(n)])  8.39 us
    ppermute x14, waiting for transfers between devices, tree_reduce(): arrived = lax.ppermute(sent, axis, route)  5.42 us
    while x16, local copies, waits for them, and re-layouts  5.3 us
  transfers between devices with their start and end apart: 48, of which 10 were waited for; matrix products, arithmetic and copies ran while one was open for 14% of the time, Pallas kernels for 0%

profile of v1, /device:TPU:6, one launch (start us, length us, event | category | flops | bytes accessed | tf_op | source)
XLA Modules:
  0.0 202.5 jit_solution(13885328350850903861)
XLA Ops:
  5.4 10.9 %collective-permute-start.4 = (f32[512]{0:T(512)S(1)}, f32[512]{0:T(512)S(1)}, u32[]{:S(2)}, u32[]{:S(2)}) collective-permute-start(f32[512]{0:T(512)S(1)} %fusion.37), channel_id=1, source_target_pairs={{0,1},{1,0},{2,3},{3,2},{4,5},{5,4},{6,7},{7,6},{8,9},{9,8},{10,11... | collective-permute-start | bytes 6152 | tf_op jit(solution)/shard_map/ppermute | solution.py:28
  23.6 3.5 %collective-permute-start.5 = (f32[512]{0:T(512)S(1)}, f32[512]{0:T(512)S(1)}, u32[]{:S(2)}, u32[]{:S(2)}) collective-permute-start(f32[512]{0:T(512)S(1)} %add.205), channel_id=1, source_target_pairs={{0,2},{1,3},{2,0},{3,1},{4,6},{5,7},{6,4},{7,5},{8,10},{9,11},{10,... | collective-permute-start | bytes 6152 | tf_op jit(solution)/shard_map/ppermute | solution.py:28
  27.2 3.2 %collective-permute-start.1 = (f32[512]{0:T(512)S(1)}, f32[512]{0:T(512)S(1)}, u32[]{:S(2)}, u32[]{:S(2)}) collective-permute-start(f32[512]{0:T(512)S(1)} %add.200), channel_id=1, source_target_pairs={{0,2},{1,3},{2,0},{3,1},{4,6},{5,7},{6,4},{7,5},{8,10},{9,11},{10,... | collective-permute-start | bytes 6152 | tf_op jit(solution)/shard_map/ppermute | solution.py:28
  30.5 4.5 %collective-permute-start.6 = (f32[512]{0:T(512)S(1)}, f32[512]{0:T(512)S(1)}, u32[]{:S(2)}, u32[]{:S(2)}) collective-permute-start(f32[512]{0:T(512)S(1)} %add.206), channel_id=1, source_target_pairs={{0,4},{1,5},{2,6},{3,7},{4,0},{5,1},{6,2},{7,3},{8,12},{9,13},{10,... | collective-permute-start | bytes 6152 | tf_op jit(solution)/shard_map/ppermute | solution.py:28
  37.3 6.9 %collective-permute-start.7 = (f32[512]{0:T(512)S(1)}, f32[512]{0:T(512)S(1)}, u32[]{:S(2)}, u32[]{:S(2)}) collective-permute-start(f32[512]{0:T(512)S(1)} %add.207), channel_id=1, source_target_pairs={{0,8},{1,9},{2,10},{3,11},{4,12},{5,13},{6,14},{7,15},{8,0},{9,1},... | collective-permute-start | bytes 6152 | tf_op jit(solution)/shard_map/ppermute | solution.py:28
  47.4 6.2 %collective-permute-start.3 = (f32[512]{0:T(512)S(1)}, f32[512]{0:T(512)S(1)}, u32[]{:S(2)}, u32[]{:S(2)}) collective-permute-start(f32[512]{0:T(512)S(1)} %add.202), channel_id=1, source_target_pairs={{0,8},{1,9},{2,10},{3,11},{4,12},{5,13},{6,14},{7,15},{8,0},{9,1},... | collective-permute-start | bytes 6152 | tf_op jit(solution)/shard_map/ppermute | solution.py:28
  62.3 4.0 %collective-permute-start.20 = (bf16[256,256]{1,0:T(8,128)(2,1)S(1)}, bf16[256,256]{1,0:T(8,128)(2,1)S(1)}, u32[]{:S(2)}, u32[]{:S(2)}) collective-permute-start(bf16[256,256]{1,0:T(8,128)(2,1)S(1)} %select_select_fusion.1), channel_id=1, source_target_pairs={{0,96},{128,224},{256,352},{384,480},{1,97},{129,225},{257,353},{3... | collective-permute-start | bytes 393224 | tf_op jit(solution)/shard_map/ppermute | solution.py:58
  70.3 4.6 %collective-permute-start.12 = (bf16[256,256]{1,0:T(8,128)(2,1)S(1)}, bf16[256,256]{1,0:T(8,128)(2,1)S(1)}, u32[]{:S(2)}, u32[]{:S(2)}) collective-permute-start(bf16[256,256]{1,0:T(8,128)(2,1)S(1)} %select_select_fusion.3), channel_id=1, source_target_pairs={{0,96},{128,224},{256,352},{384,480},{1,97},{129,225},{257,353},{3... | collective-permute-start | bytes 393224 | tf_op jit(solution)/shard_map/ppermute | solution.py:58
  86.4 14.9 %while.18 = (s32[]{:T(128)}, bf16[2,2,256,128]{3,2,1,0:T(8,128)(2,1)S(1)}, f32[2,2,256,128]{3,2,1,0:T(8,128)}, f32[2,2,1024,128]{2,3,0,1:T(8,128)}, f32[2,2,1024...) while((s32[]{:T(128)}, ...), condition=%wide.region_6.7_spmd, body=%wide.region_2.6_spmd.sunk | while | flops 813038592 | bytes 52859124 | solution.py:176
  103.1 7.8 %collective-permute-start.24 = (f32[512]{0:T(512)S(1)}, f32[512]{0:T(512)S(1)}, u32[]{:S(2)}, u32[]{:S(2)}) collective-permute-start(f32[512]{0:T(512)S(1)} %fusion.36), channel_id=1, source_target_pairs={{0,1},{1,0},{2,3},{3,2},{4,5},{5,4},{6,7},{7,6},{8,9},{9,8},{10,11... | collective-permute-start | bytes 6152 | tf_op jit(solution)/shard_map/ppermute | solution.py:28
  114.1 2.6 %collective-permute-start.25 = (f32[512]{0:T(512)S(1)}, f32[512]{0:T(512)S(1)}, u32[]{:S(2)}, u32[]{:S(2)}) collective-permute-start(f32[512]{0:T(512)S(1)} %add.213), channel_id=1, source_target_pairs={{0,2},{1,3},{2,0},{3,1},{4,6},{5,7},{6,4},{7,5},{8,10},{9,11},{10,... | collective-permute-start | bytes 6152 | tf_op jit(solution)/shard_map/ppermute | solution.py:28
  117.7 4.3 %collective-permute-start.40 = (f32[2,256,256]{1,2,0:T(8,128)}, f32[2,256,256]{1,2,0:T(8,128)S(1)}, u32[]{:S(2)}, u32[]{:S(2)}) collective-permute-start(f32[2,256,256]{1,2,0:T(8,128)} %slice.172), channel_id=1, source_target_pairs={{16,0},{32,16},{48,32},{64,48},{80,64},{96,80},{112,96},{128,112},... | collective-permute-start | bytes 1572872 | tf_op jit(solution)/shard_map/ppermute | solution.py:19
  122.0 4.3 %collective-permute-start.26 = (f32[512]{0:T(512)S(1)}, f32[512]{0:T(512)S(1)}, u32[]{:S(2)}, u32[]{:S(2)}) collective-permute-start(f32[512]{0:T(512)S(1)} %add.214), channel_id=1, source_target_pairs={{0,4},{1,5},{2,6},{3,7},{4,0},{5,1},{6,2},{7,3},{8,12},{9,13},{10,... | collective-permute-start | bytes 6152 | tf_op jit(solution)/shard_map/ppermute | solution.py:28
  128.4 6.6 %collective-permute-start.27 = (f32[512]{0:T(512)S(1)}, f32[512]{0:T(512)S(1)}, u32[]{:S(2)}, u32[]{:S(2)}) collective-permute-start(f32[512]{0:T(512)S(1)} %add.215), channel_id=1, source_target_pairs={{0,8},{1,9},{2,10},{3,11},{4,12},{5,13},{6,14},{7,15},{8,0},{9,1},... | collective-permute-start | bytes 6152 | tf_op jit(solution)/shard_map/ppermute | solution.py:28
  135.2 3.4 %collective-permute-start.28 = (f32[2,256,256]{1,2,0:T(8,128)S(1)}, f32[2,256,256]{1,2,0:T(8,128)S(1)}, u32[]{:S(2)}, u32[]{:S(2)}) collective-permute-start(f32[2,256,256]{1,2,0:T(8,128)S(1)} %slice.165), channel_id=1, source_target_pairs={{16,0},{32,16},{48,32},{64,48},{80,64},{96,80},{112,96},{128,112},... | collective-permute-start | bytes 1572872 | tf_op jit(solution)/shard_map/ppermute | solution.py:19
  144.9 2.3 %collective-permute-done.30 = bf16[256,256]{0,1:T(8,128)(2,1)S(1)} collective-permute-done((bf16[256,256]{0,1:T(8,128)(2,1)S(1)}, bf16[256,256]{0,1:T(8,128)(2,1)S(1)}, u32[]{:S(2)}, u32[]{:S(2)}) %collective-permute-start.30) | collective-permute-done | bytes 131104 | tf_op jit(solution)/shard_map/ppermute | solution.py:73
  153.0 4.6 %collective-permute-start.35 = (bf16[256,256]{0,1:T(8,128)(2,1)S(1)}, bf16[256,256]{0,1:T(8,128)(2,1)S(1)}, u32[]{:S(2)}, u32[]{:S(2)}) collective-permute-start(bf16[256,256]{0,1:T(8,128)(2,1)S(1)} %fusion.53), channel_id=1, source_target_pairs={{384,0},{385,1},{386,2},{387,3},{388,4},{389,5},{390,6},{391,7},{3... | collective-permute-start | bytes 393224 | tf_op jit(solution)/shard_map/ppermute | solution.py:73
  164.5 7.0 %collective-permute-start.36 = (f32[512]{0:T(512)S(1)}, f32[512]{0:T(512)S(1)}, u32[]{:S(2)}, u32[]{:S(2)}) collective-permute-start(f32[512]{0:T(512)S(1)} %fusion.44), channel_id=1, source_target_pairs={{0,1},{1,0},{2,3},{3,2},{4,5},{5,4},{6,7},{7,6},{8,9},{9,8},{10,11... | collective-permute-start | bytes 6152 | tf_op jit(solution)/shard_map/ppermute | solution.py:28
  173.9 3.2 %collective-permute-start.37 = (f32[512]{0:T(512)S(1)}, f32[512]{0:T(512)S(1)}, u32[]{:S(2)}, u32[]{:S(2)}) collective-permute-start(f32[512]{0:T(512)S(1)} %add.228), channel_id=1, source_target_pairs={{0,2},{1,3},{2,0},{3,1},{4,6},{5,7},{6,4},{7,5},{8,10},{9,11},{10,... | collective-permute-start | bytes 6152 | tf_op jit(solution)/shard_map/ppermute | solution.py:28
  179.6 6.1 %collective-permute-start.47 = (bf16[256,256]{0,1:T(8,128)(2,1)S(1)}, bf16[256,256]{0,1:T(8,128)(2,1)S(1)}, u32[]{:S(2)}, u32[]{:S(2)}) collective-permute-start(bf16[256,256]{0,1:T(8,128)(2,1)S(1)} %fusion.54), channel_id=1, source_target_pairs={{384,0},{385,1},{386,2},{387,3},{388,4},{389,5},{390,6},{391,7},{3... | collective-permute-start | bytes 393224 | tf_op jit(solution)/shard_map/ppermute | solution.py:73
  185.7 3.6 %collective-permute-start.38 = (f32[512]{0:T(512)S(1)}, f32[512]{0:T(512)S(1)}, u32[]{:S(2)}, u32[]{:S(2)}) collective-permute-start(f32[512]{0:T(512)S(1)} %add.229), channel_id=1, source_target_pairs={{0,4},{1,5},{2,6},{3,7},{4,0},{5,1},{6,2},{7,3},{8,12},{9,13},{10,... | collective-permute-start | bytes 6152 | tf_op jit(solution)/shard_map/ppermute | solution.py:28
  189.5 2.7 %collective-permute-done.38 = f32[512]{0:T(512)S(1)} collective-permute-done((f32[512]{0:T(512)S(1)}, f32[512]{0:T(512)S(1)}, u32[]{:S(2)}, u32[]{:S(2)}) %collective-permute-start.38) | collective-permute-done | bytes 2080 | tf_op jit(solution)/shard_map/ppermute | solution.py:28
  192.1 4.3 %collective-permute-start.39 = (f32[512]{0:T(512)S(1)}, f32[512]{0:T(512)S(1)}, u32[]{:S(2)}, u32[]{:S(2)}) collective-permute-start(f32[512]{0:T(512)S(1)} %add.230), channel_id=1, source_target_pairs={{0,8},{1,9},{2,10},{3,11},{4,12},{5,13},{6,14},{7,15},{8,0},{9,1},... | collective-permute-start | bytes 6152 | tf_op jit(solution)/shard_map/ppermute | solution.py:28
  198.6 2.9 %collective-permute-done.39 = f32[512]{0:T(512)S(1)} collective-permute-done((f32[512]{0:T(512)S(1)}, f32[512]{0:T(512)S(1)}, u32[]{:S(2)}, u32[]{:S(2)}) %collective-permute-start.39) | collective-permute-done | bytes 2080 | tf_op jit(solution)/shard_map/ppermute | solution.py:28
  (239 shorter events, 90.9 us)
Async XLA Ops:
  1.6 56.7 %collective-permute-start.17 = (bf16[256,256]{1,0:T(8,128)(2,1)S(1)}, bf16[256,256]{1,0:T(8,128)(2,1)S(1)}, u32[]{:S(2)}, u32[]{:S(2)}) collective-permute-start(bf16[256,256]{1,0:T(8,128)(2,1)S(1)} %slice.142), channel_id=1, source_target_pairs={{0,384},{1,385},{2,386},{3,387},{4,388},{5,389},{6,390},{7,391},{8... | collective-permute-start | bytes 393224 | tf_op jit(solution)/shard_map/ppermute | solution.py:58
  2.9 56.1 %collective-permute-start.18 = (bf16[256,256]{1,0:T(8,128)(2,1)S(1)}, bf16[256,256]{1,0:T(8,128)(2,1)S(1)}, u32[]{:S(2)}, u32[]{:S(2)}) collective-permute-start(bf16[256,256]{1,0:T(8,128)(2,1)S(1)} %slice.142), channel_id=1, source_target_pairs={{0,256},{1,257},{2,258},{3,259},{4,260},{5,261},{6,262},{7,263},{8... | collective-permute-start | bytes 393224 | tf_op jit(solution)/shard_map/ppermute | solution.py:58
  3.6 56.7 %collective-permute-start.19 = (bf16[256,256]{1,0:T(8,128)(2,1)S(1)}, bf16[256,256]{1,0:T(8,128)(2,1)S(1)}, u32[]{:S(2)}, u32[]{:S(2)}) collective-permute-start(bf16[256,256]{1,0:T(8,128)(2,1)S(1)} %slice.142), channel_id=1, source_target_pairs={{0,128},{1,129},{2,130},{3,131},{4,132},{5,133},{6,134},{7,135},{8... | collective-permute-start | bytes 393224 | tf_op jit(solution)/shard_map/ppermute | solution.py:58
  5.4 18.2 %collective-permute-start.4 = (f32[512]{0:T(512)S(1)}, f32[512]{0:T(512)S(1)}, u32[]{:S(2)}, u32[]{:S(2)}) collective-permute-start(f32[512]{0:T(512)S(1)} %fusion.37), channel_id=1, source_target_pairs={{0,1},{1,0},{2,3},{3,2},{4,5},{5,4},{6,7},{7,6},{8,9},{9,8},{10,11... | collective-permute-start | bytes 6152 | tf_op jit(solution)/shard_map/ppermute | solution.py:28
  17.4 9.8 %collective-permute-start = (f32[512]{0:T(512)S(1)}, f32[512]{0:T(512)S(1)}, u32[]{:S(2)}, u32[]{:S(2)}) collective-permute-start(f32[512]{0:T(512)S(1)} %fusion.29), channel_id=1, source_target_pairs={{0,1},{1,0},{2,3},{3,2},{4,5},{5,4},{6,7},{7,6},{8,9},{9,8},{10,11... | collective-permute-start | bytes 6152 | tf_op jit(solution)/shard_map/ppermute | solution.py:28
  35.0 10.4 %collective-permute-start.2 = (f32[512]{0:T(512)S(1)}, f32[512]{0:T(512)S(1)}, u32[]{:S(2)}, u32[]{:S(2)}) collective-permute-start(f32[512]{0:T(512)S(1)} %add.201), channel_id=1, source_target_pairs={{0,4},{1,5},{2,6},{3,7},{4,0},{5,1},{6,2},{7,3},{8,12},{9,13},{10,... | collective-permute-start | bytes 6152 | tf_op jit(solution)/shard_map/ppermute | solution.py:28
  37.3 10.1 %collective-permute-start.7 = (f32[512]{0:T(512)S(1)}, f32[512]{0:T(512)S(1)}, u32[]{:S(2)}, u32[]{:S(2)}) collective-permute-start(f32[512]{0:T(512)S(1)} %add.207), channel_id=1, source_target_pairs={{0,8},{1,9},{2,10},{3,11},{4,12},{5,13},{6,14},{7,15},{8,0},{9,1},... | collective-permute-start | bytes 6152 | tf_op jit(solution)/shard_map/ppermute | solution.py:28
  45.4 33.4 %collective-permute-start.16 = (bf16[512,256]{1,0:T(8,128)(2,1)S(1)}, bf16[512,256]{1,0:T(8,128)(2,1)S(1)}, u32[]{:S(2)}, u32[]{:S(2)}) collective-permute-start(bf16[512,256]{1,0:T(8,128)(2,1)S(1)} %copy-done.2), channel_id=1, source_target_pairs={{0,16},{16,32},{32,48},{48,64},{64,80},{80,96},{96,112},{112,128},... | collective-permute-start | bytes 786440 | tf_op jit(solution)/shard_map/ppermute | solution.py:19
  59.0 10.0 %collective-permute-start.9 = (bf16[256,256]{1,0:T(8,128)(2,1)S(1)}, bf16[256,256]{1,0:T(8,128)(2,1)S(1)}, u32[]{:S(2)}, u32[]{:S(2)}) collective-permute-start(bf16[256,256]{1,0:T(8,128)(2,1)S(1)} %slice.160), channel_id=1, source_target_pairs={{0,384},{1,385},{2,386},{3,387},{4,388},{5,389},{6,390},{7,391},{8... | collective-permute-start | bytes 393224 | tf_op jit(solution)/shard_map/ppermute | solution.py:58
  60.3 21.7 %collective-permute-start.8 = (bf16[512,256]{1,0:T(8,128)(2,1)S(1)}, bf16[512,256]{1,0:T(8,128)(2,1)S(1)}, u32[]{:S(2)}, u32[]{:S(2)}) collective-permute-start(bf16[512,256]{1,0:T(8,128)(2,1)S(1)} %fusion.39), channel_id=1, source_target_pairs={{0,16},{16,32},{32,48},{48,64},{64,80},{80,96},{96,112},{112,128},... | collective-permute-start | bytes 786440 | tf_op jit(solution)/shard_map/ppermute | solution.py:19
  70.3 10.0 %collective-permute-start.12 = (bf16[256,256]{1,0:T(8,128)(2,1)S(1)}, bf16[256,256]{1,0:T(8,128)(2,1)S(1)}, u32[]{:S(2)}, u32[]{:S(2)}) collective-permute-start(bf16[256,256]{1,0:T(8,128)(2,1)S(1)} %select_select_fusion.3), channel_id=1, source_target_pairs={{0,96},{128,224},{256,352},{384,480},{1,97},{129,225},{257,353},{3... | collective-permute-start | bytes 393224 | tf_op jit(solution)/shard_map/ppermute | solution.py:58
  103.1 11.0 %collective-permute-start.24 = (f32[512]{0:T(512)S(1)}, f32[512]{0:T(512)S(1)}, u32[]{:S(2)}, u32[]{:S(2)}) collective-permute-start(f32[512]{0:T(512)S(1)} %fusion.36), channel_id=1, source_target_pairs={{0,1},{1,0},{2,3},{3,2},{4,5},{5,4},{6,7},{7,6},{8,9},{9,8},{10,11... | collective-permute-start | bytes 6152 | tf_op jit(solution)/shard_map/ppermute | solution.py:28
  112.7 30.2 %collective-permute-start.41 = (bf16[256,256]{0,1:T(8,128)(2,1)S(1)}, bf16[256,256]{0,1:T(8,128)(2,1)S(1)}, u32[]{:S(2)}, u32[]{:S(2)}) collective-permute-start(bf16[256,256]{0,1:T(8,128)(2,1)S(1)} %convert_element_type.132), channel_id=1, source_target_pairs={{16,0},{48,32},{80,64},{112,96},{144,128},{176,160},{208,192},{240... | collective-permute-start | bytes 393224 | tf_op jit(solution)/shard_map/ppermute | solution.py:73
  117.7 71.7 %collective-permute-start.40 = (f32[2,256,256]{1,2,0:T(8,128)}, f32[2,256,256]{1,2,0:T(8,128)S(1)}, u32[]{:S(2)}, u32[]{:S(2)}) collective-permute-start(f32[2,256,256]{1,2,0:T(8,128)} %slice.172), channel_id=1, source_target_pairs={{16,0},{32,16},{48,32},{64,48},{80,64},{96,80},{112,96},{128,112},... | collective-permute-start | bytes 1572872 | tf_op jit(solution)/shard_map/ppermute | solution.py:19
  126.5 13.7 %collective-permute-start.29 = (bf16[256,256]{0,1:T(8,128)(2,1)S(1)}, bf16[256,256]{0,1:T(8,128)(2,1)S(1)}, u32[]{:S(2)}, u32[]{:S(2)}) collective-permute-start(bf16[256,256]{0,1:T(8,128)(2,1)S(1)} %convert_element_type.121), channel_id=1, source_target_pairs={{16,0},{48,32},{80,64},{112,96},{144,128},{176,160},{208,192},{240... | collective-permute-start | bytes 393224 | tf_op jit(solution)/shard_map/ppermute | solution.py:73
  128.4 11.2 %collective-permute-start.27 = (f32[512]{0:T(512)S(1)}, f32[512]{0:T(512)S(1)}, u32[]{:S(2)}, u32[]{:S(2)}) collective-permute-start(f32[512]{0:T(512)S(1)} %add.215), channel_id=1, source_target_pairs={{0,8},{1,9},{2,10},{3,11},{4,12},{5,13},{6,14},{7,15},{8,0},{9,1},... | collective-permute-start | bytes 6152 | tf_op jit(solution)/shard_map/ppermute | solution.py:28
  135.2 17.8 %collective-permute-start.28 = (f32[2,256,256]{1,2,0:T(8,128)S(1)}, f32[2,256,256]{1,2,0:T(8,128)S(1)}, u32[]{:S(2)}, u32[]{:S(2)}) collective-permute-start(f32[2,256,256]{1,2,0:T(8,128)S(1)} %slice.165), channel_id=1, source_target_pairs={{16,0},{32,16},{48,32},{64,48},{80,64},{96,80},{112,96},{128,112},... | collective-permute-start | bytes 1572872 | tf_op jit(solution)/shard_map/ppermute | solution.py:19
  147.1 30.0 %collective-permute-start.42 = (bf16[256,256]{0,1:T(8,128)(2,1)}, bf16[256,256]{0,1:T(8,128)(2,1)}, u32[]{:S(2)}, u32[]{:S(2)}) collective-permute-start(bf16[256,256]{0,1:T(8,128)(2,1)} %fusion.48), channel_id=1, source_target_pairs={{32,0},{160,128},{288,256},{416,384},{33,1},{161,129},{289,257},{4... | collective-permute-start | bytes 393224 | tf_op jit(solution)/shard_map/ppermute | solution.py:73
  158.5 18.6 %collective-permute-start.43 = (bf16[256,256]{0,1:T(8,128)(2,1)}, bf16[256,256]{0,1:T(8,128)(2,1)}, u32[]{:S(2)}, u32[]{:S(2)}) collective-permute-start(bf16[256,256]{0,1:T(8,128)(2,1)} %fusion.48), channel_id=1, source_target_pairs={{64,0},{192,128},{320,256},{448,384},{65,1},{193,129},{321,257},{4... | collective-permute-start | bytes 393224 | tf_op jit(solution)/shard_map/ppermute | solution.py:73
  160.0 17.2 %collective-permute-start.44 = (bf16[256,256]{0,1:T(8,128)(2,1)}, bf16[256,256]{0,1:T(8,128)(2,1)}, u32[]{:S(2)}, u32[]{:S(2)}) collective-permute-start(bf16[256,256]{0,1:T(8,128)(2,1)} %fusion.48), channel_id=1, source_target_pairs={{96,0},{224,128},{352,256},{480,384},{97,1},{225,129},{353,257},{4... | collective-permute-start | bytes 393224 | tf_op jit(solution)/shard_map/ppermute | solution.py:73
  173.9 11.8 %collective-permute-start.37 = (f32[512]{0:T(512)S(1)}, f32[512]{0:T(512)S(1)}, u32[]{:S(2)}, u32[]{:S(2)}) collective-permute-start(f32[512]{0:T(512)S(1)} %add.228), channel_id=1, source_target_pairs={{0,2},{1,3},{2,0},{3,1},{4,6},{5,7},{6,4},{7,5},{8,10},{9,11},{10,... | collective-permute-start | bytes 6152 | tf_op jit(solution)/shard_map/ppermute | solution.py:28
  178.3 18.1 %collective-permute-start.45 = (bf16[256,256]{0,1:T(8,128)(2,1)S(1)}, bf16[256,256]{0,1:T(8,128)(2,1)S(1)}, u32[]{:S(2)}, u32[]{:S(2)}) collective-permute-start(bf16[256,256]{0,1:T(8,128)(2,1)S(1)} %fusion.54), channel_id=1, source_target_pairs={{128,0},{129,1},{130,2},{131,3},{132,4},{133,5},{134,6},{135,7},{1... | collective-permute-start | bytes 393224 | tf_op jit(solution)/shard_map/ppermute | solution.py:73
  178.9 17.5 %collective-permute-start.46 = (bf16[256,256]{0,1:T(8,128)(2,1)S(1)}, bf16[256,256]{0,1:T(8,128)(2,1)S(1)}, u32[]{:S(2)}, u32[]{:S(2)}) collective-permute-start(bf16[256,256]{0,1:T(8,128)(2,1)S(1)} %fusion.54), channel_id=1, source_target_pairs={{256,0},{257,1},{258,2},{259,3},{260,4},{261,5},{262,6},{263,7},{2... | collective-permute-start | bytes 393224 | tf_op jit(solution)/shard_map/ppermute | solution.py:73
  179.6 16.8 %collective-permute-start.47 = (bf16[256,256]{0,1:T(8,128)(2,1)S(1)}, bf16[256,256]{0,1:T(8,128)(2,1)S(1)}, u32[]{:S(2)}, u32[]{:S(2)}) collective-permute-start(bf16[256,256]{0,1:T(8,128)(2,1)S(1)} %fusion.54), channel_id=1, source_target_pairs={{384,0},{385,1},{386,2},{387,3},{388,4},{389,5},{390,6},{391,7},{3... | collective-permute-start | bytes 393224 | tf_op jit(solution)/shard_map/ppermute | solution.py:73
  (50 other events, 543.3 us)

commit v2 on v1

--- a/solution.py
+++ b/solution.py
@@ -118,7 +118,7 @@
     q_float = q_in.astype(jnp.float32)
     k_float = k_in.astype(jnp.float32)
     q_power, k_power = xor_psum(
-        (jnp.sum(q_float * q_float, axis=1), jnp.sum(k_float * k_float, axis=1)), "tp"
+        jnp.stack([jnp.sum(q_float * q_float, axis=1), jnp.sum(k_float * k_float, axis=1)]), "tp"
     )
     q_rinv = lax.rsqrt(q_power / WIDTH + EPS)[:, None]
     k_rinv = lax.rsqrt(k_power / WIDTH + EPS)[:, None]
@@ -130,8 +130,8 @@
     near_live = slot_index[None, :] < near_counts[:, None]
     row_live = near_live[F_DEV:]
     grad_mask = jnp.where(row_live.reshape(row_count)[:, None], d_out, jnp.zeros_like(d_out))
-    halo_k, halo_v = shifted((k_norm, v_in), "seq", 1)
-    anchor_k, anchor_v = tree_bcast((k_norm[:CAP], v_in[:CAP]), "seq")
+    halo_k, halo_v = shifted(jnp.stack([k_norm, v_in]), "seq", 1)
+    anchor_k, anchor_v = tree_bcast(jnp.stack([k_norm[:CAP], v_in[:CAP]]), "seq")
     k_near = jnp.concatenate([halo_k, k_norm], axis=0).reshape(2 * F_DEV, CAP, local_width)
     v_near = jnp.concatenate([halo_v, v_in], axis=0).reshape(2 * F_DEV, CAP, local_width)
     k_set = jnp.concatenate(
@@ -185,17 +185,18 @@
     grad_v_near = fold_offsets(grad_v_all[:, :split], F_DEV, F_DEV, CAP)
     grad_k_anchor = jnp.sum(grad_k_all[:, split:], axis=0)
     grad_v_anchor = jnp.sum(grad_v_all[:, split:], axis=0)
-    back_k, back_v = shifted((grad_k_near[:F_DEV], grad_v_near[:F_DEV]), "seq", -1)
+    back_k, back_v = shifted(jnp.stack([grad_k_near[:F_DEV], grad_v_near[:F_DEV]]), "seq", -1)
     grad_k_own = grad_k_near[F_DEV:] + back_k
     grad_v_own = grad_v_near[F_DEV:] + back_v
-    anchor_gk, anchor_gv = tree_reduce((grad_k_anchor, grad_v_anchor), "seq", jnp.bfloat16)
+    anchor_gk, anchor_gv = tree_reduce(jnp.stack([grad_k_anchor, grad_v_anchor]), "seq", jnp.bfloat16)
     first_device = device == 0
     grad_k_own = grad_k_own.at[0].add(jnp.where(first_device, anchor_gk, 0.0))
     grad_v_own = grad_v_own.at[0].add(jnp.where(first_device, anchor_gv, 0.0))
     q_scaled = grad_qn * q_gain
     k_scaled = grad_k_own.reshape(row_count, local_width) * k_gain
-    q_dot = xor_psum(jnp.sum(q_float * q_scaled, axis=1), "tp")
-    k_dot = xor_psum(jnp.sum(k_float * k_scaled, axis=1), "tp")
+    q_dot, k_dot = xor_psum(
+        jnp.stack([jnp.sum(q_float * q_scaled, axis=1), jnp.sum(k_float * k_scaled, axis=1)]), "tp"
+    )
     grad_q = (q_rinv * q_scaled - q_float * q_rinv**3 * q_dot[:, None] / WIDTH).astype(jnp.bfloat16)
     grad_k = (k_rinv * k_scaled - k_float * k_rinv**3 * k_dot[:, None] / WIDTH).astype(jnp.bfloat16)
     grad_v = grad_v_own.reshape(row_count, local_width).astype(jnp.bfloat16)

time: 204 us -> 167 us (0.82)
  the two profiles are of different devices: /device:TPU:6 before, /device:TPU:32 now
where the time goes in v2:
time: 167 us; the launch traced here: 166 us
  starting transfers between devices  60.5 us (36%)
  waiting for transfers between devices  57.6 us (34%)
  other arithmetic  21.7 us (13%)
  local copies, waits for them, and re-layouts  16.1 us (10%)
  matrix products  8.1 us (5%)
    ppermute x8, starting transfers between devices, xor_psum(): got = lax.ppermute(values, axis, [(i, i ^ step) for i in range(n)])  33.3 us
    ppermute x8, waiting for transfers between devices, xor_psum(): got = lax.ppermute(values, axis, [(i, i ^ step) for i in range(n)])  26.2 us
    ppermute x7, waiting for transfers between devices, tree_reduce(): arrived = lax.ppermute(sent, axis, route)  18.1 us
    ppermute x7, starting transfers between devices, tree_bcast(): arrived = lax.ppermute(values, axis, route)  14.6 us
    ppermute x7, waiting for transfers between devices, tree_bcast(): arrived = lax.ppermute(values, axis, route)  13.2 us
    ppermute x7, starting transfers between devices, tree_reduce(): arrived = lax.ppermute(sent, axis, route)  9.03 us
    while x24, local copies, waits for them, and re-layouts  4.08 us
    ppermute x2, starting transfers between devices, shifted(): return lax.ppermute(block, axis, route)  3.51 us
  transfers between devices with their start and end apart: 24, of which 16 were waited for; matrix products, arithmetic and copies ran while one was open for 10% of the time, Pallas kernels for 0%

profile of v2, /device:TPU:32, one launch (start us, length us, event | category | flops | bytes accessed | tf_op | source)
XLA Modules:
  0.0 165.6 jit_solution(3487462040180531433)
XLA Ops:
  2.9 10.9 %collective-permute-start = (f32[2,512]{1,0:T(2,128)S(1)}, f32[2,512]{1,0:T(2,128)S(1)}, u32[]{:S(2)}, u32[]{:S(2)}) collective-permute-start(f32[2,512]{1,0:T(2,128)S(1)} %pad_maximum_fusion.6), channel_id=1, source_target_pairs={{0,1},{1,0},{2,3},{3,2},{4,5},{5,4},{6,7},{7,6},{8,9},{9,8},{10,11... | collective-permute-start | bytes 12296 | tf_op jit(solution)/shard_map/ppermute | solution.py:28
  16.6 2.6 %collective-permute-start.1 = (f32[2,512]{1,0:T(2,128)S(1)}, f32[2,512]{1,0:T(2,128)S(1)}, u32[]{:S(2)}, u32[]{:S(2)}) collective-permute-start(f32[2,512]{1,0:T(2,128)S(1)} %fusion.62), channel_id=1, source_target_pairs={{0,2},{1,3},{2,0},{3,1},{4,6},{5,7},{6,4},{7,5},{8,10},{9,11},{10,... | collective-permute-start | bytes 12296 | tf_op jit(solution)/shard_map/ppermute | solution.py:28
  19.9 2.2 %collective-permute-done.1 = f32[2,512]{1,0:T(2,128)S(1)} collective-permute-done((f32[2,512]{1,0:T(2,128)S(1)}, f32[2,512]{1,0:T(2,128)S(1)}, u32[]{:S(2)}, u32[]{:S(2)}) %collective-permute-start.1) | collective-permute-done | bytes 4128 | tf_op jit(solution)/shard_map/ppermute | solution.py:28
  22.1 2.7 %collective-permute-start.2 = (f32[2,512]{1,0:T(2,128)S(1)}, f32[2,512]{1,0:T(2,128)S(1)}, u32[]{:S(2)}, u32[]{:S(2)}) collective-permute-start(f32[2,512]{1,0:T(2,128)S(1)} %fusion.71), channel_id=1, source_target_pairs={{0,4},{1,5},{2,6},{3,7},{4,0},{5,1},{6,2},{7,3},{8,12},{9,13},{10,... | collective-permute-start | bytes 12296 | tf_op jit(solution)/shard_map/ppermute | solution.py:28
  25.5 3.0 %collective-permute-done.2 = f32[2,512]{1,0:T(2,128)S(1)} collective-permute-done((f32[2,512]{1,0:T(2,128)S(1)}, f32[2,512]{1,0:T(2,128)S(1)}, u32[]{:S(2)}, u32[]{:S(2)}) %collective-permute-start.2) | collective-permute-done | bytes 4128 | tf_op jit(solution)/shard_map/ppermute | solution.py:28
  28.5 3.1 %collective-permute-start.3 = (f32[2,512]{1,0:T(2,128)S(1)}, f32[2,512]{1,0:T(2,128)S(1)}, u32[]{:S(2)}, u32[]{:S(2)}) collective-permute-start(f32[2,512]{1,0:T(2,128)S(1)} %add.173), channel_id=1, source_target_pairs={{0,8},{1,9},{2,10},{3,11},{4,12},{5,13},{6,14},{7,15},{8,0},{9,1},... | collective-permute-start | bytes 12296 | tf_op jit(solution)/shard_map/ppermute | solution.py:28
  31.7 6.2 %collective-permute-done.3 = f32[2,512]{1,0:T(2,128)S(1)} collective-permute-done((f32[2,512]{1,0:T(2,128)S(1)}, f32[2,512]{1,0:T(2,128)S(1)}, u32[]{:S(2)}, u32[]{:S(2)}) %collective-permute-start.3) | collective-permute-done | bytes 4128 | tf_op jit(solution)/shard_map/ppermute | solution.py:28
  40.0 4.7 %collective-permute-start.5 = (bf16[2,256,256]{2,1,0:T(8,128)(2,1)S(1)}, bf16[2,256,256]{2,1,0:T(8,128)(2,1)S(1)}, u32[]{:S(2)}, u32[]{:S(2)}) collective-permute-start(bf16[2,256,256]{2,1,0:T(8,128)(2,1)S(1)} %pad_maximum_fusion.5), channel_id=1, source_target_pairs={{0,384},{1,385},{2,386},{3,387},{4,388},{5,389},{6,390},{7,391},{8... | collective-permute-start | bytes 786440 | tf_op jit(solution)/shard_map/ppermute | solution.py:58
  47.6 2.2 %collective-permute-start.4 = (bf16[2,512,256]{2,1,0:T(8,128)(2,1)S(1)}, bf16[2,512,256]{2,1,0:T(8,128)(2,1)}, u32[]{:S(2)}, u32[]{:S(2)}) collective-permute-start(bf16[2,512,256]{2,1,0:T(8,128)(2,1)S(1)} %pad_maximum_fusion.1), channel_id=1, source_target_pairs={{0,16},{16,32},{32,48},{48,64},{64,80},{80,96},{96,112},{112,128},... | collective-permute-start | bytes 1572872 | tf_op jit(solution)/shard_map/ppermute | solution.py:19
  49.9 8.4 %collective-permute-done.7 = bf16[2,256,256]{2,1,0:T(8,128)(2,1)S(1)} collective-permute-done((bf16[2,256,256]{2,1,0:T(8,128)(2,1)S(1)}, bf16[2,256,256]{2,1,0:T(8,128)(2,1)S(1)}, u32[]{:S(2)}, u32[]{:S(2)}) %collective-permute-start.7) | collective-permute-done | bytes 262176 | tf_op jit(solution)/shard_map/ppermute | solution.py:58
  66.3 2.8 %collective-permute-done.9 = bf16[2,256,256]{2,1,0:T(8,128)(2,1)} collective-permute-done((bf16[2,256,256]{2,1,0:T(8,128)(2,1)S(1)}, bf16[2,256,256]{2,1,0:T(8,128)(2,1)}, u32[]{:S(2)}, u32[]{:S(2)}) %collective-permute-start.9) | collective-permute-done | bytes 262176 | tf_op jit(solution)/shard_map/ppermute | solution.py:58
  78.1 13.8 %while.18 = (s32[]{:T(128)}, bf16[2,2,256,128]{3,2,1,0:T(8,128)(2,1)}, f32[2,2,256,128]{3,2,1,0:T(8,128)}, f32[2,2,1024,128]{2,3,0,1:T(8,128)}, f32[2,2,1024,128...) while((s32[]{:T(128)}, ...), condition=%wide.region_6.7_spmd, body=%wide.region_2.6_spmd.sunk | while | flops 813038592 | bytes 42373420 | solution.py:176
  104.1 7.6 %collective-permute-done.14 = bf16[2,256,256]{1,2,0:T(8,128)(2,1)S(1)} collective-permute-done((bf16[2,256,256]{1,2,0:T(8,128)(2,1)S(1)}, bf16[2,256,256]{1,2,0:T(8,128)(2,1)S(1)}, u32[]{:S(2)}, u32[]{:S(2)}) %collective-permute-start.14) | collective-permute-done | bytes 262176 | tf_op jit(solution)/shard_map/ppermute | solution.py:73
  119.0 3.1 %collective-permute-done.17 = bf16[2,256,256]{1,2,0:T(8,128)(2,1)} collective-permute-done((bf16[2,256,256]{1,2,0:T(8,128)(2,1)}, bf16[2,256,256]{1,2,0:T(8,128)(2,1)}, u32[]{:S(2)}, u32[]{:S(2)}) %collective-permute-start.17) | collective-permute-done | bytes 262176 | tf_op jit(solution)/shard_map/ppermute | solution.py:73
  122.1 2.9 %collective-permute-done.18 = bf16[2,256,256]{1,2,0:T(8,128)(2,1)} collective-permute-done((bf16[2,256,256]{1,2,0:T(8,128)(2,1)}, bf16[2,256,256]{1,2,0:T(8,128)(2,1)}, u32[]{:S(2)}, u32[]{:S(2)}) %collective-permute-start.18) | collective-permute-done | bytes 262176 | tf_op jit(solution)/shard_map/ppermute | solution.py:73
  125.0 2.7 %collective-permute-done.19 = bf16[2,256,256]{1,2,0:T(8,128)(2,1)} collective-permute-done((bf16[2,256,256]{1,2,0:T(8,128)(2,1)}, bf16[2,256,256]{1,2,0:T(8,128)(2,1)}, u32[]{:S(2)}, u32[]{:S(2)}) %collective-permute-start.19) | collective-permute-done | bytes 262176 | tf_op jit(solution)/shard_map/ppermute | solution.py:73
  132.9 6.7 %collective-permute-start.20 = (f32[2,512]{1,0:T(2,128)S(1)}, f32[2,512]{1,0:T(2,128)S(1)}, u32[]{:S(2)}, u32[]{:S(2)}) collective-permute-start(f32[2,512]{1,0:T(2,128)S(1)} %pad_maximum_fusion.7), channel_id=1, source_target_pairs={{0,1},{1,0},{2,3},{3,2},{4,5},{5,4},{6,7},{7,6},{8,9},{9,8},{10,11... | collective-permute-start | bytes 12296 | tf_op jit(solution)/shard_map/ppermute | solution.py:28
  139.5 2.7 %collective-permute-done.20 = f32[2,512]{1,0:T(2,128)S(1)} collective-permute-done((f32[2,512]{1,0:T(2,128)S(1)}, f32[2,512]{1,0:T(2,128)S(1)}, u32[]{:S(2)}, u32[]{:S(2)}) %collective-permute-start.20) | collective-permute-done | bytes 4128 | tf_op jit(solution)/shard_map/ppermute | solution.py:28
  142.3 2.6 %collective-permute-start.21 = (f32[2,512]{1,0:T(2,128)S(1)}, f32[2,512]{1,0:T(2,128)S(1)}, u32[]{:S(2)}, u32[]{:S(2)}) collective-permute-start(f32[2,512]{1,0:T(2,128)S(1)} %fusion.61), channel_id=1, source_target_pairs={{0,2},{1,3},{2,0},{3,1},{4,6},{5,7},{6,4},{7,5},{8,10},{9,11},{10,... | collective-permute-start | bytes 12296 | tf_op jit(solution)/shard_map/ppermute | solution.py:28
  144.9 2.9 %collective-permute-done.21 = f32[2,512]{1,0:T(2,128)S(1)} collective-permute-done((f32[2,512]{1,0:T(2,128)S(1)}, f32[2,512]{1,0:T(2,128)S(1)}, u32[]{:S(2)}, u32[]{:S(2)}) %collective-permute-start.21) | collective-permute-done | bytes 4128 | tf_op jit(solution)/shard_map/ppermute | solution.py:28
  147.8 2.7 %collective-permute-start.22 = (f32[2,512]{1,0:T(2,128)S(1)}, f32[2,512]{1,0:T(2,128)S(1)}, u32[]{:S(2)}, u32[]{:S(2)}) collective-permute-start(f32[2,512]{1,0:T(2,128)S(1)} %fusion.69), channel_id=1, source_target_pairs={{0,4},{1,5},{2,6},{3,7},{4,0},{5,1},{6,2},{7,3},{8,12},{9,13},{10,... | collective-permute-start | bytes 12296 | tf_op jit(solution)/shard_map/ppermute | solution.py:28
  150.5 3.7 %collective-permute-done.22 = f32[2,512]{1,0:T(2,128)S(1)} collective-permute-done((f32[2,512]{1,0:T(2,128)S(1)}, f32[2,512]{1,0:T(2,128)S(1)}, u32[]{:S(2)}, u32[]{:S(2)}) %collective-permute-start.22) | collective-permute-done | bytes 4128 | tf_op jit(solution)/shard_map/ppermute | solution.py:28
  154.2 2.0 %collective-permute-start.23 = (f32[2,512]{1,0:T(2,128)S(1)}, f32[2,512]{1,0:T(2,128)S(1)}, u32[]{:S(2)}, u32[]{:S(2)}) collective-permute-start(f32[2,512]{1,0:T(2,128)S(1)} %add.195), channel_id=1, source_target_pairs={{0,8},{1,9},{2,10},{3,11},{4,12},{5,13},{6,14},{7,15},{8,0},{9,1},... | collective-permute-start | bytes 12296 | tf_op jit(solution)/shard_map/ppermute | solution.py:28
  158.2 5.4 %collective-permute-done.23 = f32[2,512]{1,0:T(2,128)S(1)} collective-permute-done((f32[2,512]{1,0:T(2,128)S(1)}, f32[2,512]{1,0:T(2,128)S(1)}, u32[]{:S(2)}, u32[]{:S(2)}) %collective-permute-start.23) | collective-permute-done | bytes 4128 | tf_op jit(solution)/shard_map/ppermute | solution.py:28
  (185 shorter events, 70.0 us)
Async XLA Ops:
  2.9 13.7 %collective-permute-start = (f32[2,512]{1,0:T(2,128)S(1)}, f32[2,512]{1,0:T(2,128)S(1)}, u32[]{:S(2)}, u32[]{:S(2)}) collective-permute-start(f32[2,512]{1,0:T(2,128)S(1)} %pad_maximum_fusion.6), channel_id=1, source_target_pairs={{0,1},{1,0},{2,3},{3,2},{4,5},{5,4},{6,7},{7,6},{8,9},{9,8},{10,11... | collective-permute-start | bytes 12296 | tf_op jit(solution)/shard_map/ppermute | solution.py:28
  16.6 5.5 %collective-permute-start.1 = (f32[2,512]{1,0:T(2,128)S(1)}, f32[2,512]{1,0:T(2,128)S(1)}, u32[]{:S(2)}, u32[]{:S(2)}) collective-permute-start(f32[2,512]{1,0:T(2,128)S(1)} %fusion.62), channel_id=1, source_target_pairs={{0,2},{1,3},{2,0},{3,1},{4,6},{5,7},{6,4},{7,5},{8,10},{9,11},{10,... | collective-permute-start | bytes 12296 | tf_op jit(solution)/shard_map/ppermute | solution.py:28
  22.1 6.4 %collective-permute-start.2 = (f32[2,512]{1,0:T(2,128)S(1)}, f32[2,512]{1,0:T(2,128)S(1)}, u32[]{:S(2)}, u32[]{:S(2)}) collective-permute-start(f32[2,512]{1,0:T(2,128)S(1)} %fusion.71), channel_id=1, source_target_pairs={{0,4},{1,5},{2,6},{3,7},{4,0},{5,1},{6,2},{7,3},{8,12},{9,13},{10,... | collective-permute-start | bytes 12296 | tf_op jit(solution)/shard_map/ppermute | solution.py:28
  28.5 9.4 %collective-permute-start.3 = (f32[2,512]{1,0:T(2,128)S(1)}, f32[2,512]{1,0:T(2,128)S(1)}, u32[]{:S(2)}, u32[]{:S(2)}) collective-permute-start(f32[2,512]{1,0:T(2,128)S(1)} %add.173), channel_id=1, source_target_pairs={{0,8},{1,9},{2,10},{3,11},{4,12},{5,13},{6,14},{7,15},{8,0},{9,1},... | collective-permute-start | bytes 12296 | tf_op jit(solution)/shard_map/ppermute | solution.py:28
  40.0 9.8 %collective-permute-start.5 = (bf16[2,256,256]{2,1,0:T(8,128)(2,1)S(1)}, bf16[2,256,256]{2,1,0:T(8,128)(2,1)S(1)}, u32[]{:S(2)}, u32[]{:S(2)}) collective-permute-start(bf16[2,256,256]{2,1,0:T(8,128)(2,1)S(1)} %pad_maximum_fusion.5), channel_id=1, source_target_pairs={{0,384},{1,385},{2,386},{3,387},{4,388},{5,389},{6,390},{7,391},{8... | collective-permute-start | bytes 786440 | tf_op jit(solution)/shard_map/ppermute | solution.py:58
  44.7 5.2 %collective-permute-start.6 = (bf16[2,256,256]{2,1,0:T(8,128)(2,1)S(1)}, bf16[2,256,256]{2,1,0:T(8,128)(2,1)S(1)}, u32[]{:S(2)}, u32[]{:S(2)}) collective-permute-start(bf16[2,256,256]{2,1,0:T(8,128)(2,1)S(1)} %pad_maximum_fusion.5), channel_id=1, source_target_pairs={{0,256},{1,257},{2,258},{3,259},{4,260},{5,261},{6,262},{7,263},{8... | collective-permute-start | bytes 786440 | tf_op jit(solution)/shard_map/ppermute | solution.py:58
  46.0 12.3 %collective-permute-start.7 = (bf16[2,256,256]{2,1,0:T(8,128)(2,1)S(1)}, bf16[2,256,256]{2,1,0:T(8,128)(2,1)S(1)}, u32[]{:S(2)}, u32[]{:S(2)}) collective-permute-start(bf16[2,256,256]{2,1,0:T(8,128)(2,1)S(1)} %pad_maximum_fusion.5), channel_id=1, source_target_pairs={{0,128},{1,129},{2,130},{3,131},{4,132},{5,133},{6,134},{7,135},{8... | collective-permute-start | bytes 786440 | tf_op jit(solution)/shard_map/ppermute | solution.py:58
  47.6 23.6 %collective-permute-start.4 = (bf16[2,512,256]{2,1,0:T(8,128)(2,1)S(1)}, bf16[2,512,256]{2,1,0:T(8,128)(2,1)}, u32[]{:S(2)}, u32[]{:S(2)}) collective-permute-start(bf16[2,512,256]{2,1,0:T(8,128)(2,1)S(1)} %pad_maximum_fusion.1), channel_id=1, source_target_pairs={{0,16},{16,32},{32,48},{48,64},{64,80},{80,96},{96,112},{112,128},... | collective-permute-start | bytes 1572872 | tf_op jit(solution)/shard_map/ppermute | solution.py:19
  58.4 6.0 %collective-permute-start.10 = (bf16[2,256,256]{2,1,0:T(8,128)(2,1)S(1)}, bf16[2,256,256]{2,1,0:T(8,128)(2,1)S(1)}, u32[]{:S(2)}, u32[]{:S(2)}) collective-permute-start(bf16[2,256,256]{2,1,0:T(8,128)(2,1)S(1)} %select_select_fusion.1), channel_id=1, source_target_pairs={{0,32},{128,160},{256,288},{384,416},{1,33},{129,161},{257,289},{3... | collective-permute-start | bytes 786440 | tf_op jit(solution)/shard_map/ppermute | solution.py:58
  59.7 6.7 %collective-permute-start.8 = (bf16[2,256,256]{2,1,0:T(8,128)(2,1)S(1)}, bf16[2,256,256]{2,1,0:T(8,128)(2,1)}, u32[]{:S(2)}, u32[]{:S(2)}) collective-permute-start(bf16[2,256,256]{2,1,0:T(8,128)(2,1)S(1)} %select_select_fusion.1), channel_id=1, source_target_pairs={{0,96},{128,224},{256,352},{384,480},{1,97},{129,225},{257,353},{3... | collective-permute-start | bytes 786440 | tf_op jit(solution)/shard_map/ppermute | solution.py:58
  61.7 7.4 %collective-permute-start.9 = (bf16[2,256,256]{2,1,0:T(8,128)(2,1)S(1)}, bf16[2,256,256]{2,1,0:T(8,128)(2,1)}, u32[]{:S(2)}, u32[]{:S(2)}) collective-permute-start(bf16[2,256,256]{2,1,0:T(8,128)(2,1)S(1)} %select_select_fusion.1), channel_id=1, source_target_pairs={{0,64},{128,192},{256,320},{384,448},{1,65},{129,193},{257,321},{3... | collective-permute-start | bytes 786440 | tf_op jit(solution)/shard_map/ppermute | solution.py:58
  69.2 5.7 %collective-permute-start.11 = (bf16[2,256,256]{2,1,0:T(8,128)(2,1)S(1)}, bf16[2,256,256]{2,1,0:T(8,128)(2,1)}, u32[]{:S(2)}, u32[]{:S(2)}) collective-permute-start(bf16[2,256,256]{2,1,0:T(8,128)(2,1)S(1)} %select_select_fusion), channel_id=1, source_target_pairs={{0,16},{32,48},{64,80},{96,112},{128,144},{160,176},{192,208},{224... | collective-permute-start | bytes 786440 | tf_op jit(solution)/shard_map/ppermute | solution.py:58
  94.3 3.4 %collective-permute-start.13 = (bf16[2,256,256]{1,2,0:T(8,128)(2,1)S(1)}, bf16[2,256,256]{1,2,0:T(8,128)(2,1)S(1)}, u32[]{:S(2)}, u32[]{:S(2)}) collective-permute-start(bf16[2,256,256]{1,2,0:T(8,128)(2,1)S(1)} %fusion.47), channel_id=1, source_target_pairs={{16,0},{48,32},{80,64},{112,96},{144,128},{176,160},{208,192},{240... | collective-permute-start | bytes 786440 | tf_op jit(solution)/shard_map/ppermute | solution.py:73
  97.8 13.9 %collective-permute-start.14 = (bf16[2,256,256]{1,2,0:T(8,128)(2,1)S(1)}, bf16[2,256,256]{1,2,0:T(8,128)(2,1)S(1)}, u32[]{:S(2)}, u32[]{:S(2)}) collective-permute-start(bf16[2,256,256]{1,2,0:T(8,128)(2,1)S(1)} %fusion.48), channel_id=1, source_target_pairs={{32,0},{160,128},{288,256},{416,384},{33,1},{161,129},{289,257},{4... | collective-permute-start | bytes 786440 | tf_op jit(solution)/shard_map/ppermute | solution.py:73
  99.1 12.6 %collective-permute-start.15 = (bf16[2,256,256]{1,2,0:T(8,128)(2,1)S(1)}, bf16[2,256,256]{1,2,0:T(8,128)(2,1)S(1)}, u32[]{:S(2)}, u32[]{:S(2)}) collective-permute-start(bf16[2,256,256]{1,2,0:T(8,128)(2,1)S(1)} %fusion.48), channel_id=1, source_target_pairs={{64,0},{192,128},{320,256},{448,384},{65,1},{193,129},{321,257},{4... | collective-permute-start | bytes 786440 | tf_op jit(solution)/shard_map/ppermute | solution.py:73
  100.4 11.3 %collective-permute-start.16 = (bf16[2,256,256]{1,2,0:T(8,128)(2,1)S(1)}, bf16[2,256,256]{1,2,0:T(8,128)(2,1)}, u32[]{:S(2)}, u32[]{:S(2)}) collective-permute-start(bf16[2,256,256]{1,2,0:T(8,128)(2,1)S(1)} %fusion.48), channel_id=1, source_target_pairs={{96,0},{224,128},{352,256},{480,384},{97,1},{225,129},{353,257},{4... | collective-permute-start | bytes 786440 | tf_op jit(solution)/shard_map/ppermute | solution.py:73
  102.8 26.4 %collective-permute-start.12 = (f32[2,2,256,256]{2,3,1,0:T(8,128)}, f32[2,2,256,256]{2,3,1,0:T(8,128)}, u32[]{:S(2)}, u32[]{:S(2)}) collective-permute-start(f32[2,2,256,256]{2,3,1,0:T(8,128)} %pad_maximum_fusion), channel_id=1, source_target_pairs={{16,0},{32,16},{48,32},{64,48},{80,64},{96,80},{112,96},{128,112},... | collective-permute-start | bytes 3145736 | tf_op jit(solution)/shard_map/ppermute | solution.py:19
  113.5 8.6 %collective-permute-start.17 = (bf16[2,256,256]{1,2,0:T(8,128)(2,1)}, bf16[2,256,256]{1,2,0:T(8,128)(2,1)}, u32[]{:S(2)}, u32[]{:S(2)}) collective-permute-start(bf16[2,256,256]{1,2,0:T(8,128)(2,1)} %fusion.63), channel_id=1, source_target_pairs={{128,0},{129,1},{130,2},{131,3},{132,4},{133,5},{134,6},{135,7},{1... | collective-permute-start | bytes 786440 | tf_op jit(solution)/shard_map/ppermute | solution.py:73
  114.8 10.2 %collective-permute-start.18 = (bf16[2,256,256]{1,2,0:T(8,128)(2,1)}, bf16[2,256,256]{1,2,0:T(8,128)(2,1)}, u32[]{:S(2)}, u32[]{:S(2)}) collective-permute-start(bf16[2,256,256]{1,2,0:T(8,128)(2,1)} %fusion.63), channel_id=1, source_target_pairs={{256,0},{257,1},{258,2},{259,3},{260,4},{261,5},{262,6},{263,7},{2... | collective-permute-start | bytes 786440 | tf_op jit(solution)/shard_map/ppermute | solution.py:73
  116.1 11.6 %collective-permute-start.19 = (bf16[2,256,256]{1,2,0:T(8,128)(2,1)}, bf16[2,256,256]{1,2,0:T(8,128)(2,1)}, u32[]{:S(2)}, u32[]{:S(2)}) collective-permute-start(bf16[2,256,256]{1,2,0:T(8,128)(2,1)} %fusion.63), channel_id=1, source_target_pairs={{384,0},{385,1},{386,2},{387,3},{388,4},{389,5},{390,6},{391,7},{3... | collective-permute-start | bytes 786440 | tf_op jit(solution)/shard_map/ppermute | solution.py:73
  132.9 9.4 %collective-permute-start.20 = (f32[2,512]{1,0:T(2,128)S(1)}, f32[2,512]{1,0:T(2,128)S(1)}, u32[]{:S(2)}, u32[]{:S(2)}) collective-permute-start(f32[2,512]{1,0:T(2,128)S(1)} %pad_maximum_fusion.7), channel_id=1, source_target_pairs={{0,1},{1,0},{2,3},{3,2},{4,5},{5,4},{6,7},{7,6},{8,9},{9,8},{10,11... | collective-permute-start | bytes 12296 | tf_op jit(solution)/shard_map/ppermute | solution.py:28
  142.3 5.5 %collective-permute-start.21 = (f32[2,512]{1,0:T(2,128)S(1)}, f32[2,512]{1,0:T(2,128)S(1)}, u32[]{:S(2)}, u32[]{:S(2)}) collective-permute-start(f32[2,512]{1,0:T(2,128)S(1)} %fusion.61), channel_id=1, source_target_pairs={{0,2},{1,3},{2,0},{3,1},{4,6},{5,7},{6,4},{7,5},{8,10},{9,11},{10,... | collective-permute-start | bytes 12296 | tf_op jit(solution)/shard_map/ppermute | solution.py:28
  147.8 6.4 %collective-permute-start.22 = (f32[2,512]{1,0:T(2,128)S(1)}, f32[2,512]{1,0:T(2,128)S(1)}, u32[]{:S(2)}, u32[]{:S(2)}) collective-permute-start(f32[2,512]{1,0:T(2,128)S(1)} %fusion.69), channel_id=1, source_target_pairs={{0,4},{1,5},{2,6},{3,7},{4,0},{5,1},{6,2},{7,3},{8,12},{9,13},{10,... | collective-permute-start | bytes 12296 | tf_op jit(solution)/shard_map/ppermute | solution.py:28
  154.2 9.4 %collective-permute-start.23 = (f32[2,512]{1,0:T(2,128)S(1)}, f32[2,512]{1,0:T(2,128)S(1)}, u32[]{:S(2)}, u32[]{:S(2)}) collective-permute-start(f32[2,512]{1,0:T(2,128)S(1)} %add.195), channel_id=1, source_target_pairs={{0,8},{1,9},{2,10},{3,11},{4,12},{5,13},{6,14},{7,15},{8,0},{9,1},... | collective-permute-start | bytes 12296 | tf_op jit(solution)/shard_map/ppermute | solution.py:28
  (24 other events, 245.0 us)

commit v3 on v2

--- a/solution.py
+++ b/solution.py
@@ -19,16 +19,10 @@
     return lax.ppermute(block, axis, route)
 
 
-def xor_psum(values, axis):
+def gather_sum(values, axis):
     n = lax.axis_size(axis)
-    if n & (n - 1):
-        return lax.psum(values, axis)
-    step = 1
-    while step < n:
-        got = lax.ppermute(values, axis, [(i, i ^ step) for i in range(n)])
-        values = jax.tree.map(jnp.add, values, got)
-        step *= 2
-    return values
+    copies = jnp.broadcast_to(values[None], (n,) + values.shape)
+    return jnp.sum(lax.all_to_all(copies, axis, 0, 0, tiled=False), axis=0)
 
 
 def tree_plan(n):
@@ -117,7 +111,7 @@
     device = lax.axis_index("seq")
     q_float = q_in.astype(jnp.float32)
     k_float = k_in.astype(jnp.float32)
-    q_power, k_power = xor_psum(
+    q_power, k_power = gather_sum(
         jnp.stack([jnp.sum(q_float * q_float, axis=1), jnp.sum(k_float * k_float, axis=1)]), "tp"
     )
     q_rinv = lax.rsqrt(q_power / WIDTH + EPS)[:, None]
@@ -194,7 +188,7 @@
     grad_v_own = grad_v_own.at[0].add(jnp.where(first_device, anchor_gv, 0.0))
     q_scaled = grad_qn * q_gain
     k_scaled = grad_k_own.reshape(row_count, local_width) * k_gain
-    q_dot, k_dot = xor_psum(
+    q_dot, k_dot = gather_sum(
         jnp.stack([jnp.sum(q_float * q_scaled, axis=1), jnp.sum(k_float * k_scaled, axis=1)]), "tp"
     )
     grad_q = (q_rinv * q_scaled - q_float * q_rinv**3 * q_dot[:, None] / WIDTH).astype(jnp.bfloat16)

time: 167 us -> 147 us (0.88)
  the two profiles are of different devices: /device:TPU:32 before, /device:TPU:8 now
where the time goes in v3:
time: 147 us; the launch traced here: 146 us
  waiting for transfers between devices  49.2 us (33%)
  starting transfers between devices  48 us (33%)
  other arithmetic  21.5 us (15%)
  local copies, waits for them, and re-layouts  17.3 us (12%)
  matrix products  8.11 us (6%)
    all_to_all x2, starting transfers between devices, gather_sum(): return jnp.sum(lax.all_to_all(copies, axis, 0, 0, tiled=False), axis=0)  20.8 us
    ppermute x7, waiting for transfers between devices, tree_reduce(): arrived = lax.ppermute(sent, axis, route)  18.9 us
    all_to_all x2, waiting for transfers between devices, gather_sum(): return jnp.sum(lax.all_to_all(copies, axis, 0, 0, tiled=False), axis=0)  17.1 us
    ppermute x7, starting transfers between devices, tree_bcast(): arrived = lax.ppermute(values, axis, route)  14.7 us
    ppermute x7, waiting for transfers between devices, tree_bcast(): arrived = lax.ppermute(values, axis, route)  13.2 us
    ppermute x7, starting transfers between devices, tree_reduce(): arrived = lax.ppermute(sent, axis, route)  9.03 us
    while x24, local copies, waits for them, and re-layouts  4.06 us
    ppermute x2, starting transfers between devices, shifted(): return lax.ppermute(block, axis, route)  3.52 us
  transfers between devices with their start and end apart: 18, of which 11 were waited for; matrix products, arithmetic and copies ran while one was open for 11% of the time, Pallas kernels for 0%

profile of v3, /device:TPU:8, one launch (start us, length us, event | category | flops | bytes accessed | tf_op | source)
XLA Modules:
  0.0 145.8 jit_solution(13292618039706963999)
XLA Ops:
  3.6 16.0 %all-to-all-start = ((f32[16,2,512]{2,1,0:T(2,128)}), f32[16,2,512]{2,1,0:T(2,128)S(1)}, u32[]{:S(2)}, u32[]{:S(2)}) async-start(f32[16,2,512]{2,1,0:T(2,128)} %broadcast_in_dim.116), calls=%async_computation | async-start | bytes 131072 | tf_op jit(solution)/shard_map/all_to_all | solution.py:25
  23.8 7.4 %all-to-all-done = f32[16,2,512]{2,1,0:T(2,128)S(1)} async-done(((f32[16,2,512]{2,1,0:T(2,128)}), f32[16,2,512]{2,1,0:T(2,128)S(1)}, u32[]{:S(2)}, u32[]{:S(2)}) %all-to-all-start) | async-done | bytes 65568 | tf_op jit(solution)/shard_map/all_to_all | solution.py:25
  33.3 4.7 %collective-permute-start.1 = (bf16[2,256,256]{2,1,0:T(8,128)(2,1)S(1)}, bf16[2,256,256]{2,1,0:T(8,128)(2,1)S(1)}, u32[]{:S(2)}, u32[]{:S(2)}) collective-permute-start(bf16[2,256,256]{2,1,0:T(8,128)(2,1)S(1)} %pad_maximum_fusion.5), channel_id=1, source_target_pairs={{0,384},{1,385},{2,386},{3,387},{4,388},{5,389},{6,390},{7,391},{8... | collective-permute-start | bytes 786440 | tf_op jit(solution)/shard_map/ppermute | solution.py:52
  40.9 2.2 %collective-permute-start = (bf16[2,512,256]{2,1,0:T(8,128)(2,1)S(1)}, bf16[2,512,256]{2,1,0:T(8,128)(2,1)}, u32[]{:S(2)}, u32[]{:S(2)}) collective-permute-start(bf16[2,512,256]{2,1,0:T(8,128)(2,1)S(1)} %pad_maximum_fusion.1), channel_id=1, source_target_pairs={{0,16},{16,32},{32,48},{48,64},{64,80},{80,96},{96,112},{112,128},... | collective-permute-start | bytes 1572872 | tf_op jit(solution)/shard_map/ppermute | solution.py:19
  43.2 8.4 %collective-permute-done.3 = bf16[2,256,256]{2,1,0:T(8,128)(2,1)S(1)} collective-permute-done((bf16[2,256,256]{2,1,0:T(8,128)(2,1)S(1)}, bf16[2,256,256]{2,1,0:T(8,128)(2,1)S(1)}, u32[]{:S(2)}, u32[]{:S(2)}) %collective-permute-start.3) | collective-permute-done | bytes 262176 | tf_op jit(solution)/shard_map/ppermute | solution.py:52
  52.9 2.0 %collective-permute-start.5 = (bf16[2,256,256]{2,1,0:T(8,128)(2,1)S(1)}, bf16[2,256,256]{2,1,0:T(8,128)(2,1)}, u32[]{:S(2)}, u32[]{:S(2)}) collective-permute-start(bf16[2,256,256]{2,1,0:T(8,128)(2,1)S(1)} %select_select_fusion.1), channel_id=1, source_target_pairs={{0,64},{128,192},{256,320},{384,448},{1,65},{129,193},{257,321},{3... | collective-permute-start | bytes 786440 | tf_op jit(solution)/shard_map/ppermute | solution.py:52
  55.0 2.0 %collective-permute-start.6 = (bf16[2,256,256]{2,1,0:T(8,128)(2,1)S(1)}, bf16[2,256,256]{2,1,0:T(8,128)(2,1)}, u32[]{:S(2)}, u32[]{:S(2)}) collective-permute-start(bf16[2,256,256]{2,1,0:T(8,128)(2,1)S(1)} %select_select_fusion.1), channel_id=1, source_target_pairs={{0,32},{128,160},{256,288},{384,416},{1,33},{129,161},{257,289},{3... | collective-permute-start | bytes 786440 | tf_op jit(solution)/shard_map/ppermute | solution.py:52
  57.7 1.9 %collective-permute-done.5 = bf16[2,256,256]{2,1,0:T(8,128)(2,1)} collective-permute-done((bf16[2,256,256]{2,1,0:T(8,128)(2,1)S(1)}, bf16[2,256,256]{2,1,0:T(8,128)(2,1)}, u32[]{:S(2)}, u32[]{:S(2)}) %collective-permute-start.5) | collective-permute-done | bytes 262176 | tf_op jit(solution)/shard_map/ppermute | solution.py:52
  59.6 2.8 %collective-permute-done.6 = bf16[2,256,256]{2,1,0:T(8,128)(2,1)} collective-permute-done((bf16[2,256,256]{2,1,0:T(8,128)(2,1)S(1)}, bf16[2,256,256]{2,1,0:T(8,128)(2,1)}, u32[]{:S(2)}, u32[]{:S(2)}) %collective-permute-start.6) | collective-permute-done | bytes 262176 | tf_op jit(solution)/shard_map/ppermute | solution.py:52
  62.5 2.0 %collective-permute-start.7 = (bf16[2,256,256]{2,1,0:T(8,128)(2,1)S(1)}, bf16[2,256,256]{2,1,0:T(8,128)(2,1)}, u32[]{:S(2)}, u32[]{:S(2)}) collective-permute-start(bf16[2,256,256]{2,1,0:T(8,128)(2,1)S(1)} %select_select_fusion), channel_id=1, source_target_pairs={{0,16},{32,48},{64,80},{96,112},{128,144},{160,176},{192,208},{224... | collective-permute-start | bytes 786440 | tf_op jit(solution)/shard_map/ppermute | solution.py:52
  68.4 1.6 %maximum_bitcast_fusion.1 = bf16[2,2,1024,128]{3,0,2,1:T(2,128)(2,1)S(1)} fusion(bf16[2,256,2,128]{3,2,1,0:T(2,128)(2,1)S(1)} %broadcast_in_dim.120, bf16[2,256,2,128]{3,2,1,0:T(2,128)(2,1)S(1)} %concatenate.50, bf16[2,256,2,128]{3,2,1,0:T(2,128)(2,1)S(1)} %copy-done.9, bf16[2,256,2,128]{3,2,1,0:T(2,128)(2,1)S(1)} %concatenate.47), kind=kLoop, calls=%fused_computation.40 | loop fusion | flops 1572864 | bytes 2097152 | tf_op jit(solution)/shard_map/transpose | solution.py:147
  71.3 13.8 %while.18 = (s32[]{:T(128)}, bf16[2,2,256,128]{3,2,1,0:T(8,128)(2,1)}, f32[2,2,256,128]{3,2,1,0:T(8,128)}, f32[2,2,1024,128]{2,3,0,1:T(8,128)}, f32[2,2,1024,128...) while((s32[]{:T(128)}, ...), condition=%wide.region_7.8_spmd, body=%wide.region_3.7_spmd.sunk | while | flops 813038592 | bytes 42373420 | solution.py:170
  74.9 1.4 fusion.96
  81.8 1.3 fusion.96
  85.2 1.8 %slice_reduce_fusion.1 = (f32[256,256]{0,1:T(8,128)S(1)}, f32[2,256,256]{1,2,0:T(8,128)S(1)}, f32[2,256,256]{1,2,0:T(8,128)S(1)}, f32[2,256,256]{1,2,0:T(8,128)S(1)}) fusion(f32[2,1024,256]{1,2,0:T(8,128)} %bitcast.32), kind=kLoop, calls=%fused_computation.72 | loop fusion | flops 65536 | bytes 3932160 | tf_op jit(solution)/shard_map/reduce_sum | solution.py:180
  89.2 1.8 %collective-permute-done.9 = bf16[2,256,256]{1,2,0:T(8,128)(2,1)S(1)} collective-permute-done((bf16[2,256,256]{1,2,0:T(8,128)(2,1)S(1)}, bf16[2,256,256]{1,2,0:T(8,128)(2,1)S(1)}, u32[]{:S(2)}, u32[]{:S(2)}) %collective-permute-start.9) | collective-permute-done | bytes 262176 | tf_op jit(solution)/shard_map/ppermute | solution.py:67
  98.0 8.7 %collective-permute-done.10 = bf16[2,256,256]{1,2,0:T(8,128)(2,1)S(1)} collective-permute-done((bf16[2,256,256]{1,2,0:T(8,128)(2,1)}, bf16[2,256,256]{1,2,0:T(8,128)(2,1)S(1)}, u32[]{:S(2)}, u32[]{:S(2)}) %collective-permute-start.10) | collective-permute-done | bytes 262176 | tf_op jit(solution)/shard_map/ppermute | solution.py:67
  111.8 1.4 copy.78
  113.4 2.7 %collective-permute-done.13 = bf16[2,256,256]{1,2,0:T(8,128)(2,1)S(1)} collective-permute-done((bf16[2,256,256]{1,2,0:T(8,128)(2,1)S(1)}, bf16[2,256,256]{1,2,0:T(8,128)(2,1)S(1)}, u32[]{:S(2)}, u32[]{:S(2)}) %collective-permute-start.13) | collective-permute-done | bytes 262176 | tf_op jit(solution)/shard_map/ppermute | solution.py:67
  116.1 2.9 %collective-permute-done.14 = bf16[2,256,256]{1,2,0:T(8,128)(2,1)S(1)} collective-permute-done((bf16[2,256,256]{1,2,0:T(8,128)(2,1)S(1)}, bf16[2,256,256]{1,2,0:T(8,128)(2,1)S(1)}, u32[]{:S(2)}, u32[]{:S(2)}) %collective-permute-start.14) | collective-permute-done | bytes 262176 | tf_op jit(solution)/shard_map/ppermute | solution.py:67
  119.0 2.7 %collective-permute-done.15 = bf16[2,256,256]{1,2,0:T(8,128)(2,1)S(1)} collective-permute-done((bf16[2,256,256]{1,2,0:T(8,128)(2,1)S(1)}, bf16[2,256,256]{1,2,0:T(8,128)(2,1)S(1)}, u32[]{:S(2)}, u32[]{:S(2)}) %collective-permute-start.15) | collective-permute-done | bytes 262176 | tf_op jit(solution)/shard_map/ppermute | solution.py:67
  123.0 1.3 fusion.45
  127.3 4.8 %all-to-all-start.1 = ((f32[16,2,512]{2,1,0:T(2,128)}), f32[16,2,512]{2,1,0:T(2,128)S(1)}, u32[]{:S(2)}, u32[]{:S(2)}) async-start(f32[16,2,512]{2,1,0:T(2,128)} %broadcast_in_dim.125), calls=%async_computation.1 | async-start | bytes 131072 | tf_op jit(solution)/shard_map/all_to_all | solution.py:25
  134.0 9.7 %all-to-all-done.1 = f32[16,2,512]{2,1,0:T(2,128)S(1)} async-done(((f32[16,2,512]{2,1,0:T(2,128)}), f32[16,2,512]{2,1,0:T(2,128)S(1)}, u32[]{:S(2)}, u32[]{:S(2)}) %all-to-all-start.1) | async-done | bytes 65568 | tf_op jit(solution)/shard_map/all_to_all | solution.py:25
  (169 shorter events, 52.4 us)
Async XLA Ops:
  0.6 40.0 %copy-start = (bf16[512,256]{1,0:T(8,128)(2,1)S(1)}, bf16[512,256]{1,0:T(8,128)(2,1)}, u32[]{:S(2)}) copy-start(bf16[512,256]{1,0:T(8,128)(2,1)} %param.15) | copy-start | bytes 786436
  0.6 40.0 %copy-start.16 = (f32[256]{0:T(256)S(1)}, f32[256]{0:T(256)}, u32[]{:S(2)}) copy-start(f32[256]{0:T(256)} %param.18) | copy-start | bytes 3076
  0.7 40.1 %copy-start.5 = (bf16[512,256]{1,0:T(8,128)(2,1)S(1)}, bf16[512,256]{1,0:T(8,128)(2,1)}, u32[]{:S(2)}) copy-start(bf16[512,256]{1,0:T(8,128)(2,1)} %param.16) | copy-start | bytes 786436
  3.6 27.6 %all-to-all-start = ((f32[16,2,512]{2,1,0:T(2,128)}), f32[16,2,512]{2,1,0:T(2,128)S(1)}, u32[]{:S(2)}, u32[]{:S(2)}) async-start(f32[16,2,512]{2,1,0:T(2,128)} %broadcast_in_dim.116), calls=%async_computation | async-start | bytes 131072 | tf_op jit(solution)/shard_map/all_to_all | solution.py:25
  33.3 9.8 %collective-permute-start.1 = (bf16[2,256,256]{2,1,0:T(8,128)(2,1)S(1)}, bf16[2,256,256]{2,1,0:T(8,128)(2,1)S(1)}, u32[]{:S(2)}, u32[]{:S(2)}) collective-permute-start(bf16[2,256,256]{2,1,0:T(8,128)(2,1)S(1)} %pad_maximum_fusion.5), channel_id=1, source_target_pairs={{0,384},{1,385},{2,386},{3,387},{4,388},{5,389},{6,390},{7,391},{8... | collective-permute-start | bytes 786440 | tf_op jit(solution)/shard_map/ppermute | solution.py:52
  38.0 5.2 %collective-permute-start.2 = (bf16[2,256,256]{2,1,0:T(8,128)(2,1)S(1)}, bf16[2,256,256]{2,1,0:T(8,128)(2,1)S(1)}, u32[]{:S(2)}, u32[]{:S(2)}) collective-permute-start(bf16[2,256,256]{2,1,0:T(8,128)(2,1)S(1)} %pad_maximum_fusion.5), channel_id=1, source_target_pairs={{0,256},{1,257},{2,258},{3,259},{4,260},{5,261},{6,262},{7,263},{8... | collective-permute-start | bytes 786440 | tf_op jit(solution)/shard_map/ppermute | solution.py:52
  39.3 12.3 %collective-permute-start.3 = (bf16[2,256,256]{2,1,0:T(8,128)(2,1)S(1)}, bf16[2,256,256]{2,1,0:T(8,128)(2,1)S(1)}, u32[]{:S(2)}, u32[]{:S(2)}) collective-permute-start(bf16[2,256,256]{2,1,0:T(8,128)(2,1)S(1)} %pad_maximum_fusion.5), channel_id=1, source_target_pairs={{0,128},{1,129},{2,130},{3,131},{4,132},{5,133},{6,134},{7,135},{8... | collective-permute-start | bytes 786440 | tf_op jit(solution)/shard_map/ppermute | solution.py:52
  40.8 16.5 %copy-start.1 = (bf16[512,256]{1,0:T(8,128)(2,1)S(1)}, bf16[512,256]{1,0:T(8,128)(2,1)}, u32[]{:S(2)}) copy-start(bf16[512,256]{1,0:T(8,128)(2,1)} %param.14) | copy-start | bytes 786436
  40.8 16.5 %copy-start.17 = (f32[256]{0:T(256)S(1)}, f32[256]{0:T(256)}, u32[]{:S(2)}) copy-start(f32[256]{0:T(256)} %param.17) | copy-start | bytes 3076
  40.9 23.7 %collective-permute-start = (bf16[2,512,256]{2,1,0:T(8,128)(2,1)S(1)}, bf16[2,512,256]{2,1,0:T(8,128)(2,1)}, u32[]{:S(2)}, u32[]{:S(2)}) collective-permute-start(bf16[2,512,256]{2,1,0:T(8,128)(2,1)S(1)} %pad_maximum_fusion.1), channel_id=1, source_target_pairs={{0,16},{16,32},{32,48},{48,64},{64,80},{80,96},{96,112},{112,128},... | collective-permute-start | bytes 1572872 | tf_op jit(solution)/shard_map/ppermute | solution.py:19
  51.6 6.0 %collective-permute-start.4 = (bf16[2,256,256]{2,1,0:T(8,128)(2,1)S(1)}, bf16[2,256,256]{2,1,0:T(8,128)(2,1)S(1)}, u32[]{:S(2)}, u32[]{:S(2)}) collective-permute-start(bf16[2,256,256]{2,1,0:T(8,128)(2,1)S(1)} %select_select_fusion.1), channel_id=1, source_target_pairs={{0,96},{128,224},{256,352},{384,480},{1,97},{129,225},{257,353},{3... | collective-permute-start | bytes 786440 | tf_op jit(solution)/shard_map/ppermute | solution.py:52
  52.9 6.7 %collective-permute-start.5 = (bf16[2,256,256]{2,1,0:T(8,128)(2,1)S(1)}, bf16[2,256,256]{2,1,0:T(8,128)(2,1)}, u32[]{:S(2)}, u32[]{:S(2)}) collective-permute-start(bf16[2,256,256]{2,1,0:T(8,128)(2,1)S(1)} %select_select_fusion.1), channel_id=1, source_target_pairs={{0,64},{128,192},{256,320},{384,448},{1,65},{129,193},{257,321},{3... | collective-permute-start | bytes 786440 | tf_op jit(solution)/shard_map/ppermute | solution.py:52
  55.0 7.4 %collective-permute-start.6 = (bf16[2,256,256]{2,1,0:T(8,128)(2,1)S(1)}, bf16[2,256,256]{2,1,0:T(8,128)(2,1)}, u32[]{:S(2)}, u32[]{:S(2)}) collective-permute-start(bf16[2,256,256]{2,1,0:T(8,128)(2,1)S(1)} %select_select_fusion.1), channel_id=1, source_target_pairs={{0,32},{128,160},{256,288},{384,416},{1,33},{129,161},{257,289},{3... | collective-permute-start | bytes 786440 | tf_op jit(solution)/shard_map/ppermute | solution.py:52
  62.5 5.7 %collective-permute-start.7 = (bf16[2,256,256]{2,1,0:T(8,128)(2,1)S(1)}, bf16[2,256,256]{2,1,0:T(8,128)(2,1)}, u32[]{:S(2)}, u32[]{:S(2)}) collective-permute-start(bf16[2,256,256]{2,1,0:T(8,128)(2,1)S(1)} %select_select_fusion), channel_id=1, source_target_pairs={{0,16},{32,48},{64,80},{96,112},{128,144},{160,176},{192,208},{224... | collective-permute-start | bytes 786440 | tf_op jit(solution)/shard_map/ppermute | solution.py:52
  87.6 3.4 %collective-permute-start.9 = (bf16[2,256,256]{1,2,0:T(8,128)(2,1)S(1)}, bf16[2,256,256]{1,2,0:T(8,128)(2,1)S(1)}, u32[]{:S(2)}, u32[]{:S(2)}) collective-permute-start(bf16[2,256,256]{1,2,0:T(8,128)(2,1)S(1)} %fusion.47), channel_id=1, source_target_pairs={{16,0},{48,32},{80,64},{112,96},{144,128},{176,160},{208,192},{240... | collective-permute-start | bytes 786440 | tf_op jit(solution)/shard_map/ppermute | solution.py:67
  91.8 15.0 %collective-permute-start.10 = (bf16[2,256,256]{1,2,0:T(8,128)(2,1)}, bf16[2,256,256]{1,2,0:T(8,128)(2,1)S(1)}, u32[]{:S(2)}, u32[]{:S(2)}) collective-permute-start(bf16[2,256,256]{1,2,0:T(8,128)(2,1)} %fusion.48), channel_id=1, source_target_pairs={{32,0},{160,128},{288,256},{416,384},{33,1},{161,129},{289,257},{4... | collective-permute-start | bytes 786440 | tf_op jit(solution)/shard_map/ppermute | solution.py:67
  93.1 13.7 %collective-permute-start.11 = (bf16[2,256,256]{1,2,0:T(8,128)(2,1)}, bf16[2,256,256]{1,2,0:T(8,128)(2,1)S(1)}, u32[]{:S(2)}, u32[]{:S(2)}) collective-permute-start(bf16[2,256,256]{1,2,0:T(8,128)(2,1)} %fusion.48), channel_id=1, source_target_pairs={{64,0},{192,128},{320,256},{448,384},{65,1},{193,129},{321,257},{4... | collective-permute-start | bytes 786440 | tf_op jit(solution)/shard_map/ppermute | solution.py:67
  94.4 12.4 %collective-permute-start.12 = (bf16[2,256,256]{1,2,0:T(8,128)(2,1)}, bf16[2,256,256]{1,2,0:T(8,128)(2,1)}, u32[]{:S(2)}, u32[]{:S(2)}) collective-permute-start(bf16[2,256,256]{1,2,0:T(8,128)(2,1)} %fusion.48), channel_id=1, source_target_pairs={{96,0},{224,128},{352,256},{480,384},{97,1},{225,129},{353,257},{4... | collective-permute-start | bytes 786440 | tf_op jit(solution)/shard_map/ppermute | solution.py:67
  96.8 26.2 %collective-permute-start.8 = (f32[2,2,256,256]{2,3,1,0:T(8,128)}, f32[2,2,256,256]{2,3,1,0:T(8,128)}, u32[]{:S(2)}, u32[]{:S(2)}) collective-permute-start(f32[2,2,256,256]{2,3,1,0:T(8,128)} %pad_maximum_fusion), channel_id=1, source_target_pairs={{16,0},{32,16},{48,32},{64,48},{80,64},{96,80},{112,96},{128,112},... | collective-permute-start | bytes 3145736 | tf_op jit(solution)/shard_map/ppermute | solution.py:19
  107.9 8.3 %collective-permute-start.13 = (bf16[2,256,256]{1,2,0:T(8,128)(2,1)S(1)}, bf16[2,256,256]{1,2,0:T(8,128)(2,1)S(1)}, u32[]{:S(2)}, u32[]{:S(2)}) collective-permute-start(bf16[2,256,256]{1,2,0:T(8,128)(2,1)S(1)} %fusion.61), channel_id=1, source_target_pairs={{128,0},{129,1},{130,2},{131,3},{132,4},{133,5},{134,6},{135,7},{1... | collective-permute-start | bytes 786440 | tf_op jit(solution)/shard_map/ppermute | solution.py:67
  109.2 9.9 %collective-permute-start.14 = (bf16[2,256,256]{1,2,0:T(8,128)(2,1)S(1)}, bf16[2,256,256]{1,2,0:T(8,128)(2,1)S(1)}, u32[]{:S(2)}, u32[]{:S(2)}) collective-permute-start(bf16[2,256,256]{1,2,0:T(8,128)(2,1)S(1)} %fusion.61), channel_id=1, source_target_pairs={{256,0},{257,1},{258,2},{259,3},{260,4},{261,5},{262,6},{263,7},{2... | collective-permute-start | bytes 786440 | tf_op jit(solution)/shard_map/ppermute | solution.py:67
  110.5 11.3 %collective-permute-start.15 = (bf16[2,256,256]{1,2,0:T(8,128)(2,1)S(1)}, bf16[2,256,256]{1,2,0:T(8,128)(2,1)S(1)}, u32[]{:S(2)}, u32[]{:S(2)}) collective-permute-start(bf16[2,256,256]{1,2,0:T(8,128)(2,1)S(1)} %fusion.61), channel_id=1, source_target_pairs={{384,0},{385,1},{386,2},{387,3},{388,4},{389,5},{390,6},{391,7},{3... | collective-permute-start | bytes 786440 | tf_op jit(solution)/shard_map/ppermute | solution.py:67
  113.2 9.7 %copy-start.3 = (f32[4,256,256]{1,2,0:T(8,128)S(1)}, f32[4,256,256]{1,2,0:T(8,128)}, u32[]{:S(2)}) copy-start(f32[4,256,256]{1,2,0:T(8,128)} %copy-done.2) | copy-start | bytes 3145732
  127.3 16.5 %all-to-all-start.1 = ((f32[16,2,512]{2,1,0:T(2,128)}), f32[16,2,512]{2,1,0:T(2,128)S(1)}, u32[]{:S(2)}, u32[]{:S(2)}) async-start(f32[16,2,512]{2,1,0:T(2,128)} %broadcast_in_dim.125), calls=%async_computation.1 | async-start | bytes 131072 | tf_op jit(solution)/shard_map/all_to_all | solution.py:25
  (18 other events, 44.2 us)

commit v4 on v3

--- a/solution.py
+++ b/solution.py
@@ -83,26 +83,43 @@
     return result
 
 
-def attend(q_head, g_head, k_set, v_set, visible, row_live):
+def attend_split(q, g, k_win, v_win, k_anc, v_anc, seen_win, seen_anc, row_live):
     factor = HD ** (-0.5)
-    scores = jnp.einsum("fqd,fkd->fqk", q_head, k_set, preferred_element_type=jnp.float32) * factor
-    scores = jnp.where(visible[:, None, :], scores, NEG)
-    row_max = jnp.max(scores, axis=2, keepdims=True)
-    row_sum = jnp.sum(jnp.exp(scores - row_max), axis=2, keepdims=True)
+    wide = jnp.float32
+    s_win = jnp.einsum("hfqd,hfkd->hfqk", q, k_win, preferred_element_type=wide) * factor
+    s_anc = jnp.einsum("hfqd,hkd->hfqk", q, k_anc, preferred_element_type=wide) * factor
+    s_win = jnp.where(seen_win[:, :, None, :], s_win, NEG)
+    s_anc = jnp.where(seen_anc[:, :, None, :], s_anc, NEG)
+    row_max = jnp.maximum(
+        jnp.max(s_win, axis=3, keepdims=True), jnp.max(s_anc, axis=3, keepdims=True)
+    )
+    row_sum = jnp.sum(jnp.exp(s_win - row_max), axis=3, keepdims=True) + jnp.sum(
+        jnp.exp(s_anc - row_max), axis=3, keepdims=True
+    )
     lse = row_max + jnp.log(row_sum)
-    prob_wide = jnp.exp(scores - lse)
-    prob = prob_wide.astype(jnp.bfloat16)
-    out_wide = jnp.einsum("fqk,fkd->fqd", prob, v_set, preferred_element_type=jnp.float32)
+    p_win = jnp.exp(s_win - lse)
+    p_anc = jnp.exp(s_anc - lse)
+    pb_win = p_win.astype(jnp.bfloat16)
+    pb_anc = p_anc.astype(jnp.bfloat16)
+    out = jnp.einsum("hfqk,hfkd->hfqd", pb_win, v_win, preferred_element_type=wide) + jnp.einsum(
+        "hfqk,hkd->hfqd", pb_anc, v_anc, preferred_element_type=wide
+    )
     attn = lax.optimization_barrier(
-        jnp.where(row_live[:, :, None], out_wide, 0.0).astype(jnp.bfloat16)
-    )
-    delta = jnp.sum(g_head.astype(jnp.float32) * attn.astype(jnp.float32), axis=2)
-    dprob = jnp.einsum("fqd,fkd->fqk", g_head, v_set, preferred_element_type=jnp.float32)
-    dscore = (prob_wide * (dprob - delta[:, :, None]) * factor).astype(jnp.bfloat16)
-    grad_qh = jnp.einsum("fqk,fkd->fqd", dscore, k_set, preferred_element_type=jnp.float32)
-    grad_kh = jnp.einsum("fqk,fqd->fkd", dscore, q_head, preferred_element_type=jnp.float32)
-    grad_vh = jnp.einsum("fqk,fqd->fkd", prob, g_head, preferred_element_type=jnp.float32)
-    return (attn, lse[:, :, 0], delta, grad_qh, grad_kh, grad_vh)
+        jnp.where(row_live[None, :, :, None], out, 0.0).astype(jnp.bfloat16)
+    )
+    delta = jnp.sum(g.astype(wide) * attn.astype(wide), axis=3, keepdims=True)
+    dp_win = jnp.einsum("hfqd,hfkd->hfqk", g, v_win, preferred_element_type=wide)
+    dp_anc = jnp.einsum("hfqd,hkd->hfqk", g, v_anc, preferred_element_type=wide)
+    ds_win = (p_win * (dp_win - delta) * factor).astype(jnp.bfloat16)
+    ds_anc = (p_anc * (dp_anc - delta) * factor).astype(jnp.bfloat16)
+    gk_anc = jnp.einsum("hfqk,hfqd->hkd", ds_anc, q, preferred_element_type=wide)
+    gv_anc = jnp.einsum("hfqk,hfqd->hkd", pb_anc, g, preferred_element_type=wide)
+    gq = jnp.einsum("hfqk,hfkd->hfqd", ds_win, k_win, preferred_element_type=wide) + jnp.einsum(
+        "hfqk,hkd->hfqd", ds_anc, k_anc, preferred_element_type=wide
+    )
+    gk_win = jnp.einsum("hfqk,hfqd->hfkd", ds_win, q, preferred_element_type=wide)
+    gv_win = jnp.einsum("hfqk,hfqd->hfkd", pb_win, g, preferred_element_type=wide)
+    return attn, gq, gk_win, gv_win, gk_anc, gv_anc
 
 
 def on_device(q_in, k_in, v_in, q_gain, k_gain, d_out, counts, windows):
@@ -128,26 +145,14 @@
     anchor_k, anchor_v = tree_bcast(jnp.stack([k_norm[:CAP], v_in[:CAP]]), "seq")
     k_near = jnp.concatenate([halo_k, k_norm], axis=0).reshape(2 * F_DEV, CAP, local_width)
     v_near = jnp.concatenate([halo_v, v_in], axis=0).reshape(2 * F_DEV, CAP, local_width)
-    k_set = jnp.concatenate(
-        [
-            stack_offsets(k_near, F_DEV, F_DEV),
-            jnp.broadcast_to(anchor_k[None], (F_DEV, CAP, local_width)),
-        ],
-        axis=1,
-    )
-    v_set = jnp.concatenate(
-        [
-            stack_offsets(v_near, F_DEV, F_DEV),
-            jnp.broadcast_to(anchor_v[None], (F_DEV, CAP, local_width)),
-        ],
-        axis=1,
-    )
-
     def to_heads(value):
         return value.reshape(value.shape[0], value.shape[1], local_heads, HD).transpose(2, 0, 1, 3)
 
     def from_heads(value):
         return value.transpose(1, 2, 0, 3).reshape(value.shape[1], value.shape[2], local_heads * HD)
+
+    def rows_to_heads(value):
+        return value.reshape(value.shape[0], local_heads, HD).transpose(1, 0, 2)
 
     frame_local = jnp.arange(F_DEV, dtype=jnp.int32)
     offsets = jnp.arange((F_DEV + 1) * CAP, dtype=jnp.int32) // CAP
@@ -156,29 +161,28 @@
     within = offsets[None, None, :] <= windows[:, None, None]
     anchor_ok = device * F_DEV + frame_local[None, :] - windows[:, None] > 0
     anchor_live = slot_index < counts[0]
-    visible = jnp.concatenate(
-        [(live_stack & reach)[None] & within, anchor_ok[:, :, None] & anchor_live[None, None, :]],
-        axis=2,
-    )
-
-    def per_head(items):
-        q_head, g_head, k_head, v_head, seen = items
-        return attend(q_head, g_head, k_head, v_head, seen, row_live)
+    seen_win = (live_stack & reach)[None] & within
+    seen_anc = anchor_ok[:, :, None] & anchor_live[None, None, :]
 
     q_heads = to_heads(q_norm.reshape(F_DEV, CAP, local_width))
     g_heads = to_heads(grad_mask.reshape(F_DEV, CAP, local_width))
-    attn_h, lse_h, delta_h, grad_qh, grad_kh, grad_vh = lax.map(
-        per_head, (q_heads, g_heads, to_heads(k_set), to_heads(v_set), visible)
+    attn_h, grad_qh, grad_kh, grad_vh, grad_ka, grad_va = attend_split(
+        q_heads,
+        g_heads,
+        to_heads(stack_offsets(k_near, F_DEV, F_DEV)),
+        to_heads(stack_offsets(v_near, F_DEV, F_DEV)),
+        rows_to_heads(anchor_k),
+        rows_to_heads(anchor_v),
+        seen_win,
+        seen_anc,
+        row_live,
     )
     attn_out = from_heads(attn_h).reshape(row_count, local_width)
     grad_qn = from_heads(grad_qh).reshape(row_count, local_width)
-    grad_k_all = from_heads(grad_kh)
-    grad_v_all = from_heads(grad_vh)
-    split = (F_DEV + 1) * CAP
-    grad_k_near = fold_offsets(grad_k_all[:, :split], F_DEV, F_DEV, CAP)
-    grad_v_near = fold_offsets(grad_v_all[:, :split], F_DEV, F_DEV, CAP)
-    grad_k_anchor = jnp.sum(grad_k_all[:, split:], axis=0)
-    grad_v_anchor = jnp.sum(grad_v_all[:, split:], axis=0)
+    grad_k_near = fold_offsets(from_heads(grad_kh), F_DEV, F_DEV, CAP)
+    grad_v_near = fold_offsets(from_heads(grad_vh), F_DEV, F_DEV, CAP)
+    grad_k_anchor = grad_ka.transpose(1, 0, 2).reshape(CAP, local_width)
+    grad_v_anchor = grad_va.transpose(1, 0, 2).reshape(CAP, local_width)
     back_k, back_v = shifted(jnp.stack([grad_k_near[:F_DEV], grad_v_near[:F_DEV]]), "seq", -1)
     grad_k_own = grad_k_near[F_DEV:] + back_k
     grad_v_own = grad_v_near[F_DEV:] + back_v

time: 147 us -> 139 us (0.946)
  waiting for transfers between devices: 49.2 us -> 41.4 us
  other arithmetic: 21.5 us -> 13.7 us
  local copies, waits for them, and re-layouts: 17.3 us -> 21.9 us
  matrix products: 8.11 us -> 10.7 us
    unnamed x25 -> x63, local copies, waits for them, and re-layouts: 2 us -> 6.33 us
    while x26 -> x0, local copies, waits for them, and re-layouts: 4.23 us -> none
    concatenate x9 -> x12, local copies, waits for them, and re-layouts: 2.61 us -> 6.44 us  [stack_offsets(): return jnp.concatenate(blocks, axis=1)]
    ppermute x7, waiting for transfers between devices: 18.9 us -> 15.7 us  [tree_reduce(): arrived = lax.ppermute(sent, axis, route)]
    all_to_all x2, waiting for transfers between devices: 17.1 us -> 14 us  [gather_sum(): return jnp.sum(lax.all_to_all(copies, axis, 0, 0, tiled=False), axis=0)]
    another operation x0 -> x3, local copies, waits for them, and re-layouts: none -> 3.04 us  [the longest x2 1.77 us: rows_to_heads(): return value.reshape(value.shape[0], local_heads, HD).transpose(1, 0, 2)]
    all_to_all x2, starting transfers between devices: 20.8 us -> 23.6 us  [gather_sum(): return jnp.sum(lax.all_to_all(copies, axis, 0, 0, tiled=False), axis=0)]
    transpose x2 -> x0, other arithmetic: 2.68 us -> none  [to_heads(): value.reshape(value.shape[0], value.shape[1], local_heads, HD)]
  transfers between devices with their start and end apart: 18 -> 18, of which waited for: 11 -> 10; matrix products, arithmetic and copies ran while one was open for 11% -> 19% of each run, Pallas kernels for 0% -> 0%
where the time goes in v4:
time: 139 us; the launch traced here: 138 us
  starting transfers between devices  48.5 us (35%)
  waiting for transfers between devices  41.4 us (30%)
  local copies, waits for them, and re-layouts  21.9 us (16%)
  other arithmetic  13.7 us (10%)
  matrix products  10.7 us (8%)
  between operations  1.56 us (1%)
    all_to_all x2, starting transfers between devices, gather_sum(): return jnp.sum(lax.all_to_all(copies, axis, 0, 0, tiled=False), axis=0)  23.6 us
    ppermute x7, waiting for transfers between devices, tree_reduce(): arrived = lax.ppermute(sent, axis, route)  15.7 us
    all_to_all x2, waiting for transfers between devices, gather_sum(): return jnp.sum(lax.all_to_all(copies, axis, 0, 0, tiled=False), axis=0)  14 us
    ppermute x7, starting transfers between devices, tree_bcast(): arrived = lax.ppermute(values, axis, route)  12.8 us
    ppermute x7, waiting for transfers between devices, tree_bcast(): arrived = lax.ppermute(values, axis, route)  11.7 us
    ppermute x7, starting transfers between devices, tree_reduce(): arrived = lax.ppermute(sent, axis, route)  9.36 us
    concatenate x12, local copies, waits for them, and re-layouts, stack_offsets(): return jnp.concatenate(blocks, axis=1)  6.44 us
    unnamed x63, local copies, waits for them, and re-layouts  6.33 us
  transfers between devices with their start and end apart: 18, of which 10 were waited for; matrix products, arithmetic and copies ran while one was open for 19% of the time, Pallas kernels for 0%

profile of v4, /device:TPU:8, one launch (start us, length us, event | category | flops | bytes accessed | tf_op | source)
XLA Modules:
  0.0 137.7 jit_solution(8674253329415420911)
XLA Ops:
  3.7 16.0 %all-to-all-start = ((f32[16,2,512]{2,1,0:T(2,128)}), f32[16,2,512]{2,1,0:T(2,128)S(1)}, u32[]{:S(2)}, u32[]{:S(2)}) async-start(f32[16,2,512]{2,1,0:T(2,128)} %broadcast_in_dim.58), calls=%async_computation | async-start | bytes 131072 | tf_op jit(solution)/shard_map/all_to_all | solution.py:25
  26.9 4.4 %all-to-all-done = f32[16,2,512]{2,1,0:T(2,128)S(1)} async-done(((f32[16,2,512]{2,1,0:T(2,128)}), f32[16,2,512]{2,1,0:T(2,128)S(1)}, u32[]{:S(2)}, u32[]{:S(2)}) %all-to-all-start) | async-done | bytes 65568 | tf_op jit(solution)/shard_map/all_to_all | solution.py:25
  31.5 3.4 %collective-permute-start.3 = (bf16[2,256,256]{1,2,0:T(8,128)(2,1)S(1)}, bf16[2,256,256]{1,2,0:T(8,128)(2,1)S(1)}, u32[]{:S(2)}, u32[]{:S(2)}) collective-permute-start(bf16[2,256,256]{1,2,0:T(8,128)(2,1)S(1)} %pad_maximum_fusion.5), channel_id=1, source_target_pairs={{0,128},{1,129},{2,130},{3,131},{4,132},{5,133},{6,134},{7,135},{8... | collective-permute-start | bytes 786440 | tf_op jit(solution)/shard_map/ppermute | solution.py:52
  34.9 2.2 %collective-permute-start.2 = (bf16[2,256,256]{1,2,0:T(8,128)(2,1)S(1)}, bf16[2,256,256]{1,2,0:T(8,128)(2,1)S(1)}, u32[]{:S(2)}, u32[]{:S(2)}) collective-permute-start(bf16[2,256,256]{1,2,0:T(8,128)(2,1)S(1)} %pad_maximum_fusion.5), channel_id=1, source_target_pairs={{0,256},{1,257},{2,258},{3,259},{4,260},{5,261},{6,262},{7,263},{8... | collective-permute-start | bytes 786440 | tf_op jit(solution)/shard_map/ppermute | solution.py:52
  37.1 1.3 collective-permute-start.1
  38.6 1.3 collective-permute-start
  40.0 7.3 %collective-permute-done.2 = bf16[2,256,256]{1,2,0:T(8,128)(2,1)S(1)} collective-permute-done((bf16[2,256,256]{1,2,0:T(8,128)(2,1)S(1)}, bf16[2,256,256]{1,2,0:T(8,128)(2,1)S(1)}, u32[]{:S(2)}, u32[]{:S(2)}) %collective-permute-start.2) | collective-permute-done | bytes 262176 | tf_op jit(solution)/shard_map/ppermute | solution.py:52
  48.6 1.3 collective-permute-start.5
  50.0 1.3 collective-permute-start.4
  53.7 1.6 %collective-permute-done.5 = bf16[2,256,256]{1,2,0:T(8,128)(2,1)S(1)} collective-permute-done((bf16[2,256,256]{1,2,0:T(8,128)(2,1)S(1)}, bf16[2,256,256]{1,2,0:T(8,128)(2,1)S(1)}, u32[]{:S(2)}, u32[]{:S(2)}) %collective-permute-start.5) | collective-permute-done | bytes 262176 | tf_op jit(solution)/shard_map/ppermute | solution.py:52
  55.3 2.8 %collective-permute-done.4 = bf16[2,256,256]{1,2,0:T(8,128)(2,1)S(1)} collective-permute-done((bf16[2,256,256]{1,2,0:T(8,128)(2,1)S(1)}, bf16[2,256,256]{1,2,0:T(8,128)(2,1)S(1)}, u32[]{:S(2)}, u32[]{:S(2)}) %collective-permute-start.4) | collective-permute-done | bytes 262176 | tf_op jit(solution)/shard_map/ppermute | solution.py:52
  58.9 2.0 %collective-permute-start.7 = (bf16[2,256,256]{1,2,0:T(8,128)(2,1)}, bf16[2,256,256]{1,2,0:T(8,128)(2,1)}, u32[]{:S(2)}, u32[]{:S(2)}) collective-permute-start(bf16[2,256,256]{1,2,0:T(8,128)(2,1)} %select_select_fusion), channel_id=1, source_target_pairs={{0,16},{32,48},{64,80},{96,112},{128,144},{160,176},{192,208},{224... | collective-permute-start | bytes 786440 | tf_op jit(solution)/shard_map/ppermute | solution.py:52
  64.8 2.5 %fusion.1 = (f32[2,2,256]{2,1,0:T(2,128)}, f32[2,2,256,768]{3,2,1,0:T(8,128)S(1)}) fusion(pred[2,2,768]{2,1,0:T(4,128)(4,1)S(1)} %broadcast_and_fusion, bf16[2,256,2,128]{3,1,0,2:T(8,128)(2,1)} %copy.147, bf16[2,256,2,128]{3,1,0,2:T(8,128)(2,1)} %copy.146, bf16[2,256,2,128]{3,1,0,2:T(8,128)(2,1)} %copy.145, bf16[2,256,2,128]{1,0,3,2:T(2,128)(2,1)} %reshape_reshape.12), kind=kOutput, calls=%fused_computation.5 | convolution fusion | flops 206044160 | bytes 4201472 | tf_op jit(solution)/shard_map/hfqd,hfkd->hfqk/dot_general | solution.py:89
  70.7 1.3 fusion.85
  89.6 3.7 %collective-permute-done.12 = bf16[2,256,256]{1,2,0:T(8,128)(2,1)S(1)} collective-permute-done((bf16[2,256,256]{1,2,0:T(8,128)(2,1)S(1)}, bf16[2,256,256]{1,2,0:T(8,128)(2,1)S(1)}, u32[]{:S(2)}, u32[]{:S(2)}) %collective-permute-start.12) | collective-permute-done | bytes 262176 | tf_op jit(solution)/shard_map/ppermute | solution.py:67
  93.2 2.7 %collective-permute-done.11 = bf16[2,256,256]{1,2,0:T(8,128)(2,1)S(1)} collective-permute-done((bf16[2,256,256]{1,2,0:T(8,128)(2,1)S(1)}, bf16[2,256,256]{1,2,0:T(8,128)(2,1)S(1)}, u32[]{:S(2)}, u32[]{:S(2)}) %collective-permute-start.11) | collective-permute-done | bytes 262176 | tf_op jit(solution)/shard_map/ppermute | solution.py:67
  95.9 2.7 %collective-permute-done.10 = bf16[2,256,256]{1,2,0:T(8,128)(2,1)S(1)} collective-permute-done((bf16[2,256,256]{1,2,0:T(8,128)(2,1)S(1)}, bf16[2,256,256]{1,2,0:T(8,128)(2,1)S(1)}, u32[]{:S(2)}, u32[]{:S(2)}) %collective-permute-start.10) | collective-permute-done | bytes 262176 | tf_op jit(solution)/shard_map/ppermute | solution.py:67
  99.5 1.6 %collective-permute-start.15 = (bf16[2,256,256]{1,2,0:T(8,128)(2,1)}, bf16[2,256,256]{1,2,0:T(8,128)(2,1)}, u32[]{:S(2)}, u32[]{:S(2)}) collective-permute-start(bf16[2,256,256]{1,2,0:T(8,128)(2,1)} %fusion.79), channel_id=1, source_target_pairs={{384,0},{385,1},{386,2},{387,3},{388,4},{389,5},{390,6},{391,7},{3... | collective-permute-start | bytes 786440 | tf_op jit(solution)/shard_map/ppermute | solution.py:67
  103.8 1.4 %fusion.6 = f32[2,256,2,128]{3,1,0,2:T(8,128)} fusion(f32[2,2,256,128]{3,2,1,0:T(8,128)S(1)} %fusion.56, bf16[2,2,256,768]{3,2,1,0:T(8,128)(2,1)S(1)} %multiply_convert_fusion, bf16[2,256,2,128]{3,1,0,2:T(8,128)(2,1)S(1)} %copy-done.17, bf16[2,256,2,128]{3,1,0,2:T(8,128)(2,1)S(1)} %copy-done.16, bf16[2,256,2,128]{3,1,0,2:T(8,128)(2,1)S(1)} %copy-done.14), kind=kOutput, calls=%fused_computation.15 | convolution fusion | flops 203816960 | bytes 3407872 | tf_op jit(solution)/shard_map/hfqk,hfkd->hfqd/dot_general | solution.py:117
  106.7 5.7 %collective-permute-done.15 = bf16[2,256,256]{1,2,0:T(8,128)(2,1)} collective-permute-done((bf16[2,256,256]{1,2,0:T(8,128)(2,1)}, bf16[2,256,256]{1,2,0:T(8,128)(2,1)}, u32[]{:S(2)}, u32[]{:S(2)}) %collective-permute-start.15) | collective-permute-done | bytes 262176 | tf_op jit(solution)/shard_map/ppermute | solution.py:67
  112.5 1.6 %convert_add_fusion = f32[2,256,256]{1,2,0:T(8,128)S(1)} fusion(bf16[2,256,256]{1,2,0:T(8,128)(2,1)} %collective-permute-done.15, bf16[2,256,256]{1,2,0:T(8,128)(2,1)} %collective-permute-done.14, bf16[2,256,256]{1,2,0:T(8,128)(2,1)} %collective-permute-done.13, bf16[2,256,256]{1,2,0:T(8,128)(2,1)} %copy-done.11, bf16[2,256,256]{1,2,0:T(8,128)(2,1)} %copy-done.12, ...), kind=kLoop, calls=%fused_computation.59 | loop fusion | flops 1966080 | bytes 2883584 | tf_op jit(solution)/shard_map/add | solution.py:68
  114.1 1.4 fusion.26
  116.5 7.6 %all-to-all-start.1 = ((f32[16,2,512]{2,1,0:T(2,128)}), f32[16,2,512]{2,1,0:T(2,128)S(1)}, u32[]{:S(2)}, u32[]{:S(2)}) async-start(f32[16,2,512]{2,1,0:T(2,128)} %broadcast_in_dim.103), calls=%async_computation.1 | async-start | bytes 131072 | tf_op jit(solution)/shard_map/all_to_all | solution.py:25
  126.1 9.6 %all-to-all-done.1 = f32[16,2,512]{2,1,0:T(2,128)S(1)} async-done(((f32[16,2,512]{2,1,0:T(2,128)}), f32[16,2,512]{2,1,0:T(2,128)S(1)}, u32[]{:S(2)}, u32[]{:S(2)}) %all-to-all-start.1) | async-done | bytes 65568 | tf_op jit(solution)/shard_map/all_to_all | solution.py:25
  (168 shorter events, 49.3 us)
Async XLA Ops:
  0.6 25.4 %copy-start.27 = (s32[2]{0:T(128)S(1)}, s32[2]{0:T(128)}, u32[]{:S(2)}) copy-start(s32[2]{0:T(128)} %param.19) | copy-start | bytes 28
  0.6 30.7 %copy-start.20 = (f32[256]{0:T(256)S(1)}, f32[256]{0:T(256)}, u32[]{:S(2)}) copy-start(f32[256]{0:T(256)} %param.16) | copy-start | bytes 3076
  2.9 48.3 %copy-start = (bf16[512,256]{0,1:T(8,128)(2,1)}, bf16[512,256]{0,1:T(8,128)(2,1)S(1)}, u32[]{:S(2)}) copy-start(bf16[512,256]{0,1:T(8,128)(2,1)S(1)} %copy.137) | copy-start | bytes 786436
  3.7 27.6 %all-to-all-start = ((f32[16,2,512]{2,1,0:T(2,128)}), f32[16,2,512]{2,1,0:T(2,128)S(1)}, u32[]{:S(2)}, u32[]{:S(2)}) async-start(f32[16,2,512]{2,1,0:T(2,128)} %broadcast_in_dim.58), calls=%async_computation | async-start | bytes 131072 | tf_op jit(solution)/shard_map/all_to_all | solution.py:25
  21.8 29.4 %copy-start.22 = (f32[256]{0:T(256)S(1)}, f32[256]{0:T(256)}, u32[]{:S(2)}) copy-start(f32[256]{0:T(256)} %param.15) | copy-start | bytes 3076
  31.5 8.5 %collective-permute-start.3 = (bf16[2,256,256]{1,2,0:T(8,128)(2,1)S(1)}, bf16[2,256,256]{1,2,0:T(8,128)(2,1)S(1)}, u32[]{:S(2)}, u32[]{:S(2)}) collective-permute-start(bf16[2,256,256]{1,2,0:T(8,128)(2,1)S(1)} %pad_maximum_fusion.5), channel_id=1, source_target_pairs={{0,128},{1,129},{2,130},{3,131},{4,132},{5,133},{6,134},{7,135},{8... | collective-permute-start | bytes 786440 | tf_op jit(solution)/shard_map/ppermute | solution.py:52
  34.9 12.3 %collective-permute-start.2 = (bf16[2,256,256]{1,2,0:T(8,128)(2,1)S(1)}, bf16[2,256,256]{1,2,0:T(8,128)(2,1)S(1)}, u32[]{:S(2)}, u32[]{:S(2)}) collective-permute-start(bf16[2,256,256]{1,2,0:T(8,128)(2,1)S(1)} %pad_maximum_fusion.5), channel_id=1, source_target_pairs={{0,256},{1,257},{2,258},{3,259},{4,260},{5,261},{6,262},{7,263},{8... | collective-permute-start | bytes 786440 | tf_op jit(solution)/shard_map/ppermute | solution.py:52
  37.1 10.1 %collective-permute-start.1 = (bf16[2,256,256]{1,2,0:T(8,128)(2,1)S(1)}, bf16[2,256,256]{1,2,0:T(8,128)(2,1)S(1)}, u32[]{:S(2)}, u32[]{:S(2)}) collective-permute-start(bf16[2,256,256]{1,2,0:T(8,128)(2,1)S(1)} %pad_maximum_fusion.5), channel_id=1, source_target_pairs={{0,384},{1,385},{2,386},{3,387},{4,388},{5,389},{6,390},{7,391},{8... | collective-permute-start | bytes 786440 | tf_op jit(solution)/shard_map/ppermute | solution.py:52
  38.6 22.2 %collective-permute-start = (bf16[2,512,256]{1,2,0:T(8,128)(2,1)S(1)}, bf16[2,512,256]{1,2,0:T(8,128)(2,1)S(1)}, u32[]{:S(2)}, u32[]{:S(2)}) collective-permute-start(bf16[2,512,256]{1,2,0:T(8,128)(2,1)S(1)} %pad_maximum_fusion.1), channel_id=1, source_target_pairs={{0,16},{16,32},{32,48},{48,64},{64,80},{80,96},{96,112},{112,128},... | collective-permute-start | bytes 1572872 | tf_op jit(solution)/shard_map/ppermute | solution.py:19
  47.3 6.4 %collective-permute-start.6 = (bf16[2,256,256]{1,2,0:T(8,128)(2,1)S(1)}, bf16[2,256,256]{1,2,0:T(8,128)(2,1)S(1)}, u32[]{:S(2)}, u32[]{:S(2)}) collective-permute-start(bf16[2,256,256]{1,2,0:T(8,128)(2,1)S(1)} %select_select_fusion.1), channel_id=1, source_target_pairs={{0,32},{128,160},{256,288},{384,416},{1,33},{129,161},{257,289},{3... | collective-permute-start | bytes 786440 | tf_op jit(solution)/shard_map/ppermute | solution.py:52
  48.6 6.7 %collective-permute-start.5 = (bf16[2,256,256]{1,2,0:T(8,128)(2,1)S(1)}, bf16[2,256,256]{1,2,0:T(8,128)(2,1)S(1)}, u32[]{:S(2)}, u32[]{:S(2)}) collective-permute-start(bf16[2,256,256]{1,2,0:T(8,128)(2,1)S(1)} %select_select_fusion.1), channel_id=1, source_target_pairs={{0,64},{128,192},{256,320},{384,448},{1,65},{129,193},{257,321},{3... | collective-permute-start | bytes 786440 | tf_op jit(solution)/shard_map/ppermute | solution.py:52
  50.0 8.2 %collective-permute-start.4 = (bf16[2,256,256]{1,2,0:T(8,128)(2,1)S(1)}, bf16[2,256,256]{1,2,0:T(8,128)(2,1)S(1)}, u32[]{:S(2)}, u32[]{:S(2)}) collective-permute-start(bf16[2,256,256]{1,2,0:T(8,128)(2,1)S(1)} %select_select_fusion.1), channel_id=1, source_target_pairs={{0,96},{128,224},{256,352},{384,480},{1,97},{129,225},{257,353},{3... | collective-permute-start | bytes 786440 | tf_op jit(solution)/shard_map/ppermute | solution.py:52
  58.9 8.4 %collective-permute-start.7 = (bf16[2,256,256]{1,2,0:T(8,128)(2,1)}, bf16[2,256,256]{1,2,0:T(8,128)(2,1)}, u32[]{:S(2)}, u32[]{:S(2)}) collective-permute-start(bf16[2,256,256]{1,2,0:T(8,128)(2,1)} %select_select_fusion), channel_id=1, source_target_pairs={{0,16},{32,48},{64,80},{96,112},{128,144},{160,176},{192,208},{224... | collective-permute-start | bytes 786440 | tf_op jit(solution)/shard_map/ppermute | solution.py:52
  74.2 24.4 %copy-start.3 = (f32[2,256,128,1]{1,2,3,0:T(8,128)}, f32[2,256,128,1]{1,2,3,0:T(8,128)S(1)}, u32[]{:S(2)}) copy-start(f32[2,256,128,1]{1,2,3,0:T(8,128)S(1)} %fusion.35) | copy-start | bytes 786436
  79.5 3.4 %collective-permute-start.9 = (bf16[2,256,256]{1,2,0:T(8,128)(2,1)S(1)}, bf16[2,256,256]{1,2,0:T(8,128)(2,1)S(1)}, u32[]{:S(2)}, u32[]{:S(2)}) collective-permute-start(bf16[2,256,256]{1,2,0:T(8,128)(2,1)S(1)} %fusion.28), channel_id=1, source_target_pairs={{16,0},{48,32},{80,64},{112,96},{144,128},{176,160},{208,192},{240... | collective-permute-start | bytes 786440 | tf_op jit(solution)/shard_map/ppermute | solution.py:67
  82.0 21.8 %copy-start.14 = (bf16[2,256,2,128]{3,1,0,2:T(8,128)(2,1)S(1)}, bf16[2,256,2,128]{3,1,0,2:T(8,128)(2,1)}, u32[]{:S(2)}) copy-start(bf16[2,256,2,128]{3,1,0,2:T(8,128)(2,1)} %copy.145) | copy-start | bytes 786436
  83.0 10.3 %collective-permute-start.12 = (bf16[2,256,256]{1,2,0:T(8,128)(2,1)S(1)}, bf16[2,256,256]{1,2,0:T(8,128)(2,1)S(1)}, u32[]{:S(2)}, u32[]{:S(2)}) collective-permute-start(bf16[2,256,256]{1,2,0:T(8,128)(2,1)S(1)} %fusion.30), channel_id=1, source_target_pairs={{96,0},{224,128},{352,256},{480,384},{97,1},{225,129},{353,257},{4... | collective-permute-start | bytes 786440 | tf_op jit(solution)/shard_map/ppermute | solution.py:67
  84.3 11.7 %collective-permute-start.11 = (bf16[2,256,256]{1,2,0:T(8,128)(2,1)S(1)}, bf16[2,256,256]{1,2,0:T(8,128)(2,1)S(1)}, u32[]{:S(2)}, u32[]{:S(2)}) collective-permute-start(bf16[2,256,256]{1,2,0:T(8,128)(2,1)S(1)} %fusion.30), channel_id=1, source_target_pairs={{64,0},{192,128},{320,256},{448,384},{65,1},{193,129},{321,257},{4... | collective-permute-start | bytes 786440 | tf_op jit(solution)/shard_map/ppermute | solution.py:67
  85.6 13.1 %collective-permute-start.10 = (bf16[2,256,256]{1,2,0:T(8,128)(2,1)S(1)}, bf16[2,256,256]{1,2,0:T(8,128)(2,1)S(1)}, u32[]{:S(2)}, u32[]{:S(2)}) collective-permute-start(bf16[2,256,256]{1,2,0:T(8,128)(2,1)S(1)} %fusion.30), channel_id=1, source_target_pairs={{32,0},{160,128},{288,256},{416,384},{33,1},{161,129},{289,257},{4... | collective-permute-start | bytes 786440 | tf_op jit(solution)/shard_map/ppermute | solution.py:67
  87.9 26.2 %collective-permute-start.8 = (f32[2,2,256,256]{2,3,1,0:T(8,128)}, f32[2,2,256,256]{2,3,1,0:T(8,128)}, u32[]{:S(2)}, u32[]{:S(2)}) collective-permute-start(f32[2,2,256,256]{2,3,1,0:T(8,128)} %pad_maximum_fusion), channel_id=1, source_target_pairs={{16,0},{32,16},{48,32},{64,48},{80,64},{96,80},{112,96},{128,112},... | collective-permute-start | bytes 3145736 | tf_op jit(solution)/shard_map/ppermute | solution.py:19
  99.5 12.9 %collective-permute-start.15 = (bf16[2,256,256]{1,2,0:T(8,128)(2,1)}, bf16[2,256,256]{1,2,0:T(8,128)(2,1)}, u32[]{:S(2)}, u32[]{:S(2)}) collective-permute-start(bf16[2,256,256]{1,2,0:T(8,128)(2,1)} %fusion.79), channel_id=1, source_target_pairs={{384,0},{385,1},{386,2},{387,3},{388,4},{389,5},{390,6},{391,7},{3... | collective-permute-start | bytes 786440 | tf_op jit(solution)/shard_map/ppermute | solution.py:67
  101.2 11.3 %collective-permute-start.14 = (bf16[2,256,256]{1,2,0:T(8,128)(2,1)}, bf16[2,256,256]{1,2,0:T(8,128)(2,1)}, u32[]{:S(2)}, u32[]{:S(2)}) collective-permute-start(bf16[2,256,256]{1,2,0:T(8,128)(2,1)} %fusion.79), channel_id=1, source_target_pairs={{256,0},{257,1},{258,2},{259,3},{260,4},{261,5},{262,6},{263,7},{2... | collective-permute-start | bytes 786440 | tf_op jit(solution)/shard_map/ppermute | solution.py:67
  102.5 10.0 %collective-permute-start.13 = (bf16[2,256,256]{1,2,0:T(8,128)(2,1)}, bf16[2,256,256]{1,2,0:T(8,128)(2,1)}, u32[]{:S(2)}, u32[]{:S(2)}) collective-permute-start(bf16[2,256,256]{1,2,0:T(8,128)(2,1)} %fusion.79), channel_id=1, source_target_pairs={{128,0},{129,1},{130,2},{131,3},{132,4},{133,5},{134,6},{135,7},{1... | collective-permute-start | bytes 786440 | tf_op jit(solution)/shard_map/ppermute | solution.py:67
  116.5 19.1 %all-to-all-start.1 = ((f32[16,2,512]{2,1,0:T(2,128)}), f32[16,2,512]{2,1,0:T(2,128)S(1)}, u32[]{:S(2)}, u32[]{:S(2)}) async-start(f32[16,2,512]{2,1,0:T(2,128)} %broadcast_in_dim.103), calls=%async_computation.1 | async-start | bytes 131072 | tf_op jit(solution)/shard_map/all_to_all | solution.py:25
  (22 other events, 164.5 us)

commit v5 on v4

--- a/solution.py
+++ b/solution.py
@@ -1,3 +1,5 @@
+import functools
+
 import jax
 import jax.numpy as jnp
 from jax import lax
@@ -38,19 +40,33 @@
     for f in fans:
         plan.append((step, f))
         step *= f
-    return plan
+    return plan[::-1]
+
+
+def digit(i, step, fan):
+    return (i // step) % fan
+
+
+def tree_rounds(n):
+    done = []
+    for step, fan in tree_plan(n):
+        base = [i for i in range(n) if digit(i, step, fan) == 0 and all(digit(i, s, f) == 0 for s, f in done)]
+        yield step, fan, list(done), base
+        done.append((step, fan))
 
 
 def tree_bcast(values, axis):
     n = lax.axis_size(axis)
     me = lax.axis_index(axis)
-    for step, fan in reversed(tree_plan(n)):
-        span = step * fan
+    for step, fan, done, base in reversed(list(tree_rounds(n))):
+        clear = functools.reduce(
+            lambda acc, sf: acc & (digit(me, *sf) == 0), done, jnp.bool_(True)
+        )
         got = values
         for j in range(1, fan):
-            route = [(i, i + j * step) for i in range(0, n, span) if i + j * step < n]
+            route = [(i, i + j * step) for i in base if i + j * step < n]
             arrived = lax.ppermute(values, axis, route)
-            hit = me % span == j * step
+            hit = clear & (digit(me, step, fan) == j)
             got = jax.tree.map(lambda a, g: jnp.where(hit, a, g), arrived, got)
         values = got
     return values
@@ -58,11 +74,10 @@
 
 def tree_reduce(values, axis, wire):
     n = lax.axis_size(axis)
-    for step, fan in tree_plan(n):
-        span = step * fan
+    for step, fan, done, base in tree_rounds(n):
         total = values
         for j in range(1, fan):
-            route = [(i + j * step, i) for i in range(0, n, span) if i + j * step < n]
+            route = [(i + j * step, i) for i in base if i + j * step < n]
             sent = jax.tree.map(lambda a: a.astype(wire), values)
             arrived = lax.ppermute(sent, axis, route)
             total = jax.tree.map(lambda t, a: t + a.astype(t.dtype), total, arrived)

time: 139 us -> 156 us (1.12)
  the two profiles are of different devices: /device:TPU:8 before, /device:TPU:1 now
where the time goes in v5:
time: 156 us; the launch traced here: 155 us
  waiting for transfers between devices  54.6 us (35%)
  starting transfers between devices  53.4 us (34%)
  local copies, waits for them, and re-layouts  22.1 us (14%)
  other arithmetic  13.2 us (8%)
  matrix products  10.6 us (7%)
  between operations  1.56 us (1%)
    ppermute x7, waiting for transfers between devices, tree_reduce(): arrived = lax.ppermute(sent, axis, route)  23.9 us
    all_to_all x2, starting transfers between devices, gather_sum(): return jnp.sum(lax.all_to_all(copies, axis, 0, 0, tiled=False), axis=0)  21.7 us
    all_to_all x2, waiting for transfers between devices, gather_sum(): return jnp.sum(lax.all_to_all(copies, axis, 0, 0, tiled=False), axis=0)  14.8 us
    ppermute x7, starting transfers between devices, tree_bcast(): arrived = lax.ppermute(values, axis, route)  14.3 us
    ppermute x7, waiting for transfers between devices, tree_bcast(): arrived = lax.ppermute(values, axis, route)  12.9 us
    ppermute x7, starting transfers between devices, tree_reduce(): arrived = lax.ppermute(sent, axis, route)  10.9 us
    ppermute x2, starting transfers between devices, shifted(): return lax.ppermute(block, axis, route)  6.55 us
    unnamed x59, local copies, waits for them, and re-layouts  6.45 us
  transfers between devices with their start and end apart: 18, of which 10 were waited for; matrix products, arithmetic and copies ran while one was open for 18% of the time, Pallas kernels for 0%

profile of v5, /device:TPU:1, one launch (start us, length us, event | category | flops | bytes accessed | tf_op | source)
XLA Modules:
  0.0 155.5 jit_solution(738194909715206122)
XLA Ops:
  3.7 16.2 %all-to-all-start = ((f32[16,2,512]{2,1,0:T(2,128)}), f32[16,2,512]{2,1,0:T(2,128)S(1)}, u32[]{:S(2)}, u32[]{:S(2)}) async-start(f32[16,2,512]{2,1,0:T(2,128)} %broadcast_in_dim.58), calls=%async_computation | async-start | bytes 131072 | tf_op jit(solution)/shard_map/all_to_all | solution.py:27
  26.8 4.9 %all-to-all-done = f32[16,2,512]{2,1,0:T(2,128)S(1)} async-done(((f32[16,2,512]{2,1,0:T(2,128)}), f32[16,2,512]{2,1,0:T(2,128)S(1)}, u32[]{:S(2)}, u32[]{:S(2)}) %all-to-all-start) | async-done | bytes 65568 | tf_op jit(solution)/shard_map/all_to_all | solution.py:27
  33.5 4.5 %collective-permute-start = (bf16[2,512,256]{1,2,0:T(8,128)(2,1)S(1)}, bf16[2,512,256]{1,2,0:T(8,128)(2,1)S(1)}, u32[]{:S(2)}, u32[]{:S(2)}) collective-permute-start(bf16[2,512,256]{1,2,0:T(8,128)(2,1)S(1)} %pad_maximum_fusion.1), channel_id=1, source_target_pairs={{0,16},{16,32},{32,48},{48,64},{64,80},{80,96},{96,112},{112,128},... | collective-permute-start | bytes 1572872 | tf_op jit(solution)/shard_map/ppermute | solution.py:21
  38.7 3.1 %collective-permute-start.4 = (bf16[2,256,256]{1,2,0:T(8,128)(2,1)}, bf16[2,256,256]{1,2,0:T(8,128)(2,1)S(1)}, u32[]{:S(2)}, u32[]{:S(2)}) collective-permute-start(bf16[2,256,256]{1,2,0:T(8,128)(2,1)} %broadcast_select_fusion.1), channel_id=1, source_target_pairs={{0,32},{16,48},{1,33},{17,49},{2,34},{18,50},{3,35},{19,51},{4,36}... | collective-permute-start | bytes 786440 | tf_op jit(solution)/shard_map/ppermute | solution.py:68
  41.8 1.6 %collective-permute-start.3 = (bf16[2,256,256]{1,2,0:T(8,128)(2,1)}, bf16[2,256,256]{1,2,0:T(8,128)(2,1)S(1)}, u32[]{:S(2)}, u32[]{:S(2)}) collective-permute-start(bf16[2,256,256]{1,2,0:T(8,128)(2,1)} %broadcast_select_fusion.1), channel_id=1, source_target_pairs={{0,64},{16,80},{1,65},{17,81},{2,66},{18,82},{3,67},{19,83},{4,68}... | collective-permute-start | bytes 786440 | tf_op jit(solution)/shard_map/ppermute | solution.py:68
  43.4 2.3 %collective-permute-start.2 = (bf16[2,256,256]{1,2,0:T(8,128)(2,1)}, bf16[2,256,256]{1,2,0:T(8,128)(2,1)}, u32[]{:S(2)}, u32[]{:S(2)}) collective-permute-start(bf16[2,256,256]{1,2,0:T(8,128)(2,1)} %broadcast_select_fusion.1), channel_id=1, source_target_pairs={{0,96},{16,112},{1,97},{17,113},{2,98},{18,114},{3,99},{19,115},{4... | collective-permute-start | bytes 786440 | tf_op jit(solution)/shard_map/ppermute | solution.py:68
  48.1 3.8 %collective-permute-done.4 = bf16[2,256,256]{1,2,0:T(8,128)(2,1)S(1)} collective-permute-done((bf16[2,256,256]{1,2,0:T(8,128)(2,1)}, bf16[2,256,256]{1,2,0:T(8,128)(2,1)S(1)}, u32[]{:S(2)}, u32[]{:S(2)}) %collective-permute-start.4) | collective-permute-done | bytes 262176 | tf_op jit(solution)/shard_map/ppermute | solution.py:68
  51.9 5.6 %collective-permute-done.3 = bf16[2,256,256]{1,2,0:T(8,128)(2,1)S(1)} collective-permute-done((bf16[2,256,256]{1,2,0:T(8,128)(2,1)}, bf16[2,256,256]{1,2,0:T(8,128)(2,1)S(1)}, u32[]{:S(2)}, u32[]{:S(2)}) %collective-permute-start.3) | collective-permute-done | bytes 262176 | tf_op jit(solution)/shard_map/ppermute | solution.py:68
  57.5 3.5 %collective-permute-done.2 = bf16[2,256,256]{1,2,0:T(8,128)(2,1)} collective-permute-done((bf16[2,256,256]{1,2,0:T(8,128)(2,1)}, bf16[2,256,256]{1,2,0:T(8,128)(2,1)}, u32[]{:S(2)}, u32[]{:S(2)}) %collective-permute-start.2) | collective-permute-done | bytes 262176 | tf_op jit(solution)/shard_map/ppermute | solution.py:68
  61.7 2.0 %collective-permute-start.7 = (bf16[2,256,256]{1,2,0:T(8,128)(2,1)}, bf16[2,256,256]{1,2,0:T(8,128)(2,1)}, u32[]{:S(2)}, u32[]{:S(2)}) collective-permute-start(bf16[2,256,256]{1,2,0:T(8,128)(2,1)} %select_select_fusion.1), channel_id=1, source_target_pairs={{0,128},{16,144},{32,160},{48,176},{64,192},{80,208},{96,224},{112... | collective-permute-start | bytes 786440 | tf_op jit(solution)/shard_map/ppermute | solution.py:68
  63.7 2.0 %collective-permute-start.6 = (bf16[2,256,256]{1,2,0:T(8,128)(2,1)}, bf16[2,256,256]{1,2,0:T(8,128)(2,1)}, u32[]{:S(2)}, u32[]{:S(2)}) collective-permute-start(bf16[2,256,256]{1,2,0:T(8,128)(2,1)} %select_select_fusion.1), channel_id=1, source_target_pairs={{0,256},{16,272},{32,288},{48,304},{64,320},{80,336},{96,352},{112... | collective-permute-start | bytes 786440 | tf_op jit(solution)/shard_map/ppermute | solution.py:68
  65.7 2.0 %collective-permute-start.5 = (bf16[2,256,256]{1,2,0:T(8,128)(2,1)}, bf16[2,256,256]{1,2,0:T(8,128)(2,1)}, u32[]{:S(2)}, u32[]{:S(2)}) collective-permute-start(bf16[2,256,256]{1,2,0:T(8,128)(2,1)} %select_select_fusion.1), channel_id=1, source_target_pairs={{0,384},{16,400},{32,416},{48,432},{64,448},{80,464},{96,480},{112... | collective-permute-start | bytes 786440 | tf_op jit(solution)/shard_map/ppermute | solution.py:68
  71.6 2.5 %fusion.1 = (f32[2,2,256]{2,1,0:T(2,128)}, f32[2,2,256,768]{3,2,1,0:T(8,128)S(1)}) fusion(pred[2,2,768]{2,1,0:T(4,128)(4,1)S(1)} %broadcast_and_fusion, bf16[2,256,2,128]{3,1,0,2:T(8,128)(2,1)} %copy.147, bf16[2,256,2,128]{3,1,0,2:T(8,128)(2,1)} %copy.146, bf16[2,256,2,128]{3,1,0,2:T(8,128)(2,1)} %copy.145, bf16[2,256,2,128]{1,0,3,2:T(2,128)(2,1)} %reshape_reshape.12), kind=kOutput, calls=%fused_computation.5 | convolution fusion | flops 206044160 | bytes 4201472 | tf_op jit(solution)/shard_map/hfqd,hfkd->hfqk/dot_general | solution.py:104
  91.1 7.9 %collective-permute-done.11 = bf16[2,256,256]{1,2,0:T(8,128)(2,1)S(1)} collective-permute-done((bf16[2,256,256]{1,2,0:T(8,128)(2,1)S(1)}, bf16[2,256,256]{1,2,0:T(8,128)(2,1)S(1)}, u32[]{:S(2)}, u32[]{:S(2)}) %collective-permute-start.11) | collective-permute-done | bytes 262176 | tf_op jit(solution)/shard_map/ppermute | solution.py:82
  104.1 2.1 %collective-permute-start.8 = (f32[2,2,256,256]{2,3,1,0:T(8,128)}, f32[2,2,256,256]{2,3,1,0:T(8,128)}, u32[]{:S(2)}, u32[]{:S(2)}) collective-permute-start(f32[2,2,256,256]{2,3,1,0:T(8,128)} %pad_maximum_fusion), channel_id=1, source_target_pairs={{16,0},{32,16},{48,32},{64,48},{80,64},{96,80},{112,96},{128,112},... | collective-permute-start | bytes 3145736 | tf_op jit(solution)/shard_map/ppermute | solution.py:21
  106.6 5.9 %collective-permute-done.14 = bf16[2,256,256]{1,2,0:T(8,128)(2,1)S(1)} collective-permute-done((bf16[2,256,256]{1,2,0:T(8,128)(2,1)S(1)}, bf16[2,256,256]{1,2,0:T(8,128)(2,1)S(1)}, u32[]{:S(2)}, u32[]{:S(2)}) %collective-permute-start.14) | collective-permute-done | bytes 262176 | tf_op jit(solution)/shard_map/ppermute | solution.py:82
  112.4 4.5 %collective-permute-done.13 = bf16[2,256,256]{1,2,0:T(8,128)(2,1)S(1)} collective-permute-done((bf16[2,256,256]{1,2,0:T(8,128)(2,1)S(1)}, bf16[2,256,256]{1,2,0:T(8,128)(2,1)S(1)}, u32[]{:S(2)}, u32[]{:S(2)}) %collective-permute-start.13) | collective-permute-done | bytes 262176 | tf_op jit(solution)/shard_map/ppermute | solution.py:82
  116.9 5.7 %collective-permute-done.12 = bf16[2,256,256]{1,2,0:T(8,128)(2,1)S(1)} collective-permute-done((bf16[2,256,256]{1,2,0:T(8,128)(2,1)S(1)}, bf16[2,256,256]{1,2,0:T(8,128)(2,1)S(1)}, u32[]{:S(2)}, u32[]{:S(2)}) %collective-permute-start.12) | collective-permute-done | bytes 262176 | tf_op jit(solution)/shard_map/ppermute | solution.py:82
  123.4 3.1 %collective-permute-start.15 = (bf16[2,256,256]{1,2,0:T(8,128)(2,1)}, bf16[2,256,256]{1,2,0:T(8,128)(2,1)}, u32[]{:S(2)}, u32[]{:S(2)}) collective-permute-start(bf16[2,256,256]{1,2,0:T(8,128)(2,1)} %fusion.60), channel_id=1, source_target_pairs={{16,0},{17,1},{18,2},{19,3},{20,4},{21,5},{22,6},{23,7},{24,8},{25... | collective-permute-start | bytes 786440 | tf_op jit(solution)/shard_map/ppermute | solution.py:82
  126.6 1.4 fusion.6
  130.8 2.9 %collective-permute-done.8 = f32[2,2,256,256]{2,3,1,0:T(8,128)} collective-permute-done((f32[2,2,256,256]{2,3,1,0:T(8,128)}, f32[2,2,256,256]{2,3,1,0:T(8,128)}, u32[]{:S(2)}, u32[]{:S(2)}) %collective-permute-start.8) | collective-permute-done | bytes 1048608 | tf_op jit(solution)/shard_map/ppermute | solution.py:21
  133.7 1.3 fusion.26
  136.1 5.6 %all-to-all-start.1 = ((f32[16,2,512]{2,1,0:T(2,128)}), f32[16,2,512]{2,1,0:T(2,128)S(1)}, u32[]{:S(2)}, u32[]{:S(2)}) async-start(f32[16,2,512]{2,1,0:T(2,128)} %broadcast_in_dim.103), calls=%async_computation.1 | async-start | bytes 131072 | tf_op jit(solution)/shard_map/all_to_all | solution.py:27
  143.6 9.9 %all-to-all-done.1 = f32[16,2,512]{2,1,0:T(2,128)S(1)} async-done(((f32[16,2,512]{2,1,0:T(2,128)}), f32[16,2,512]{2,1,0:T(2,128)S(1)}, u32[]{:S(2)}, u32[]{:S(2)}) %all-to-all-start.1) | async-done | bytes 65568 | tf_op jit(solution)/shard_map/all_to_all | solution.py:27
  (164 shorter events, 49.7 us)
Async XLA Ops:
  0.6 25.3 %copy-start.25 = (s32[2]{0:T(128)S(1)}, s32[2]{0:T(128)}, u32[]{:S(2)}) copy-start(s32[2]{0:T(128)} %param.19) | copy-start | bytes 28
  0.7 31.2 %copy-start.18 = (f32[256]{0:T(256)S(1)}, f32[256]{0:T(256)}, u32[]{:S(2)}) copy-start(f32[256]{0:T(256)} %param.16) | copy-start | bytes 3076
  3.0 42.7 %copy-start = (bf16[512,256]{0,1:T(8,128)(2,1)}, bf16[512,256]{0,1:T(8,128)(2,1)S(1)}, u32[]{:S(2)}) copy-start(bf16[512,256]{0,1:T(8,128)(2,1)S(1)} %copy.137) | copy-start | bytes 786436
  3.7 28.0 %all-to-all-start = ((f32[16,2,512]{2,1,0:T(2,128)}), f32[16,2,512]{2,1,0:T(2,128)S(1)}, u32[]{:S(2)}, u32[]{:S(2)}) async-start(f32[16,2,512]{2,1,0:T(2,128)} %broadcast_in_dim.58), calls=%async_computation | async-start | bytes 131072 | tf_op jit(solution)/shard_map/all_to_all | solution.py:27
  32.0 5.9 %collective-permute-start.1 = (bf16[2,256,256]{1,2,0:T(8,128)(2,1)S(1)}, bf16[2,256,256]{1,2,0:T(8,128)(2,1)S(1)}, u32[]{:S(2)}, u32[]{:S(2)}) collective-permute-start(bf16[2,256,256]{1,2,0:T(8,128)(2,1)S(1)} %pad_maximum_fusion.5), channel_id=1, source_target_pairs={{0,16},{1,17},{2,18},{3,19},{4,20},{5,21},{6,22},{7,23},{8,24},{9,... | collective-permute-start | bytes 786440 | tf_op jit(solution)/shard_map/ppermute | solution.py:68
  33.5 34.3 %collective-permute-start = (bf16[2,512,256]{1,2,0:T(8,128)(2,1)S(1)}, bf16[2,512,256]{1,2,0:T(8,128)(2,1)S(1)}, u32[]{:S(2)}, u32[]{:S(2)}) collective-permute-start(bf16[2,512,256]{1,2,0:T(8,128)(2,1)S(1)} %pad_maximum_fusion.1), channel_id=1, source_target_pairs={{0,16},{16,32},{32,48},{48,64},{64,80},{80,96},{96,112},{112,128},... | collective-permute-start | bytes 1572872 | tf_op jit(solution)/shard_map/ppermute | solution.py:21
  38.7 13.2 %collective-permute-start.4 = (bf16[2,256,256]{1,2,0:T(8,128)(2,1)}, bf16[2,256,256]{1,2,0:T(8,128)(2,1)S(1)}, u32[]{:S(2)}, u32[]{:S(2)}) collective-permute-start(bf16[2,256,256]{1,2,0:T(8,128)(2,1)} %broadcast_select_fusion.1), channel_id=1, source_target_pairs={{0,32},{16,48},{1,33},{17,49},{2,34},{18,50},{3,35},{19,51},{4,36}... | collective-permute-start | bytes 786440 | tf_op jit(solution)/shard_map/ppermute | solution.py:68
  41.8 15.7 %collective-permute-start.3 = (bf16[2,256,256]{1,2,0:T(8,128)(2,1)}, bf16[2,256,256]{1,2,0:T(8,128)(2,1)S(1)}, u32[]{:S(2)}, u32[]{:S(2)}) collective-permute-start(bf16[2,256,256]{1,2,0:T(8,128)(2,1)} %broadcast_select_fusion.1), channel_id=1, source_target_pairs={{0,64},{16,80},{1,65},{17,81},{2,66},{18,82},{3,67},{19,83},{4,68}... | collective-permute-start | bytes 786440 | tf_op jit(solution)/shard_map/ppermute | solution.py:68
  43.4 17.6 %collective-permute-start.2 = (bf16[2,256,256]{1,2,0:T(8,128)(2,1)}, bf16[2,256,256]{1,2,0:T(8,128)(2,1)}, u32[]{:S(2)}, u32[]{:S(2)}) collective-permute-start(bf16[2,256,256]{1,2,0:T(8,128)(2,1)} %broadcast_select_fusion.1), channel_id=1, source_target_pairs={{0,96},{16,112},{1,97},{17,113},{2,98},{18,114},{3,99},{19,115},{4... | collective-permute-start | bytes 786440 | tf_op jit(solution)/shard_map/ppermute | solution.py:68
  61.7 12.4 %collective-permute-start.7 = (bf16[2,256,256]{1,2,0:T(8,128)(2,1)}, bf16[2,256,256]{1,2,0:T(8,128)(2,1)}, u32[]{:S(2)}, u32[]{:S(2)}) collective-permute-start(bf16[2,256,256]{1,2,0:T(8,128)(2,1)} %select_select_fusion.1), channel_id=1, source_target_pairs={{0,128},{16,144},{32,160},{48,176},{64,192},{80,208},{96,224},{112... | collective-permute-start | bytes 786440 | tf_op jit(solution)/shard_map/ppermute | solution.py:68
  63.7 10.4 %collective-permute-start.6 = (bf16[2,256,256]{1,2,0:T(8,128)(2,1)}, bf16[2,256,256]{1,2,0:T(8,128)(2,1)}, u32[]{:S(2)}, u32[]{:S(2)}) collective-permute-start(bf16[2,256,256]{1,2,0:T(8,128)(2,1)} %select_select_fusion.1), channel_id=1, source_target_pairs={{0,256},{16,272},{32,288},{48,304},{64,320},{80,336},{96,352},{112... | collective-permute-start | bytes 786440 | tf_op jit(solution)/shard_map/ppermute | solution.py:68
  65.7 8.4 %collective-permute-start.5 = (bf16[2,256,256]{1,2,0:T(8,128)(2,1)}, bf16[2,256,256]{1,2,0:T(8,128)(2,1)}, u32[]{:S(2)}, u32[]{:S(2)}) collective-permute-start(bf16[2,256,256]{1,2,0:T(8,128)(2,1)} %select_select_fusion.1), channel_id=1, source_target_pairs={{0,384},{16,400},{32,416},{48,432},{64,448},{80,464},{96,480},{112... | collective-permute-start | bytes 786440 | tf_op jit(solution)/shard_map/ppermute | solution.py:68
  83.5 15.4 %collective-permute-start.11 = (bf16[2,256,256]{1,2,0:T(8,128)(2,1)S(1)}, bf16[2,256,256]{1,2,0:T(8,128)(2,1)S(1)}, u32[]{:S(2)}, u32[]{:S(2)}) collective-permute-start(bf16[2,256,256]{1,2,0:T(8,128)(2,1)S(1)} %fusion.28), channel_id=1, source_target_pairs={{384,0},{400,16},{416,32},{432,48},{448,64},{464,80},{480,96},{496... | collective-permute-start | bytes 786440 | tf_op jit(solution)/shard_map/ppermute | solution.py:82
  84.8 14.1 %collective-permute-start.10 = (bf16[2,256,256]{1,2,0:T(8,128)(2,1)S(1)}, bf16[2,256,256]{1,2,0:T(8,128)(2,1)S(1)}, u32[]{:S(2)}, u32[]{:S(2)}) collective-permute-start(bf16[2,256,256]{1,2,0:T(8,128)(2,1)S(1)} %fusion.28), channel_id=1, source_target_pairs={{256,0},{272,16},{288,32},{304,48},{320,64},{336,80},{352,96},{368... | collective-permute-start | bytes 786440 | tf_op jit(solution)/shard_map/ppermute | solution.py:82
  86.1 12.8 %collective-permute-start.9 = (bf16[2,256,256]{1,2,0:T(8,128)(2,1)S(1)}, bf16[2,256,256]{1,2,0:T(8,128)(2,1)S(1)}, u32[]{:S(2)}, u32[]{:S(2)}) collective-permute-start(bf16[2,256,256]{1,2,0:T(8,128)(2,1)S(1)} %fusion.28), channel_id=1, source_target_pairs={{128,0},{144,16},{160,32},{176,48},{192,64},{208,80},{224,96},{240... | collective-permute-start | bytes 786440 | tf_op jit(solution)/shard_map/ppermute | solution.py:82
  91.0 35.5 %copy-start.12 = (bf16[2,256,2,128]{3,1,0,2:T(8,128)(2,1)S(1)}, bf16[2,256,2,128]{3,1,0,2:T(8,128)(2,1)}, u32[]{:S(2)}) copy-start(bf16[2,256,2,128]{3,1,0,2:T(8,128)(2,1)} %copy.145) | copy-start | bytes 786436
  91.0 35.5 %copy-start.14 = (bf16[2,256,2,128]{3,1,0,2:T(8,128)(2,1)S(1)}, bf16[2,256,2,128]{3,1,0,2:T(8,128)(2,1)}, u32[]{:S(2)}) copy-start(bf16[2,256,2,128]{3,1,0,2:T(8,128)(2,1)} %copy.146) | copy-start | bytes 786436
  91.1 35.5 %copy-start.15 = (bf16[2,256,2,128]{3,1,0,2:T(8,128)(2,1)S(1)}, bf16[2,256,2,128]{3,1,0,2:T(8,128)(2,1)}, u32[]{:S(2)}) copy-start(bf16[2,256,2,128]{3,1,0,2:T(8,128)(2,1)} %copy.147) | copy-start | bytes 786436
  99.1 13.3 %collective-permute-start.14 = (bf16[2,256,256]{1,2,0:T(8,128)(2,1)S(1)}, bf16[2,256,256]{1,2,0:T(8,128)(2,1)S(1)}, u32[]{:S(2)}, u32[]{:S(2)}) collective-permute-start(bf16[2,256,256]{1,2,0:T(8,128)(2,1)S(1)} %get-tuple-element.44), channel_id=1, source_target_pairs={{96,0},{112,16},{97,1},{113,17},{98,2},{114,18},{99,3},{115,19},{1... | collective-permute-start | bytes 786440 | tf_op jit(solution)/shard_map/ppermute | solution.py:82
  100.4 16.5 %collective-permute-start.13 = (bf16[2,256,256]{1,2,0:T(8,128)(2,1)S(1)}, bf16[2,256,256]{1,2,0:T(8,128)(2,1)S(1)}, u32[]{:S(2)}, u32[]{:S(2)}) collective-permute-start(bf16[2,256,256]{1,2,0:T(8,128)(2,1)S(1)} %get-tuple-element.44), channel_id=1, source_target_pairs={{64,0},{80,16},{65,1},{81,17},{66,2},{82,18},{67,3},{83,19},{68,4}... | collective-permute-start | bytes 786440 | tf_op jit(solution)/shard_map/ppermute | solution.py:82
  101.7 20.9 %collective-permute-start.12 = (bf16[2,256,256]{1,2,0:T(8,128)(2,1)S(1)}, bf16[2,256,256]{1,2,0:T(8,128)(2,1)S(1)}, u32[]{:S(2)}, u32[]{:S(2)}) collective-permute-start(bf16[2,256,256]{1,2,0:T(8,128)(2,1)S(1)} %get-tuple-element.44), channel_id=1, source_target_pairs={{32,0},{48,16},{33,1},{49,17},{34,2},{50,18},{35,3},{51,19},{36,4}... | collective-permute-start | bytes 786440 | tf_op jit(solution)/shard_map/ppermute | solution.py:82
  104.1 29.6 %collective-permute-start.8 = (f32[2,2,256,256]{2,3,1,0:T(8,128)}, f32[2,2,256,256]{2,3,1,0:T(8,128)}, u32[]{:S(2)}, u32[]{:S(2)}) collective-permute-start(f32[2,2,256,256]{2,3,1,0:T(8,128)} %pad_maximum_fusion), channel_id=1, source_target_pairs={{16,0},{32,16},{48,32},{64,48},{80,64},{96,80},{112,96},{128,112},... | collective-permute-start | bytes 3145736 | tf_op jit(solution)/shard_map/ppermute | solution.py:21
  123.4 6.0 %collective-permute-start.15 = (bf16[2,256,256]{1,2,0:T(8,128)(2,1)}, bf16[2,256,256]{1,2,0:T(8,128)(2,1)}, u32[]{:S(2)}, u32[]{:S(2)}) collective-permute-start(bf16[2,256,256]{1,2,0:T(8,128)(2,1)} %fusion.60), channel_id=1, source_target_pairs={{16,0},{17,1},{18,2},{19,3},{20,4},{21,5},{22,6},{23,7},{24,8},{25... | collective-permute-start | bytes 786440 | tf_op jit(solution)/shard_map/ppermute | solution.py:82
  136.1 17.4 %all-to-all-start.1 = ((f32[16,2,512]{2,1,0:T(2,128)}), f32[16,2,512]{2,1,0:T(2,128)S(1)}, u32[]{:S(2)}, u32[]{:S(2)}) async-start(f32[16,2,512]{2,1,0:T(2,128)} %broadcast_in_dim.103), calls=%async_computation.1 | async-start | bytes 131072 | tf_op jit(solution)/shard_map/all_to_all | solution.py:27
  (20 other events, 138.7 us)

commit v6 on v4

--- a/solution.py
+++ b/solution.py
@@ -56,9 +56,9 @@
     return values
 
 
-def tree_reduce(values, axis, wire):
+def tree_reduce(values, axis, wire, first=0, last=None):
     n = lax.axis_size(axis)
-    for step, fan in tree_plan(n):
+    for step, fan in tree_plan(n)[first:last]:
         span = step * fan
         total = values
         for j in range(1, fan):
@@ -186,15 +186,39 @@
     back_k, back_v = shifted(jnp.stack([grad_k_near[:F_DEV], grad_v_near[:F_DEV]]), "seq", -1)
     grad_k_own = grad_k_near[F_DEV:] + back_k
     grad_v_own = grad_v_near[F_DEV:] + back_v
-    anchor_gk, anchor_gv = tree_reduce(jnp.stack([grad_k_anchor, grad_v_anchor]), "seq", jnp.bfloat16)
+    anchor_grads = tree_reduce(
+        jnp.stack([grad_k_anchor, grad_v_anchor]), "seq", jnp.bfloat16, last=2
+    )
+    q_scaled = grad_qn * q_gain
+    local_scaled = grad_k_near[F_DEV:].reshape(row_count, local_width) * k_gain
+    back_part = jnp.sum(
+        halo_k.astype(jnp.float32) * grad_k_near[:F_DEV].reshape(row_count, local_width), axis=1
+    )
+    anchor_part = jnp.sum(anchor_k.astype(jnp.float32) * grad_k_anchor, axis=1)
+    q_dot, local_dot, back_part, anchor_part = gather_sum(
+        jnp.stack(
+            [
+                jnp.sum(q_float * q_scaled, axis=1),
+                jnp.sum(k_float * local_scaled, axis=1),
+                back_part,
+                jnp.pad(anchor_part, (0, row_count - CAP)),
+            ]
+        ),
+        "tp",
+    )
+    anchor_grads, q_dot, local_dot, back_part, anchor_part = lax.optimization_barrier(
+        (anchor_grads, q_dot, local_dot, back_part, anchor_part)
+    )
+    anchor_gk, anchor_gv = tree_reduce(anchor_grads, "seq", jnp.bfloat16, first=2)
+    anchor_part = tree_reduce(anchor_part[:CAP], "seq", jnp.float32)
+    back_part = shifted(back_part, "seq", -1)
     first_device = device == 0
     grad_k_own = grad_k_own.at[0].add(jnp.where(first_device, anchor_gk, 0.0))
     grad_v_own = grad_v_own.at[0].add(jnp.where(first_device, anchor_gv, 0.0))
-    q_scaled = grad_qn * q_gain
     k_scaled = grad_k_own.reshape(row_count, local_width) * k_gain
-    q_dot, k_dot = gather_sum(
-        jnp.stack([jnp.sum(q_float * q_scaled, axis=1), jnp.sum(k_float * k_scaled, axis=1)]), "tp"
-    )
+    anchor_rows = first_device & (jnp.arange(row_count) < CAP)
+    far_part = back_part + jnp.where(anchor_rows, jnp.pad(anchor_part, (0, row_count - CAP)), 0.0)
+    k_dot = local_dot + far_part / k_rinv[:, 0]
     grad_q = (q_rinv * q_scaled - q_float * q_rinv**3 * q_dot[:, None] / WIDTH).astype(jnp.bfloat16)
     grad_k = (k_rinv * k_scaled - k_float * k_rinv**3 * k_dot[:, None] / WIDTH).astype(jnp.bfloat16)
     grad_v = grad_v_own.reshape(row_count, local_width).astype(jnp.bfloat16)

time: 139 us -> 153 us (1.10)
  starting transfers between devices: 48.5 us -> 58.7 us
  other arithmetic: 13.7 us -> 19.4 us
  waiting for transfers between devices: 41.4 us -> 38.5 us
    ppermute x7 -> x14, starting transfers between devices: 9.36 us -> 18.4 us  [tree_reduce(): arrived = lax.ppermute(sent, axis, route)]
    ppermute x7, waiting for transfers between devices: 11.7 us -> 8.62 us  [tree_bcast(): arrived = lax.ppermute(values, axis, route)]
    ppermute x7 -> x14, waiting for transfers between devices: 15.7 us -> 13.8 us  [tree_reduce(): arrived = lax.ppermute(sent, axis, route)]
    ppermute x2 -> x3, waiting for transfers between devices: 0.01 us -> 1.74 us  [shifted(): return lax.ppermute(block, axis, route)]
    convert_element_type x3, other arithmetic: 0.98 us -> 2.59 us  [tree_reduce(): sent = jax.tree.map(lambda a: a.astype(wire), values)]
    unnamed x63 -> x62, local copies, waits for them, and re-layouts: 6.33 us -> 7.88 us
    ppermute x2 -> x3, starting transfers between devices: 2.6 us -> 3.89 us  [shifted(): return lax.ppermute(block, axis, route)]
  transfers between devices with their start and end apart: 18 -> 26, of which waited for: 10 -> 11; matrix products, arithmetic and copies ran while one was open for 19% -> 20% of each run, Pallas kernels for 0% -> 0%
where the time goes in v6:
time: 153 us; the launch traced here: 152 us
  starting transfers between devices  58.7 us (38%)
  waiting for transfers between devices  38.5 us (25%)
  local copies, waits for them, and re-layouts  23.4 us (15%)
  other arithmetic  19.4 us (13%)
  matrix products  9.89 us (6%)
  between operations  1.68 us (1%)
    all_to_all x2, starting transfers between devices, gather_sum(): return jnp.sum(lax.all_to_all(copies, axis, 0, 0, tiled=False), axis=0)  22.2 us
    ppermute x14, starting transfers between devices, tree_reduce(): arrived = lax.ppermute(sent, axis, route)  18.4 us
    all_to_all x2, waiting for transfers between devices, gather_sum(): return jnp.sum(lax.all_to_all(copies, axis, 0, 0, tiled=False), axis=0)  14.3 us
    ppermute x7, starting transfers between devices, tree_bcast(): arrived = lax.ppermute(values, axis, route)  14.2 us
    ppermute x14, waiting for transfers between devices, tree_reduce(): arrived = lax.ppermute(sent, axis, route)  13.8 us
    ppermute x7, waiting for transfers between devices, tree_bcast(): arrived = lax.ppermute(values, axis, route)  8.62 us
    unnamed x62, local copies, waits for them, and re-layouts  7.88 us
    concatenate x12, local copies, waits for them, and re-layouts, stack_offsets(): return jnp.concatenate(blocks, axis=1)  5.48 us
  transfers between devices with their start and end apart: 26, of which 11 were waited for; matrix products, arithmetic and copies ran while one was open for 20% of the time, Pallas kernels for 0%

profile of v6, /device:TPU:8, one launch (start us, length us, event | category | flops | bytes accessed | tf_op | source)
XLA Modules:
  0.0 151.6 jit_solution(17920095250518354393)
XLA Ops:
  3.7 16.0 %all-to-all-start = ((f32[16,2,512]{2,1,0:T(2,128)}), f32[16,2,512]{2,1,0:T(2,128)S(1)}, u32[]{:S(2)}, u32[]{:S(2)}) async-start(f32[16,2,512]{2,1,0:T(2,128)} %broadcast_in_dim.61), calls=%async_computation | async-start | bytes 131072 | tf_op jit(solution)/shard_map/all_to_all | solution.py:25
  25.4 5.8 %all-to-all-done = f32[16,2,512]{2,1,0:T(2,128)S(1)} async-done(((f32[16,2,512]{2,1,0:T(2,128)}), f32[16,2,512]{2,1,0:T(2,128)S(1)}, u32[]{:S(2)}, u32[]{:S(2)}) %all-to-all-start) | async-done | bytes 65568 | tf_op jit(solution)/shard_map/all_to_all | solution.py:25
  32.8 3.4 %collective-permute-start.3 = (bf16[2,256,256]{1,2,0:T(8,128)(2,1)S(1)}, bf16[2,256,256]{1,2,0:T(8,128)(2,1)S(1)}, u32[]{:S(2)}, u32[]{:S(2)}) collective-permute-start(bf16[2,256,256]{1,2,0:T(8,128)(2,1)S(1)} %pad_maximum_fusion.5), channel_id=1, source_target_pairs={{0,128},{1,129},{2,130},{3,131},{4,132},{5,133},{6,134},{7,135},{8... | collective-permute-start | bytes 786440 | tf_op jit(solution)/shard_map/ppermute | solution.py:52
  36.2 2.2 %collective-permute-start.2 = (bf16[2,256,256]{1,2,0:T(8,128)(2,1)S(1)}, bf16[2,256,256]{1,2,0:T(8,128)(2,1)S(1)}, u32[]{:S(2)}, u32[]{:S(2)}) collective-permute-start(bf16[2,256,256]{1,2,0:T(8,128)(2,1)S(1)} %pad_maximum_fusion.5), channel_id=1, source_target_pairs={{0,256},{1,257},{2,258},{3,259},{4,260},{5,261},{6,262},{7,263},{8... | collective-permute-start | bytes 786440 | tf_op jit(solution)/shard_map/ppermute | solution.py:52
  39.9 1.3 collective-permute-start
  41.2 7.3 %collective-permute-done.2 = bf16[2,256,256]{1,2,0:T(8,128)(2,1)S(1)} collective-permute-done((bf16[2,256,256]{1,2,0:T(8,128)(2,1)S(1)}, bf16[2,256,256]{1,2,0:T(8,128)(2,1)S(1)}, u32[]{:S(2)}, u32[]{:S(2)}) %collective-permute-start.2) | collective-permute-done | bytes 262176 | tf_op jit(solution)/shard_map/ppermute | solution.py:52
  49.9 2.0 %collective-permute-start.5 = (bf16[2,256,256]{1,2,0:T(8,128)(2,1)S(1)}, bf16[2,256,256]{1,2,0:T(8,128)(2,1)}, u32[]{:S(2)}, u32[]{:S(2)}) collective-permute-start(bf16[2,256,256]{1,2,0:T(8,128)(2,1)S(1)} %select_select_fusion.1), channel_id=1, source_target_pairs={{0,64},{128,192},{256,320},{384,448},{1,65},{129,193},{257,321},{3... | collective-permute-start | bytes 786440 | tf_op jit(solution)/shard_map/ppermute | solution.py:52
  51.9 2.0 %collective-permute-start.4 = (bf16[2,256,256]{1,2,0:T(8,128)(2,1)S(1)}, bf16[2,256,256]{1,2,0:T(8,128)(2,1)}, u32[]{:S(2)}, u32[]{:S(2)}) collective-permute-start(bf16[2,256,256]{1,2,0:T(8,128)(2,1)S(1)} %select_select_fusion.1), channel_id=1, source_target_pairs={{0,96},{128,224},{256,352},{384,480},{1,97},{129,225},{257,353},{3... | collective-permute-start | bytes 786440 | tf_op jit(solution)/shard_map/ppermute | solution.py:52
  58.0 1.3 collective-permute-done.4
  60.1 2.0 %collective-permute-start.7 = (bf16[2,256,256]{1,2,0:T(8,128)(2,1)}, bf16[2,256,256]{1,2,0:T(8,128)(2,1)}, u32[]{:S(2)}, u32[]{:S(2)}) collective-permute-start(bf16[2,256,256]{1,2,0:T(8,128)(2,1)} %select_select_fusion), channel_id=1, source_target_pairs={{0,16},{32,48},{64,80},{96,112},{128,144},{160,176},{192,208},{224... | collective-permute-start | bytes 786440 | tf_op jit(solution)/shard_map/ppermute | solution.py:52
  67.2 2.5 %fusion.1 = (f32[2,2,256]{2,1,0:T(2,128)}, f32[2,2,256,768]{3,2,1,0:T(8,128)S(1)}) fusion(pred[2,2,768]{2,1,0:T(4,128)(4,1)S(1)} %broadcast_and_fusion, bf16[2,256,2,128]{3,1,0,2:T(8,128)(2,1)} %copy.156, bf16[2,256,2,128]{3,1,0,2:T(8,128)(2,1)} %copy.155, bf16[2,256,2,128]{3,1,0,2:T(8,128)(2,1)} %copy.154, bf16[2,256,2,128]{1,0,3,2:T(2,128)(2,1)} %reshape_reshape.12), kind=kOutput, calls=%fused_computation.5 | convolution fusion | flops 206044160 | bytes 4201472 | tf_op jit(solution)/shard_map/hfqd,hfkd->hfqk/dot_general | solution.py:89
  86.3 1.5 collective-permute-start.8
  91.0 1.8 %fusion.31 = bf16[2,256,256]{1,2,0:T(8,128)(2,1)} fusion(bf16[2,256,256]{1,2,0:T(8,128)(2,1)} %collective-permute-done.8, f32[1,256,256]{1,2,0:T(8,128)S(1)} %bitcast.178, f32[1,256,256]{1,2,0:T(8,128)} %bitcast.181), kind=kLoop, calls=%fused_computation.68 | loop fusion | flops 524288 | bytes 1048576 | tf_op jit(solution)/shard_map/convert_element_type | solution.py:66
  92.8 1.4 collective-permute-start.11
  96.8 2.5 %fusion.26 = (f32[2,256,256]{1,2,0:T(8,128)}, f32[2,256,256]{1,2,0:T(8,128)}, f32[2,256]{1,0:T(2,128)S(1)}, f32[2,32,8,256]{3,2,1,0:T(8,128)S(1)}) fusion(f32[2,2,256,256]{2,3,1,0:T(8,128)} %collective-permute-done.12, f32[4,256,256]{1,2,0:T(8,128)S(1)} %pad_add_fusion, f32[4,256,256]{1,2,0:T(8,128)S(1)} %pad_add_fusion.1, f32[2,256,256]{1,0,2:T(2,128)} %reshape.321), kind=kLoop, calls=%fused_computation.52 | loop fusion | flops 523776 | bytes 4720640 | tf_op jit(solution)/shard_map/add | solution.py:188
  100.3 6.2 %all-to-all-start.1 = ((f32[16,4,512]{2,1,0:T(4,128)}), f32[16,4,512]{2,1,0:T(4,128)S(1)}, u32[]{:S(2)}, u32[]{:S(2)}) async-start(f32[16,4,512]{2,1,0:T(4,128)} %broadcast_in_dim.71), calls=%async_computation.1 | async-start | bytes 262144 | tf_op jit(solution)/shard_map/all_to_all | solution.py:25
  106.9 2.4 %collective-permute-done.9 = bf16[2,256,256]{1,2,0:T(8,128)(2,1)} collective-permute-done((bf16[2,256,256]{1,2,0:T(8,128)(2,1)}, bf16[2,256,256]{1,2,0:T(8,128)(2,1)}, u32[]{:S(2)}, u32[]{:S(2)}) %collective-permute-start.9) | collective-permute-done | bytes 262176 | tf_op jit(solution)/shard_map/ppermute | solution.py:67
  109.3 1.4 convert_add_fusion.1
  110.7 8.5 %all-to-all-done.1 = f32[16,4,512]{2,1,0:T(4,128)S(1)} async-done(((f32[16,4,512]{2,1,0:T(4,128)}), f32[16,4,512]{2,1,0:T(4,128)S(1)}, u32[]{:S(2)}, u32[]{:S(2)}) %all-to-all-start.1) | async-done | bytes 131104 | tf_op jit(solution)/shard_map/all_to_all | solution.py:25
  120.6 1.7 %collective-permute-done.17 = f32[256]{0:T(256)S(1)} collective-permute-done((f32[256]{0:T(256)S(1)}, f32[256]{0:T(256)S(1)}, u32[]{:S(2)}, u32[]{:S(2)}) %collective-permute-start.17) | collective-permute-done | bytes 1056 | tf_op jit(solution)/shard_map/ppermute | solution.py:67
  129.9 2.5 %collective-permute-done.20 = f32[256]{0:T(256)S(1)} collective-permute-done((f32[256]{0:T(256)S(1)}, f32[256]{0:T(256)S(1)}, u32[]{:S(2)}, u32[]{:S(2)}) %collective-permute-start.20) | collective-permute-done | bytes 1056 | tf_op jit(solution)/shard_map/ppermute | solution.py:67
  137.3 2.9 %collective-permute-done.23 = f32[256]{0:T(256)S(1)} collective-permute-done((f32[256]{0:T(256)S(1)}, f32[256]{0:T(256)S(1)}, u32[]{:S(2)}, u32[]{:S(2)}) %collective-permute-start.23) | collective-permute-done | bytes 1056 | tf_op jit(solution)/shard_map/ppermute | solution.py:67
  142.8 1.7 %collective-permute-done.16 = f32[512]{0:T(512)S(1)} collective-permute-done((f32[512]{0:T(512)S(1)}, f32[512]{0:T(512)S(1)}, u32[]{:S(2)}, u32[]{:S(2)}) %collective-permute-start.16) | collective-permute-done | bytes 2080 | tf_op jit(solution)/shard_map/ppermute | solution.py:19
  144.5 3.9 %collective-permute-done.13 = bf16[2,256,256]{1,2,0:T(8,128)(2,1)S(1)} collective-permute-done((bf16[2,256,256]{1,2,0:T(8,128)(2,1)S(1)}, bf16[2,256,256]{1,2,0:T(8,128)(2,1)S(1)}, u32[]{:S(2)}, u32[]{:S(2)}) %collective-permute-start.13) | collective-permute-done | bytes 262176 | tf_op jit(solution)/shard_map/ppermute | solution.py:67
  (192 shorter events, 65.6 us)
Async XLA Ops:
  3.7 27.6 %all-to-all-start = ((f32[16,2,512]{2,1,0:T(2,128)}), f32[16,2,512]{2,1,0:T(2,128)S(1)}, u32[]{:S(2)}, u32[]{:S(2)}) async-start(f32[16,2,512]{2,1,0:T(2,128)} %broadcast_in_dim.61), calls=%async_computation | async-start | bytes 131072 | tf_op jit(solution)/shard_map/all_to_all | solution.py:25
  32.8 8.5 %collective-permute-start.3 = (bf16[2,256,256]{1,2,0:T(8,128)(2,1)S(1)}, bf16[2,256,256]{1,2,0:T(8,128)(2,1)S(1)}, u32[]{:S(2)}, u32[]{:S(2)}) collective-permute-start(bf16[2,256,256]{1,2,0:T(8,128)(2,1)S(1)} %pad_maximum_fusion.5), channel_id=1, source_target_pairs={{0,128},{1,129},{2,130},{3,131},{4,132},{5,133},{6,134},{7,135},{8... | collective-permute-start | bytes 786440 | tf_op jit(solution)/shard_map/ppermute | solution.py:52
  36.2 12.3 %collective-permute-start.2 = (bf16[2,256,256]{1,2,0:T(8,128)(2,1)S(1)}, bf16[2,256,256]{1,2,0:T(8,128)(2,1)S(1)}, u32[]{:S(2)}, u32[]{:S(2)}) collective-permute-start(bf16[2,256,256]{1,2,0:T(8,128)(2,1)S(1)} %pad_maximum_fusion.5), channel_id=1, source_target_pairs={{0,256},{1,257},{2,258},{3,259},{4,260},{5,261},{6,262},{7,263},{8... | collective-permute-start | bytes 786440 | tf_op jit(solution)/shard_map/ppermute | solution.py:52
  38.4 10.1 %collective-permute-start.1 = (bf16[2,256,256]{1,2,0:T(8,128)(2,1)S(1)}, bf16[2,256,256]{1,2,0:T(8,128)(2,1)S(1)}, u32[]{:S(2)}, u32[]{:S(2)}) collective-permute-start(bf16[2,256,256]{1,2,0:T(8,128)(2,1)S(1)} %pad_maximum_fusion.5), channel_id=1, source_target_pairs={{0,384},{1,385},{2,386},{3,387},{4,388},{5,389},{6,390},{7,391},{8... | collective-permute-start | bytes 786440 | tf_op jit(solution)/shard_map/ppermute | solution.py:52
  39.9 22.2 %collective-permute-start = (bf16[2,512,256]{1,2,0:T(8,128)(2,1)S(1)}, bf16[2,512,256]{1,2,0:T(8,128)(2,1)S(1)}, u32[]{:S(2)}, u32[]{:S(2)}) collective-permute-start(bf16[2,512,256]{1,2,0:T(8,128)(2,1)S(1)} %pad_maximum_fusion.1), channel_id=1, source_target_pairs={{0,16},{16,32},{32,48},{48,64},{64,80},{80,96},{96,112},{112,128},... | collective-permute-start | bytes 1572872 | tf_op jit(solution)/shard_map/ppermute | solution.py:19
  48.6 9.4 %collective-permute-start.6 = (bf16[2,256,256]{1,2,0:T(8,128)(2,1)S(1)}, bf16[2,256,256]{1,2,0:T(8,128)(2,1)S(1)}, u32[]{:S(2)}, u32[]{:S(2)}) collective-permute-start(bf16[2,256,256]{1,2,0:T(8,128)(2,1)S(1)} %select_select_fusion.1), channel_id=1, source_target_pairs={{0,32},{128,160},{256,288},{384,416},{1,33},{129,161},{257,289},{3... | collective-permute-start | bytes 786440 | tf_op jit(solution)/shard_map/ppermute | solution.py:52
  49.9 8.1 %collective-permute-start.5 = (bf16[2,256,256]{1,2,0:T(8,128)(2,1)S(1)}, bf16[2,256,256]{1,2,0:T(8,128)(2,1)}, u32[]{:S(2)}, u32[]{:S(2)}) collective-permute-start(bf16[2,256,256]{1,2,0:T(8,128)(2,1)S(1)} %select_select_fusion.1), channel_id=1, source_target_pairs={{0,64},{128,192},{256,320},{384,448},{1,65},{129,193},{257,321},{3... | collective-permute-start | bytes 786440 | tf_op jit(solution)/shard_map/ppermute | solution.py:52
  51.9 7.5 %collective-permute-start.4 = (bf16[2,256,256]{1,2,0:T(8,128)(2,1)S(1)}, bf16[2,256,256]{1,2,0:T(8,128)(2,1)}, u32[]{:S(2)}, u32[]{:S(2)}) collective-permute-start(bf16[2,256,256]{1,2,0:T(8,128)(2,1)S(1)} %select_select_fusion.1), channel_id=1, source_target_pairs={{0,96},{128,224},{256,352},{384,480},{1,97},{129,225},{257,353},{3... | collective-permute-start | bytes 786440 | tf_op jit(solution)/shard_map/ppermute | solution.py:52
  60.1 9.6 %collective-permute-start.7 = (bf16[2,256,256]{1,2,0:T(8,128)(2,1)}, bf16[2,256,256]{1,2,0:T(8,128)(2,1)}, u32[]{:S(2)}, u32[]{:S(2)}) collective-permute-start(bf16[2,256,256]{1,2,0:T(8,128)(2,1)} %select_select_fusion), channel_id=1, source_target_pairs={{0,16},{32,48},{64,80},{96,112},{128,144},{160,176},{192,208},{224... | collective-permute-start | bytes 786440 | tf_op jit(solution)/shard_map/ppermute | solution.py:52
  83.8 13.0 %collective-permute-start.12 = (f32[2,2,256,256]{2,3,1,0:T(8,128)}, f32[2,2,256,256]{2,3,1,0:T(8,128)}, u32[]{:S(2)}, u32[]{:S(2)}) collective-permute-start(f32[2,2,256,256]{2,3,1,0:T(8,128)} %pad_maximum_fusion), channel_id=1, source_target_pairs={{16,0},{32,16},{48,32},{64,48},{80,64},{96,80},{112,96},{128,112},... | collective-permute-start | bytes 3145736 | tf_op jit(solution)/shard_map/ppermute | solution.py:19
  86.3 4.7 %collective-permute-start.8 = (bf16[2,256,256]{1,2,0:T(8,128)(2,1)}, bf16[2,256,256]{1,2,0:T(8,128)(2,1)}, u32[]{:S(2)}, u32[]{:S(2)}) collective-permute-start(bf16[2,256,256]{1,2,0:T(8,128)(2,1)} %fusion.29), channel_id=1, source_target_pairs={{16,0},{48,32},{80,64},{112,96},{144,128},{176,160},{208,192},{240... | collective-permute-start | bytes 786440 | tf_op jit(solution)/shard_map/ppermute | solution.py:67
  92.8 14.1 %collective-permute-start.11 = (bf16[2,256,256]{1,2,0:T(8,128)(2,1)}, bf16[2,256,256]{1,2,0:T(8,128)(2,1)}, u32[]{:S(2)}, u32[]{:S(2)}) collective-permute-start(bf16[2,256,256]{1,2,0:T(8,128)(2,1)} %fusion.31), channel_id=1, source_target_pairs={{96,0},{224,128},{352,256},{480,384},{97,1},{225,129},{353,257},{4... | collective-permute-start | bytes 786440 | tf_op jit(solution)/shard_map/ppermute | solution.py:67
  94.2 12.7 %collective-permute-start.10 = (bf16[2,256,256]{1,2,0:T(8,128)(2,1)}, bf16[2,256,256]{1,2,0:T(8,128)(2,1)}, u32[]{:S(2)}, u32[]{:S(2)}) collective-permute-start(bf16[2,256,256]{1,2,0:T(8,128)(2,1)} %fusion.31), channel_id=1, source_target_pairs={{64,0},{192,128},{320,256},{448,384},{65,1},{193,129},{321,257},{4... | collective-permute-start | bytes 786440 | tf_op jit(solution)/shard_map/ppermute | solution.py:67
  95.5 13.8 %collective-permute-start.9 = (bf16[2,256,256]{1,2,0:T(8,128)(2,1)}, bf16[2,256,256]{1,2,0:T(8,128)(2,1)}, u32[]{:S(2)}, u32[]{:S(2)}) collective-permute-start(bf16[2,256,256]{1,2,0:T(8,128)(2,1)} %fusion.31), channel_id=1, source_target_pairs={{32,0},{160,128},{288,256},{416,384},{33,1},{161,129},{289,257},{4... | collective-permute-start | bytes 786440 | tf_op jit(solution)/shard_map/ppermute | solution.py:67
  100.3 19.0 %all-to-all-start.1 = ((f32[16,4,512]{2,1,0:T(4,128)}), f32[16,4,512]{2,1,0:T(4,128)S(1)}, u32[]{:S(2)}, u32[]{:S(2)}) async-start(f32[16,4,512]{2,1,0:T(4,128)} %broadcast_in_dim.71), calls=%async_computation.1 | async-start | bytes 262144 | tf_op jit(solution)/shard_map/all_to_all | solution.py:25
  122.4 10.0 %collective-permute-start.20 = (f32[256]{0:T(256)S(1)}, f32[256]{0:T(256)S(1)}, u32[]{:S(2)}, u32[]{:S(2)}) collective-permute-start(f32[256]{0:T(256)S(1)} %slice_add_fusion), channel_id=1, source_target_pairs={{96,0},{224,128},{352,256},{480,384},{97,1},{225,129},{353,257},{4... | collective-permute-start | bytes 3080 | tf_op jit(solution)/shard_map/ppermute | solution.py:67
  123.6 8.8 %collective-permute-start.19 = (f32[256]{0:T(256)S(1)}, f32[256]{0:T(256)S(1)}, u32[]{:S(2)}, u32[]{:S(2)}) collective-permute-start(f32[256]{0:T(256)S(1)} %slice_add_fusion), channel_id=1, source_target_pairs={{64,0},{192,128},{320,256},{448,384},{65,1},{193,129},{321,257},{4... | collective-permute-start | bytes 3080 | tf_op jit(solution)/shard_map/ppermute | solution.py:67
  124.9 7.5 %collective-permute-start.18 = (f32[256]{0:T(256)S(1)}, f32[256]{0:T(256)S(1)}, u32[]{:S(2)}, u32[]{:S(2)}) collective-permute-start(f32[256]{0:T(256)S(1)} %slice_add_fusion), channel_id=1, source_target_pairs={{32,0},{160,128},{288,256},{416,384},{33,1},{161,129},{289,257},{4... | collective-permute-start | bytes 3080 | tf_op jit(solution)/shard_map/ppermute | solution.py:67
  127.3 17.2 %collective-permute-start.15 = (bf16[2,256,256]{1,2,0:T(8,128)(2,1)S(1)}, bf16[2,256,256]{1,2,0:T(8,128)(2,1)S(1)}, u32[]{:S(2)}, u32[]{:S(2)}) collective-permute-start(bf16[2,256,256]{1,2,0:T(8,128)(2,1)S(1)} %convert_element_type.123), channel_id=1, source_target_pairs={{384,0},{385,1},{386,2},{387,3},{388,4},{389,5},{390,6},{391,7},{3... | collective-permute-start | bytes 786440 | tf_op jit(solution)/shard_map/ppermute | solution.py:67
  128.6 15.9 %collective-permute-start.14 = (bf16[2,256,256]{1,2,0:T(8,128)(2,1)S(1)}, bf16[2,256,256]{1,2,0:T(8,128)(2,1)}, u32[]{:S(2)}, u32[]{:S(2)}) collective-permute-start(bf16[2,256,256]{1,2,0:T(8,128)(2,1)S(1)} %convert_element_type.123), channel_id=1, source_target_pairs={{256,0},{257,1},{258,2},{259,3},{260,4},{261,5},{262,6},{263,7},{2... | collective-permute-start | bytes 786440 | tf_op jit(solution)/shard_map/ppermute | solution.py:67
  132.4 7.7 %collective-permute-start.23 = (f32[256]{0:T(256)S(1)}, f32[256]{0:T(256)S(1)}, u32[]{:S(2)}, u32[]{:S(2)}) collective-permute-start(f32[256]{0:T(256)S(1)} %add_add_fusion.1), channel_id=1, source_target_pairs={{384,0},{385,1},{386,2},{387,3},{388,4},{389,5},{390,6},{391,7},{3... | collective-permute-start | bytes 3080 | tf_op jit(solution)/shard_map/ppermute | solution.py:67
  133.7 7.7 %collective-permute-start.22 = (f32[256]{0:T(256)S(1)}, f32[256]{0:T(256)S(1)}, u32[]{:S(2)}, u32[]{:S(2)}) collective-permute-start(f32[256]{0:T(256)S(1)} %add_add_fusion.1), channel_id=1, source_target_pairs={{256,0},{257,1},{258,2},{259,3},{260,4},{261,5},{262,6},{263,7},{2... | collective-permute-start | bytes 3080 | tf_op jit(solution)/shard_map/ppermute | solution.py:67
  135.0 7.7 %collective-permute-start.21 = (f32[256]{0:T(256)S(1)}, f32[256]{0:T(256)S(1)}, u32[]{:S(2)}, u32[]{:S(2)}) collective-permute-start(f32[256]{0:T(256)S(1)} %add_add_fusion.1), channel_id=1, source_target_pairs={{128,0},{129,1},{130,2},{131,3},{132,4},{133,5},{134,6},{135,7},{1... | collective-permute-start | bytes 3080 | tf_op jit(solution)/shard_map/ppermute | solution.py:67
  140.2 8.3 %collective-permute-start.13 = (bf16[2,256,256]{1,2,0:T(8,128)(2,1)S(1)}, bf16[2,256,256]{1,2,0:T(8,128)(2,1)S(1)}, u32[]{:S(2)}, u32[]{:S(2)}) collective-permute-start(bf16[2,256,256]{1,2,0:T(8,128)(2,1)S(1)} %convert_element_type.123), channel_id=1, source_target_pairs={{128,0},{129,1},{130,2},{131,3},{132,4},{133,5},{134,6},{135,7},{1... | collective-permute-start | bytes 786440 | tf_op jit(solution)/shard_map/ppermute | solution.py:67
  (29 other events, 383.7 us)

commit v7 on v4

--- a/solution.py
+++ b/solution.py
@@ -41,10 +41,10 @@
     return plan
 
 
-def tree_bcast(values, axis):
+def tree_bcast(values, axis, first=0):
     n = lax.axis_size(axis)
     me = lax.axis_index(axis)
-    for step, fan in reversed(tree_plan(n)):
+    for step, fan in reversed(tree_plan(n)[first:]):
         span = step * fan
         got = values
         for j in range(1, fan):
@@ -56,9 +56,9 @@
     return values
 
 
-def tree_reduce(values, axis, wire):
+def tree_reduce(values, axis, wire, first=0):
     n = lax.axis_size(axis)
-    for step, fan in tree_plan(n):
+    for step, fan in tree_plan(n)[first:]:
         span = step * fan
         total = values
         for j in range(1, fan):
@@ -141,8 +141,17 @@
     near_live = slot_index[None, :] < near_counts[:, None]
     row_live = near_live[F_DEV:]
     grad_mask = jnp.where(row_live.reshape(row_count)[:, None], d_out, jnp.zeros_like(d_out))
-    halo_k, halo_v = shifted(jnp.stack([k_norm, v_in]), "seq", 1)
-    anchor_k, anchor_v = tree_bcast(jnp.stack([k_norm[:CAP], v_in[:CAP]]), "seq")
+    odd = device % 2 == 1
+    pair_first = tree_plan(lax.axis_size("seq"))[0] == (1, 2)
+    anchor = jnp.stack([k_norm[:CAP], v_in[:CAP]])
+    if pair_first:
+        anchor = tree_bcast(anchor, "seq", first=1)
+        both = shifted(jnp.concatenate([jnp.stack([k_norm, v_in]), anchor], axis=1), "seq", 1)
+        halo_k, halo_v = both[:, :row_count]
+        anchor_k, anchor_v = jnp.where(odd, both[:, row_count:], anchor)
+    else:
+        halo_k, halo_v = shifted(jnp.stack([k_norm, v_in]), "seq", 1)
+        anchor_k, anchor_v = tree_bcast(anchor, "seq")
     k_near = jnp.concatenate([halo_k, k_norm], axis=0).reshape(2 * F_DEV, CAP, local_width)
     v_near = jnp.concatenate([halo_v, v_in], axis=0).reshape(2 * F_DEV, CAP, local_width)
     def to_heads(value):
@@ -183,10 +192,18 @@
     grad_v_near = fold_offsets(from_heads(grad_vh), F_DEV, F_DEV, CAP)
     grad_k_anchor = grad_ka.transpose(1, 0, 2).reshape(CAP, local_width)
     grad_v_anchor = grad_va.transpose(1, 0, 2).reshape(CAP, local_width)
-    back_k, back_v = shifted(jnp.stack([grad_k_near[:F_DEV], grad_v_near[:F_DEV]]), "seq", -1)
+    back = jnp.stack([grad_k_near[:F_DEV], grad_v_near[:F_DEV]]).reshape(2, row_count, local_width)
+    anchor_grads = jnp.stack([grad_k_anchor, grad_v_anchor])
+    if pair_first:
+        both = shifted(jnp.concatenate([back, anchor_grads], axis=1), "seq", -1)
+        back_k, back_v = both[:, :row_count].reshape(2, F_DEV, CAP, local_width)
+        anchor_grads = anchor_grads + jnp.where(odd, 0.0, both[:, row_count:])
+        anchor_gk, anchor_gv = tree_reduce(anchor_grads, "seq", jnp.bfloat16, first=1)
+    else:
+        back_k, back_v = shifted(back, "seq", -1).reshape(2, F_DEV, CAP, local_width)
+        anchor_gk, anchor_gv = tree_reduce(anchor_grads, "seq", jnp.bfloat16)
     grad_k_own = grad_k_near[F_DEV:] + back_k
     grad_v_own = grad_v_near[F_DEV:] + back_v
-    anchor_gk, anchor_gv = tree_reduce(jnp.stack([grad_k_anchor, grad_v_anchor]), "seq", jnp.bfloat16)
     first_device = device == 0
     grad_k_own = grad_k_own.at[0].add(jnp.where(first_device, anchor_gk, 0.0))
     grad_v_own = grad_v_own.at[0].add(jnp.where(first_device, anchor_gv, 0.0))

time: 139 us -> 169 us (1.22)
  waiting for transfers between devices: 41.4 us -> 66.5 us
  local copies, waits for them, and re-layouts: 21.9 us -> 34 us
  starting transfers between devices: 48.5 us -> 42.2 us
    ppermute x7 -> x6, waiting for transfers between devices: 15.7 us -> 31.8 us  [tree_reduce(): arrived = lax.ppermute(sent, axis, route)]
    another operation x3 -> x8, local copies, waits for them, and re-layouts: 0.77 us -> 11.6 us  [the longest x5 10.4 us: on_device(): back_k, back_v = both[:, :row_count].reshape(2, F_DEV, CAP, local_width)]
    all_to_all x2, waiting for transfers between devices: 14 us -> 20.9 us  [gather_sum(): return jnp.sum(lax.all_to_all(copies, axis, 0, 0, tiled=False), axis=0)]
    ppermute x2, waiting for transfers between devices: 0.01 us -> 4.48 us  [shifted(): return lax.ppermute(block, axis, route)]
    concatenate x12, local copies, waits for them, and re-layouts: 6.44 us -> 2.76 us  [stack_offsets(): return jnp.concatenate(blocks, axis=1)]
    concatenate x0 -> x3, other arithmetic: none -> 3.5 us  [the longest x1 2.54 us: on_device(): both = shifted(jnp.concatenate([back, anchor_grads], axis=1), 'seq', -1)]
    slice x0 -> x4, local copies, waits for them, and re-layouts: none -> 3.1 us  [the longest x2 2.87 us: on_device(): grad_v_near[:F_DEV]]
    another operation x2, local copies, waits for them, and re-layouts: 0.07 us -> 3.05 us  [on_device(): jnp.stack([grad_k_near[:F_DEV], grad_v_near[:F_DEV]])]
  transfers between devices with their start and end apart: 18 -> 16, of which waited for: 10 -> 14; matrix products, arithmetic and copies ran while one was open for 19% -> 13% of each run, Pallas kernels for 0% -> 0%
where the time goes in v7:
time: 169 us; the launch traced here: 168 us
  waiting for transfers between devices  66.5 us (39%)
  starting transfers between devices  42.2 us (25%)
  local copies, waits for them, and re-layouts  34 us (20%)
  other arithmetic  13.5 us (8%)
  matrix products  10.4 us (6%)
    ppermute x6, waiting for transfers between devices, tree_reduce(): arrived = lax.ppermute(sent, axis, route)  31.8 us
    all_to_all x2, waiting for transfers between devices, gather_sum(): return jnp.sum(lax.all_to_all(copies, axis, 0, 0, tiled=False), axis=0)  20.9 us
    all_to_all x2, starting transfers between devices, gather_sum(): return jnp.sum(lax.all_to_all(copies, axis, 0, 0, tiled=False), axis=0)  20.8 us
    ppermute x6, starting transfers between devices, tree_bcast(): arrived = lax.ppermute(values, axis, route)  10.8 us
    another operation x5, local copies, waits for them, and re-layouts, on_device(): back_k, back_v = both[:, :row_count].reshape(2, F_DEV, CAP, local_width)  10.4 us
    ppermute x6, waiting for transfers between devices, tree_bcast(): arrived = lax.ppermute(values, axis, route)  9.38 us
    unnamed x53, local copies, waits for them, and re-layouts  8.01 us
    ppermute x6, starting transfers between devices, tree_reduce(): arrived = lax.ppermute(sent, axis, route)  7.74 us
  transfers between devices with their start and end apart: 16, of which 14 were waited for; matrix products, arithmetic and copies ran while one was open for 13% of the time, Pallas kernels for 0%

profile of v7, /device:TPU:8, one launch (start us, length us, event | category | flops | bytes accessed | tf_op | source)
XLA Modules:
  0.0 168.1 jit_solution(7808147088416563508)
XLA Ops:
  3.8 16.0 %all-to-all-start = ((f32[16,2,512]{2,1,0:T(2,128)}), f32[16,2,512]{2,1,0:T(2,128)S(1)}, u32[]{:S(2)}, u32[]{:S(2)}) async-start(f32[16,2,512]{2,1,0:T(2,128)} %broadcast_in_dim.63), calls=%async_computation | async-start | bytes 131072 | tf_op jit(solution)/shard_map/all_to_all | solution.py:25
  20.2 11.1 %all-to-all-done = f32[16,2,512]{2,1,0:T(2,128)S(1)} async-done(((f32[16,2,512]{2,1,0:T(2,128)}), f32[16,2,512]{2,1,0:T(2,128)S(1)}, u32[]{:S(2)}, u32[]{:S(2)}) %all-to-all-start) | async-done | bytes 65568 | tf_op jit(solution)/shard_map/all_to_all | solution.py:25
  31.6 3.4 %collective-permute-start.2 = (bf16[2,256,256]{1,2,0:T(8,128)(2,1)S(1)}, bf16[2,256,256]{1,2,0:T(8,128)(2,1)S(1)}, u32[]{:S(2)}, u32[]{:S(2)}) collective-permute-start(bf16[2,256,256]{1,2,0:T(8,128)(2,1)S(1)} %pad_maximum_fusion.3), channel_id=1, source_target_pairs={{0,128},{1,129},{2,130},{3,131},{4,132},{5,133},{6,134},{7,135},{8... | collective-permute-start | bytes 786440 | tf_op jit(solution)/shard_map/ppermute | solution.py:52
  35.0 2.2 %collective-permute-start.1 = (bf16[2,256,256]{1,2,0:T(8,128)(2,1)S(1)}, bf16[2,256,256]{1,2,0:T(8,128)(2,1)S(1)}, u32[]{:S(2)}, u32[]{:S(2)}) collective-permute-start(bf16[2,256,256]{1,2,0:T(8,128)(2,1)S(1)} %pad_maximum_fusion.3), channel_id=1, source_target_pairs={{0,256},{1,257},{2,258},{3,259},{4,260},{5,261},{6,262},{7,263},{8... | collective-permute-start | bytes 786440 | tf_op jit(solution)/shard_map/ppermute | solution.py:52
  38.9 2.8 %collective-permute-done.1 = bf16[2,256,256]{1,2,0:T(8,128)(2,1)S(1)} collective-permute-done((bf16[2,256,256]{1,2,0:T(8,128)(2,1)S(1)}, bf16[2,256,256]{1,2,0:T(8,128)(2,1)S(1)}, u32[]{:S(2)}, u32[]{:S(2)}) %collective-permute-start.1) | collective-permute-done | bytes 262176 | tf_op jit(solution)/shard_map/ppermute | solution.py:52
  47.6 2.8 %collective-permute-done.4 = bf16[2,256,256]{1,2,0:T(8,128)(2,1)S(1)} collective-permute-done((bf16[2,256,256]{1,2,0:T(8,128)(2,1)S(1)}, bf16[2,256,256]{1,2,0:T(8,128)(2,1)S(1)}, u32[]{:S(2)}, u32[]{:S(2)}) %collective-permute-start.4) | collective-permute-done | bytes 262176 | tf_op jit(solution)/shard_map/ppermute | solution.py:52
  50.4 2.8 %collective-permute-done.3 = bf16[2,256,256]{1,2,0:T(8,128)(2,1)S(1)} collective-permute-done((bf16[2,256,256]{1,2,0:T(8,128)(2,1)S(1)}, bf16[2,256,256]{1,2,0:T(8,128)(2,1)S(1)}, u32[]{:S(2)}, u32[]{:S(2)}) %collective-permute-start.3) | collective-permute-done | bytes 262176 | tf_op jit(solution)/shard_map/ppermute | solution.py:52
  56.2 1.5 collective-permute-done.6
  76.6 2.0 %copy.186 = f32[2,256,256]{2,1,0:T(8,128)} copy(f32[2,256,256]{1,2,0:T(8,128)} %slice.171) | data formatting | bytes 1048576 | tf_op jit(solution)/shard_map/slice | solution.py:195
  78.7 2.0 %copy.188 = f32[1,512,256]{1,2,0:T(8,128)} copy(f32[1,512,256]{2,1,0:T(8,128)} %bitcast.163) | data formatting | bytes 1048576 | tf_op jit(solution)/shard_map/stack | solution.py:195
  80.7 2.5 %maximum_maximum_fusion = f32[2,768,256]{1,2,0:T(8,128)} fusion(f32[1,256,256]{1,2,0:T(8,128)S(1)} %bitcast.154, f32[1,256,256]{1,2,0:T(8,128)} %bitcast.157, f32[1,512,256]{1,2,0:T(8,128)} %copy.188, f32[1,512,256]{1,2,0:T(8,128)} %copy.187), kind=kLoop, calls=%fused_computation.6 | loop fusion | flops 1179648 | bytes 3145728 | tf_op jit(solution)/shard_map/concatenate | solution.py:198
  83.3 1.5 collective-permute-start.7
  85.7 2.1 %fusion.6 = f32[2,256,2,128]{3,1,0,2:T(8,128)S(1)} fusion(f32[2,2,256,128]{3,2,1,0:T(8,128)S(1)} %fusion.53, bf16[2,2,256,768]{3,2,1,0:T(8,128)(2,1)} %copy-done.7, bf16[2,256,2,128]{3,1,0,2:T(8,128)(2,1)} %copy-done.16, bf16[2,256,2,128]{3,1,0,2:T(8,128)(2,1)} %copy-done.15, bf16[2,256,2,128]{3,1,0,2:T(8,128)(2,1)} %copy-done.13), kind=kOutput, calls=%fused_computation.16 | convolution fusion | flops 203816960 | bytes 3407872 | tf_op jit(solution)/shard_map/hfqk,hfkd->hfqd/dot_general | solution.py:117
  90.1 3.0 %collective-permute-done.7 = f32[2,768,256]{1,2,0:T(8,128)} collective-permute-done((f32[2,768,256]{1,2,0:T(8,128)}, f32[2,768,256]{1,2,0:T(8,128)}, u32[]{:S(2)}, u32[]{:S(2)}) %collective-permute-start.7) | collective-permute-done | bytes 1572896 | tf_op jit(solution)/shard_map/ppermute | solution.py:19
  93.1 1.8 %fusion.58 = bf16[2,256,256]{1,2,0:T(8,128)(2,1)} fusion(f32[2,768,256]{1,2,0:T(8,128)} %collective-permute-done.7, pred[]{:T(512)S(6)} %eq.38, f32[1,256,256]{1,2,0:T(8,128)S(1)} %bitcast.155, f32[1,256,256]{1,2,0:T(8,128)S(1)} %bitcast.158), kind=kLoop, calls=%fused_computation.100 | loop fusion | flops 524288 | bytes 1310721 | tf_op jit(solution)/shard_map/convert_element_type | solution.py:66
  98.8 2.2 %fusion.78 = (f32[1,512,256]{1,2,0:T(8,128)}, f32[1,512,256]{1,2,0:T(8,128)}) fusion(f32[2,768,256]{1,2,0:T(8,128)} %collective-permute-done.7), kind=kLoop, calls=%fused_computation.143 | loop fusion | bytes 2097152 | tf_op jit(solution)/shard_map/unstack | solution.py:199
  101.1 2.0 %copy.196 = f32[1,512,256]{2,1,0:T(8,128)} copy(f32[1,512,256]{1,2,0:T(8,128)} %get-tuple-element.46) | data formatting | bytes 1048576 | tf_op jit(solution)/shard_map/unstack | solution.py:199
  103.1 2.0 %copy.197 = f32[2,256,256]{1,2,0:T(8,128)} copy(f32[2,256,256]{2,1,0:T(8,128)} %bitcast.165) | data formatting | bytes 1048576 | tf_op jit(solution)/shard_map/unstack | solution.py:199
  105.2 2.0 %copy.192 = f32[1,512,256]{2,1,0:T(8,128)} copy(f32[1,512,256]{1,2,0:T(8,128)} %get-tuple-element.47) | data formatting | bytes 1048576 | tf_op jit(solution)/shard_map/unstack | solution.py:199
  107.2 2.1 %copy.193 = f32[2,256,256]{1,2,0:T(8,128)} copy(f32[2,256,256]{2,1,0:T(8,128)} %bitcast.166) | data formatting | bytes 1048576 | tf_op jit(solution)/shard_map/unstack | solution.py:199
  110.4 15.3 %collective-permute-done.10 = bf16[2,256,256]{1,2,0:T(8,128)(2,1)} collective-permute-done((bf16[2,256,256]{1,2,0:T(8,128)(2,1)}, bf16[2,256,256]{1,2,0:T(8,128)(2,1)}, u32[]{:S(2)}, u32[]{:S(2)}) %collective-permute-start.10) | collective-permute-done | bytes 262176 | tf_op jit(solution)/shard_map/ppermute | solution.py:67
  131.9 15.7 %collective-permute-done.13 = bf16[2,256,256]{1,2,0:T(8,128)(2,1)S(1)} collective-permute-done((bf16[2,256,256]{1,2,0:T(8,128)(2,1)S(1)}, bf16[2,256,256]{1,2,0:T(8,128)(2,1)S(1)}, u32[]{:S(2)}, u32[]{:S(2)}) %collective-permute-start.13) | collective-permute-done | bytes 262176 | tf_op jit(solution)/shard_map/ppermute | solution.py:67
  149.6 4.8 %all-to-all-start.1 = ((f32[16,2,512]{2,1,0:T(2,128)}), f32[16,2,512]{2,1,0:T(2,128)S(1)}, u32[]{:S(2)}, u32[]{:S(2)}) async-start(f32[16,2,512]{2,1,0:T(2,128)} %broadcast_in_dim.108), calls=%async_computation.1 | async-start | bytes 131072 | tf_op jit(solution)/shard_map/all_to_all | solution.py:25
  156.3 9.7 %all-to-all-done.1 = f32[16,2,512]{2,1,0:T(2,128)S(1)} async-done(((f32[16,2,512]{2,1,0:T(2,128)}), f32[16,2,512]{2,1,0:T(2,128)S(1)}, u32[]{:S(2)}, u32[]{:S(2)}) %all-to-all-start.1) | async-done | bytes 65568 | tf_op jit(solution)/shard_map/all_to_all | solution.py:25
  (164 shorter events, 52.9 us)
Async XLA Ops:
  0.6 19.2 %copy-start.22 = (s32[64]{0:T(128)S(1)}, s32[64]{0:T(128)}, u32[]{:S(2)}) copy-start(s32[64]{0:T(128)} %param.18) | copy-start | bytes 772
  0.6 19.3 %copy-start.8 = (bf16[512,256]{1,0:T(8,128)(2,1)S(1)}, bf16[512,256]{1,0:T(8,128)(2,1)}, u32[]{:S(2)}) copy-start(bf16[512,256]{1,0:T(8,128)(2,1)} %param.14) | copy-start | bytes 786436
  0.7 19.5 %copy-start.21 = (s32[2]{0:T(128)S(1)}, s32[2]{0:T(128)}, u32[]{:S(2)}) copy-start(s32[2]{0:T(128)} %param.19) | copy-start | bytes 28
  0.7 30.8 %copy-start.18 = (f32[256]{0:T(256)S(1)}, f32[256]{0:T(256)}, u32[]{:S(2)}) copy-start(f32[256]{0:T(256)} %param.16) | copy-start | bytes 3076
  1.9 36.7 %copy-start.12 = (bf16[512,256]{1,0:T(8,128)(2,1)S(1)}, bf16[512,256]{1,0:T(8,128)(2,1)}, u32[]{:S(2)}) copy-start(bf16[512,256]{1,0:T(8,128)(2,1)} %param.17) | copy-start | bytes 786436
  3.8 27.6 %all-to-all-start = ((f32[16,2,512]{2,1,0:T(2,128)}), f32[16,2,512]{2,1,0:T(2,128)S(1)}, u32[]{:S(2)}, u32[]{:S(2)}) async-start(f32[16,2,512]{2,1,0:T(2,128)} %broadcast_in_dim.63), calls=%async_computation | async-start | bytes 131072 | tf_op jit(solution)/shard_map/all_to_all | solution.py:25
  31.6 7.3 %collective-permute-start.2 = (bf16[2,256,256]{1,2,0:T(8,128)(2,1)S(1)}, bf16[2,256,256]{1,2,0:T(8,128)(2,1)S(1)}, u32[]{:S(2)}, u32[]{:S(2)}) collective-permute-start(bf16[2,256,256]{1,2,0:T(8,128)(2,1)S(1)} %pad_maximum_fusion.3), channel_id=1, source_target_pairs={{0,128},{1,129},{2,130},{3,131},{4,132},{5,133},{6,134},{7,135},{8... | collective-permute-start | bytes 786440 | tf_op jit(solution)/shard_map/ppermute | solution.py:52
  35.0 6.7 %collective-permute-start.1 = (bf16[2,256,256]{1,2,0:T(8,128)(2,1)S(1)}, bf16[2,256,256]{1,2,0:T(8,128)(2,1)S(1)}, u32[]{:S(2)}, u32[]{:S(2)}) collective-permute-start(bf16[2,256,256]{1,2,0:T(8,128)(2,1)S(1)} %pad_maximum_fusion.3), channel_id=1, source_target_pairs={{0,256},{1,257},{2,258},{3,259},{4,260},{5,261},{6,262},{7,263},{8... | collective-permute-start | bytes 786440 | tf_op jit(solution)/shard_map/ppermute | solution.py:52
  37.2 5.2 %collective-permute-start = (bf16[2,256,256]{1,2,0:T(8,128)(2,1)S(1)}, bf16[2,256,256]{1,2,0:T(8,128)(2,1)S(1)}, u32[]{:S(2)}, u32[]{:S(2)}) collective-permute-start(bf16[2,256,256]{1,2,0:T(8,128)(2,1)S(1)} %pad_maximum_fusion.3), channel_id=1, source_target_pairs={{0,384},{1,385},{2,386},{3,387},{4,388},{5,389},{6,390},{7,391},{8... | collective-permute-start | bytes 786440 | tf_op jit(solution)/shard_map/ppermute | solution.py:52
  42.5 5.2 %collective-permute-start.5 = (bf16[2,256,256]{1,2,0:T(8,128)(2,1)S(1)}, bf16[2,256,256]{1,2,0:T(8,128)(2,1)S(1)}, u32[]{:S(2)}, u32[]{:S(2)}) collective-permute-start(bf16[2,256,256]{1,2,0:T(8,128)(2,1)S(1)} %select_select_fusion.1), channel_id=1, source_target_pairs={{0,32},{128,160},{256,288},{384,416},{1,33},{129,161},{257,289},{3... | collective-permute-start | bytes 786440 | tf_op jit(solution)/shard_map/ppermute | solution.py:52
  43.8 6.7 %collective-permute-start.4 = (bf16[2,256,256]{1,2,0:T(8,128)(2,1)S(1)}, bf16[2,256,256]{1,2,0:T(8,128)(2,1)S(1)}, u32[]{:S(2)}, u32[]{:S(2)}) collective-permute-start(bf16[2,256,256]{1,2,0:T(8,128)(2,1)S(1)} %select_select_fusion.1), channel_id=1, source_target_pairs={{0,64},{128,192},{256,320},{384,448},{1,65},{129,193},{257,321},{3... | collective-permute-start | bytes 786440 | tf_op jit(solution)/shard_map/ppermute | solution.py:52
  45.1 8.2 %collective-permute-start.3 = (bf16[2,256,256]{1,2,0:T(8,128)(2,1)S(1)}, bf16[2,256,256]{1,2,0:T(8,128)(2,1)S(1)}, u32[]{:S(2)}, u32[]{:S(2)}) collective-permute-start(bf16[2,256,256]{1,2,0:T(8,128)(2,1)S(1)} %select_select_fusion.1), channel_id=1, source_target_pairs={{0,96},{128,224},{256,352},{384,480},{1,97},{129,225},{257,353},{3... | collective-permute-start | bytes 786440 | tf_op jit(solution)/shard_map/ppermute | solution.py:52
  54.3 3.4 %collective-permute-start.6 = (bf16[2,768,256]{1,2,0:T(8,128)(2,1)}, bf16[2,768,256]{1,2,0:T(8,128)(2,1)S(1)}, u32[]{:S(2)}, u32[]{:S(2)}) collective-permute-start(bf16[2,768,256]{1,2,0:T(8,128)(2,1)} %pad_maximum_fusion), channel_id=1, source_target_pairs={{0,16},{16,32},{32,48},{48,64},{64,80},{80,96},{96,112},{112,128},... | collective-permute-start | bytes 2359304 | tf_op jit(solution)/shard_map/ppermute | solution.py:19
  83.3 9.9 %collective-permute-start.7 = (f32[2,768,256]{1,2,0:T(8,128)}, f32[2,768,256]{1,2,0:T(8,128)}, u32[]{:S(2)}, u32[]{:S(2)}) collective-permute-start(f32[2,768,256]{1,2,0:T(8,128)} %maximum_maximum_fusion), channel_id=1, source_target_pairs={{16,0},{32,16},{48,32},{64,48},{80,64},{96,80},{112,96},{128,112},... | collective-permute-start | bytes 4718600 | tf_op jit(solution)/shard_map/ppermute | solution.py:19
  95.0 30.8 %collective-permute-start.10 = (bf16[2,256,256]{1,2,0:T(8,128)(2,1)}, bf16[2,256,256]{1,2,0:T(8,128)(2,1)}, u32[]{:S(2)}, u32[]{:S(2)}) collective-permute-start(bf16[2,256,256]{1,2,0:T(8,128)(2,1)} %fusion.58), channel_id=1, source_target_pairs={{96,0},{224,128},{352,256},{480,384},{97,1},{225,129},{353,257},{4... | collective-permute-start | bytes 786440 | tf_op jit(solution)/shard_map/ppermute | solution.py:67
  96.2 29.9 %collective-permute-start.9 = (bf16[2,256,256]{1,2,0:T(8,128)(2,1)}, bf16[2,256,256]{1,2,0:T(8,128)(2,1)}, u32[]{:S(2)}, u32[]{:S(2)}) collective-permute-start(bf16[2,256,256]{1,2,0:T(8,128)(2,1)} %fusion.58), channel_id=1, source_target_pairs={{64,0},{192,128},{320,256},{448,384},{65,1},{193,129},{321,257},{4... | collective-permute-start | bytes 786440 | tf_op jit(solution)/shard_map/ppermute | solution.py:67
  97.5 28.9 %collective-permute-start.8 = (bf16[2,256,256]{1,2,0:T(8,128)(2,1)}, bf16[2,256,256]{1,2,0:T(8,128)(2,1)}, u32[]{:S(2)}, u32[]{:S(2)}) collective-permute-start(bf16[2,256,256]{1,2,0:T(8,128)(2,1)} %fusion.58), channel_id=1, source_target_pairs={{32,0},{160,128},{288,256},{416,384},{33,1},{161,129},{289,257},{4... | collective-permute-start | bytes 786440 | tf_op jit(solution)/shard_map/ppermute | solution.py:67
  109.3 17.2 %copy-start.3 = (f32[2,256,128,1]{1,2,3,0:T(8,128)S(1)}, f32[2,256,128,1]{1,2,3,0:T(8,128)}, u32[]{:S(2)}) copy-start(f32[2,256,128,1]{1,2,3,0:T(8,128)} %fusion.38) | copy-start | bytes 786436
  110.4 21.4 %copy-start.6 = (f32[2,256,256]{1,2,0:T(8,128)S(1)}, f32[2,256,256]{1,2,0:T(8,128)}, u32[]{:S(2)}) copy-start(f32[2,256,256]{1,2,0:T(8,128)} %copy.193) | copy-start | bytes 1572868
  127.9 19.7 %collective-permute-start.13 = (bf16[2,256,256]{1,2,0:T(8,128)(2,1)S(1)}, bf16[2,256,256]{1,2,0:T(8,128)(2,1)S(1)}, u32[]{:S(2)}, u32[]{:S(2)}) collective-permute-start(bf16[2,256,256]{1,2,0:T(8,128)(2,1)S(1)} %get-tuple-element.44), channel_id=1, source_target_pairs={{384,0},{385,1},{386,2},{387,3},{388,4},{389,5},{390,6},{391,7},{3... | collective-permute-start | bytes 786440 | tf_op jit(solution)/shard_map/ppermute | solution.py:67
  129.2 18.4 %collective-permute-start.12 = (bf16[2,256,256]{1,2,0:T(8,128)(2,1)S(1)}, bf16[2,256,256]{1,2,0:T(8,128)(2,1)S(1)}, u32[]{:S(2)}, u32[]{:S(2)}) collective-permute-start(bf16[2,256,256]{1,2,0:T(8,128)(2,1)S(1)} %get-tuple-element.44), channel_id=1, source_target_pairs={{256,0},{257,1},{258,2},{259,3},{260,4},{261,5},{262,6},{263,7},{2... | collective-permute-start | bytes 786440 | tf_op jit(solution)/shard_map/ppermute | solution.py:67
  130.5 17.1 %collective-permute-start.11 = (bf16[2,256,256]{1,2,0:T(8,128)(2,1)S(1)}, bf16[2,256,256]{1,2,0:T(8,128)(2,1)S(1)}, u32[]{:S(2)}, u32[]{:S(2)}) collective-permute-start(bf16[2,256,256]{1,2,0:T(8,128)(2,1)S(1)} %get-tuple-element.44), channel_id=1, source_target_pairs={{128,0},{129,1},{130,2},{131,3},{132,4},{133,5},{134,6},{135,7},{1... | collective-permute-start | bytes 786440 | tf_op jit(solution)/shard_map/ppermute | solution.py:67
  149.6 16.5 %all-to-all-start.1 = ((f32[16,2,512]{2,1,0:T(2,128)}), f32[16,2,512]{2,1,0:T(2,128)S(1)}, u32[]{:S(2)}, u32[]{:S(2)}) async-start(f32[16,2,512]{2,1,0:T(2,128)} %broadcast_in_dim.108), calls=%async_computation.1 | async-start | bytes 131072 | tf_op jit(solution)/shard_map/all_to_all | solution.py:25
  155.4 11.7 %copy-start.20 = (f32[512]{0:T(512)S(1)}, f32[512]{0:T(512)}, u32[]{:S(2)}) copy-start(f32[512]{0:T(512)} %multiply_multiply_fusion.1) | copy-start | bytes 6148
  (15 other events, 46.7 us)

commit v8 on v7

--- a/solution.py
+++ b/solution.py
@@ -192,18 +192,10 @@
     grad_v_near = fold_offsets(from_heads(grad_vh), F_DEV, F_DEV, CAP)
     grad_k_anchor = grad_ka.transpose(1, 0, 2).reshape(CAP, local_width)
     grad_v_anchor = grad_va.transpose(1, 0, 2).reshape(CAP, local_width)
-    back = jnp.stack([grad_k_near[:F_DEV], grad_v_near[:F_DEV]]).reshape(2, row_count, local_width)
-    anchor_grads = jnp.stack([grad_k_anchor, grad_v_anchor])
-    if pair_first:
-        both = shifted(jnp.concatenate([back, anchor_grads], axis=1), "seq", -1)
-        back_k, back_v = both[:, :row_count].reshape(2, F_DEV, CAP, local_width)
-        anchor_grads = anchor_grads + jnp.where(odd, 0.0, both[:, row_count:])
-        anchor_gk, anchor_gv = tree_reduce(anchor_grads, "seq", jnp.bfloat16, first=1)
-    else:
-        back_k, back_v = shifted(back, "seq", -1).reshape(2, F_DEV, CAP, local_width)
-        anchor_gk, anchor_gv = tree_reduce(anchor_grads, "seq", jnp.bfloat16)
+    back_k, back_v = shifted(jnp.stack([grad_k_near[:F_DEV], grad_v_near[:F_DEV]]), "seq", -1)
     grad_k_own = grad_k_near[F_DEV:] + back_k
     grad_v_own = grad_v_near[F_DEV:] + back_v
+    anchor_gk, anchor_gv = tree_reduce(jnp.stack([grad_k_anchor, grad_v_anchor]), "seq", jnp.bfloat16)
     first_device = device == 0
     grad_k_own = grad_k_own.at[0].add(jnp.where(first_device, anchor_gk, 0.0))
     grad_v_own = grad_v_own.at[0].add(jnp.where(first_device, anchor_gv, 0.0))

time: 169 us -> 137 us (0.81)
  local copies, waits for them, and re-layouts: 34 us -> 14.9 us
  waiting for transfers between devices: 66.5 us -> 53.4 us
  matrix products: 10.4 us -> 8.17 us
    another operation x5 -> x0, local copies, waits for them, and re-layouts: 10.4 us -> none  [on_device(): back_k, back_v = both[:, :row_count].reshape(2, F_DEV, CAP, local_width)]
    ppermute x6 -> x7, waiting for transfers between devices: 31.8 us -> 26.2 us  [tree_reduce(): arrived = lax.ppermute(sent, axis, route)]
    ppermute x2, waiting for transfers between devices: 4.48 us -> 0.01 us  [shifted(): return lax.ppermute(block, axis, route)]
    slice x4 -> x0, local copies, waits for them, and re-layouts: 3.1 us -> none  [the longest x2 2.87 us: on_device(): grad_v_near[:F_DEV]]
    another operation x2, local copies, waits for them, and re-layouts: 3.05 us -> 0.07 us  [on_device(): jnp.stack([grad_k_near[:F_DEV], grad_v_near[:F_DEV]])]
    all_to_all x2, waiting for transfers between devices: 20.9 us -> 18 us  [gather_sum(): return jnp.sum(lax.all_to_all(copies, axis, 0, 0, tiled=False), axis=0)]
    concatenate x1 -> x0, other arithmetic: 2.54 us -> none  [on_device(): both = shifted(jnp.concatenate([back, anchor_grads], axis=1), 'seq', -1)]
    convert_element_type x2 -> x3, other arithmetic: 3.25 us -> 0.95 us  [tree_reduce(): sent = jax.tree.map(lambda a: a.astype(wire), values)]
  transfers between devices with their start and end apart: 16 -> 17, of which waited for: 14 -> 11; matrix products, arithmetic and copies ran while one was open for 13% -> 14% of each run, Pallas kernels for 0% -> 0%
where the time goes in v8:
time: 137 us; the launch traced here: 136 us
  waiting for transfers between devices  53.4 us (39%)
  starting transfers between devices  43.6 us (32%)
  local copies, waits for them, and re-layouts  14.9 us (11%)
  other arithmetic  14.4 us (11%)
  matrix products  8.17 us (6%)
  between operations  1.53 us (1%)
    ppermute x7, waiting for transfers between devices, tree_reduce(): arrived = lax.ppermute(sent, axis, route)  26.2 us
    all_to_all x2, starting transfers between devices, gather_sum(): return jnp.sum(lax.all_to_all(copies, axis, 0, 0, tiled=False), axis=0)  20.8 us
    all_to_all x2, waiting for transfers between devices, gather_sum(): return jnp.sum(lax.all_to_all(copies, axis, 0, 0, tiled=False), axis=0)  18 us
    ppermute x6, starting transfers between devices, tree_bcast(): arrived = lax.ppermute(values, axis, route)  10.8 us
    ppermute x7, starting transfers between devices, tree_reduce(): arrived = lax.ppermute(sent, axis, route)  9.35 us
    ppermute x6, waiting for transfers between devices, tree_bcast(): arrived = lax.ppermute(values, axis, route)  9.14 us
    unnamed x51, local copies, waits for them, and re-layouts  5.89 us
    concatenate x12, local copies, waits for them, and re-layouts, stack_offsets(): return jnp.concatenate(blocks, axis=1)  3.44 us
  transfers between devices with their start and end apart: 17, of which 11 were waited for; matrix products, arithmetic and copies ran while one was open for 14% of the time, Pallas kernels for 0%

profile of v8, /device:TPU:8, one launch (start us, length us, event | category | flops | bytes accessed | tf_op | source)
XLA Modules:
  0.0 136.0 jit_solution(8811111934524745067)
XLA Ops:
  3.7 16.0 %all-to-all-start = ((f32[16,2,512]{2,1,0:T(2,128)}), f32[16,2,512]{2,1,0:T(2,128)S(1)}, u32[]{:S(2)}, u32[]{:S(2)}) async-start(f32[16,2,512]{2,1,0:T(2,128)} %broadcast_in_dim.58), calls=%async_computation | async-start | bytes 131072 | tf_op jit(solution)/shard_map/all_to_all | solution.py:25
  21.7 1.3 fusion.63
  23.0 8.3 %all-to-all-done = f32[16,2,512]{2,1,0:T(2,128)S(1)} async-done(((f32[16,2,512]{2,1,0:T(2,128)}), f32[16,2,512]{2,1,0:T(2,128)S(1)}, u32[]{:S(2)}, u32[]{:S(2)}) %all-to-all-start) | async-done | bytes 65568 | tf_op jit(solution)/shard_map/all_to_all | solution.py:25
  32.2 3.4 %collective-permute-start.2 = (bf16[2,256,256]{1,2,0:T(8,128)(2,1)S(1)}, bf16[2,256,256]{1,2,0:T(8,128)(2,1)S(1)}, u32[]{:S(2)}, u32[]{:S(2)}) collective-permute-start(bf16[2,256,256]{1,2,0:T(8,128)(2,1)S(1)} %pad_maximum_fusion.5), channel_id=1, source_target_pairs={{0,128},{1,129},{2,130},{3,131},{4,132},{5,133},{6,134},{7,135},{8... | collective-permute-start | bytes 786440 | tf_op jit(solution)/shard_map/ppermute | solution.py:52
  35.6 2.2 %collective-permute-start.1 = (bf16[2,256,256]{1,2,0:T(8,128)(2,1)S(1)}, bf16[2,256,256]{1,2,0:T(8,128)(2,1)S(1)}, u32[]{:S(2)}, u32[]{:S(2)}) collective-permute-start(bf16[2,256,256]{1,2,0:T(8,128)(2,1)S(1)} %pad_maximum_fusion.5), channel_id=1, source_target_pairs={{0,256},{1,257},{2,258},{3,259},{4,260},{5,261},{6,262},{7,263},{8... | collective-permute-start | bytes 786440 | tf_op jit(solution)/shard_map/ppermute | solution.py:52
  37.9 1.3 collective-permute-start
  39.9 2.4 %collective-permute-done.1 = bf16[2,256,256]{1,2,0:T(8,128)(2,1)S(1)} collective-permute-done((bf16[2,256,256]{1,2,0:T(8,128)(2,1)S(1)}, bf16[2,256,256]{1,2,0:T(8,128)(2,1)S(1)}, u32[]{:S(2)}, u32[]{:S(2)}) %collective-permute-start.1) | collective-permute-done | bytes 262176 | tf_op jit(solution)/shard_map/ppermute | solution.py:52
  43.1 1.3 collective-permute-start.5
  44.4 1.3 collective-permute-start.4
  45.7 1.3 collective-permute-start.3
  48.3 2.8 %collective-permute-done.4 = bf16[2,256,256]{1,2,0:T(8,128)(2,1)S(1)} collective-permute-done((bf16[2,256,256]{1,2,0:T(8,128)(2,1)S(1)}, bf16[2,256,256]{1,2,0:T(8,128)(2,1)S(1)}, u32[]{:S(2)}, u32[]{:S(2)}) %collective-permute-start.4) | collective-permute-done | bytes 262176 | tf_op jit(solution)/shard_map/ppermute | solution.py:52
  51.1 2.8 %collective-permute-done.3 = bf16[2,256,256]{1,2,0:T(8,128)(2,1)S(1)} collective-permute-done((bf16[2,256,256]{1,2,0:T(8,128)(2,1)S(1)}, bf16[2,256,256]{1,2,0:T(8,128)(2,1)S(1)}, u32[]{:S(2)}, u32[]{:S(2)}) %collective-permute-start.3) | collective-permute-done | bytes 262176 | tf_op jit(solution)/shard_map/ppermute | solution.py:52
  54.9 1.3 collective-permute-start.6
  70.1 1.3 collective-permute-start.8
  72.6 2.5 %collective-permute-done.8 = bf16[2,256,256]{1,2,0:T(8,128)(2,1)S(1)} collective-permute-done((bf16[2,256,256]{1,2,0:T(8,128)(2,1)S(1)}, bf16[2,256,256]{1,2,0:T(8,128)(2,1)S(1)}, u32[]{:S(2)}, u32[]{:S(2)}) %collective-permute-start.8) | collective-permute-done | bytes 262176 | tf_op jit(solution)/shard_map/ppermute | solution.py:67
  81.7 10.0 %collective-permute-done.11 = bf16[2,256,256]{1,2,0:T(8,128)(2,1)S(1)} collective-permute-done((bf16[2,256,256]{1,2,0:T(8,128)(2,1)S(1)}, bf16[2,256,256]{1,2,0:T(8,128)(2,1)S(1)}, u32[]{:S(2)}, u32[]{:S(2)}) %collective-permute-start.11) | collective-permute-done | bytes 262176 | tf_op jit(solution)/shard_map/ppermute | solution.py:67
  93.2 1.4 %collective-permute-start.14 = (bf16[2,256,256]{1,2,0:T(8,128)(2,1)}, bf16[2,256,256]{1,2,0:T(8,128)(2,1)}, u32[]{:S(2)}, u32[]{:S(2)}) collective-permute-start(bf16[2,256,256]{1,2,0:T(8,128)(2,1)} %fusion.79), channel_id=1, source_target_pairs={{384,0},{385,1},{386,2},{387,3},{388,4},{389,5},{390,6},{391,7},{3... | collective-permute-start | bytes 786440 | tf_op jit(solution)/shard_map/ppermute | solution.py:67
  95.9 1.5 %collective-permute-start.12 = (bf16[2,256,256]{1,2,0:T(8,128)(2,1)}, bf16[2,256,256]{1,2,0:T(8,128)(2,1)}, u32[]{:S(2)}, u32[]{:S(2)}) collective-permute-start(bf16[2,256,256]{1,2,0:T(8,128)(2,1)} %fusion.79), channel_id=1, source_target_pairs={{128,0},{129,1},{130,2},{131,3},{132,4},{133,5},{134,6},{135,7},{1... | collective-permute-start | bytes 786440 | tf_op jit(solution)/shard_map/ppermute | solution.py:67
  97.5 1.4 %fusion.6 = f32[2,256,2,128]{3,1,0,2:T(8,128)} fusion(f32[2,2,256,128]{3,2,1,0:T(8,128)S(1)} %fusion.56, bf16[2,2,256,768]{3,2,1,0:T(8,128)(2,1)S(1)} %multiply_convert_fusion, bf16[2,256,2,128]{3,1,0,2:T(8,128)(2,1)S(1)} %copy-done.12, bf16[2,256,2,128]{3,1,0,2:T(8,128)(2,1)S(1)} %copy.147, bf16[2,256,2,128]{3,1,0,2:T(8,128)(2,1)S(1)} %copy-done.10), kind=kOutput, calls=%fused_computation.15 | convolution fusion | flops 203816960 | bytes 3407872 | tf_op jit(solution)/shard_map/hfqk,hfkd->hfqd/dot_general | solution.py:117
  100.3 13.1 %collective-permute-done.14 = bf16[2,256,256]{1,2,0:T(8,128)(2,1)} collective-permute-done((bf16[2,256,256]{1,2,0:T(8,128)(2,1)}, bf16[2,256,256]{1,2,0:T(8,128)(2,1)}, u32[]{:S(2)}, u32[]{:S(2)}) %collective-permute-start.14) | collective-permute-done | bytes 262176 | tf_op jit(solution)/shard_map/ppermute | solution.py:67
  113.5 1.6 %convert_add_fusion = f32[2,256,256]{1,2,0:T(8,128)S(1)} fusion(bf16[2,256,256]{1,2,0:T(8,128)(2,1)} %collective-permute-done.14, bf16[2,256,256]{1,2,0:T(8,128)(2,1)} %collective-permute-done.13, bf16[2,256,256]{1,2,0:T(8,128)(2,1)} %collective-permute-done.12, bf16[2,256,256]{1,2,0:T(8,128)(2,1)} %copy-done.5, bf16[2,256,256]{1,2,0:T(8,128)(2,1)} %copy-done.6, ...), kind=kLoop, calls=%fused_computation.59 | loop fusion | flops 1966080 | bytes 2883584 | tf_op jit(solution)/shard_map/add | solution.py:68
  115.1 1.4 %fusion.26 = (f32[2,256,256]{1,2,0:T(8,128)S(1)}, f32[2,256,256]{1,2,0:T(8,128)S(1)}) fusion(f32[2,2,256,256]{2,3,1,0:T(8,128)} %collective-permute-done.7, f32[4,256,256]{1,2,0:T(8,128)S(1)} %copy-done.1, f32[4,256,256]{1,2,0:T(8,128)S(1)} %pad_add_fusion.1), kind=kLoop, calls=%fused_computation.53 | loop fusion | flops 262144 | bytes 3145728 | tf_op jit(solution)/shard_map/add | solution.py:197
  117.5 4.8 %all-to-all-start.1 = ((f32[16,2,512]{2,1,0:T(2,128)}), f32[16,2,512]{2,1,0:T(2,128)S(1)}, u32[]{:S(2)}, u32[]{:S(2)}) async-start(f32[16,2,512]{2,1,0:T(2,128)} %broadcast_in_dim.103), calls=%async_computation.1 | async-start | bytes 131072 | tf_op jit(solution)/shard_map/all_to_all | solution.py:25
  124.2 9.7 %all-to-all-done.1 = f32[16,2,512]{2,1,0:T(2,128)S(1)} async-done(((f32[16,2,512]{2,1,0:T(2,128)}), f32[16,2,512]{2,1,0:T(2,128)S(1)}, u32[]{:S(2)}, u32[]{:S(2)}) %all-to-all-start.1) | async-done | bytes 65568 | tf_op jit(solution)/shard_map/all_to_all | solution.py:25
  (155 shorter events, 40.0 us)
Async XLA Ops:
  0.6 38.5 %copy-start.20 = (s32[2]{0:T(128)S(1)}, s32[2]{0:T(128)}, u32[]{:S(2)}) copy-start(s32[2]{0:T(128)} %param.19) | copy-start | bytes 28
  0.6 47.1 %copy-start.15 = (f32[256]{0:T(256)S(1)}, f32[256]{0:T(256)}, u32[]{:S(2)}) copy-start(f32[256]{0:T(256)} %param.16) | copy-start | bytes 3076
  0.7 39.1 %copy-start.8 = (bf16[512,256]{1,0:T(8,128)(2,1)S(1)}, bf16[512,256]{1,0:T(8,128)(2,1)}, u32[]{:S(2)}) copy-start(bf16[512,256]{1,0:T(8,128)(2,1)} %param.17) | copy-start | bytes 786436
  3.7 27.6 %all-to-all-start = ((f32[16,2,512]{2,1,0:T(2,128)}), f32[16,2,512]{2,1,0:T(2,128)S(1)}, u32[]{:S(2)}, u32[]{:S(2)}) async-start(f32[16,2,512]{2,1,0:T(2,128)} %broadcast_in_dim.58), calls=%async_computation | async-start | bytes 131072 | tf_op jit(solution)/shard_map/all_to_all | solution.py:25
  32.2 24.1 %copy-start.2 = (bf16[512,256]{1,0:T(8,128)(2,1)S(1)}, bf16[512,256]{1,0:T(8,128)(2,1)}, u32[]{:S(2)}) copy-start(bf16[512,256]{1,0:T(8,128)(2,1)} %param.14) | copy-start | bytes 786436
  32.2 7.7 %collective-permute-start.2 = (bf16[2,256,256]{1,2,0:T(8,128)(2,1)S(1)}, bf16[2,256,256]{1,2,0:T(8,128)(2,1)S(1)}, u32[]{:S(2)}, u32[]{:S(2)}) collective-permute-start(bf16[2,256,256]{1,2,0:T(8,128)(2,1)S(1)} %pad_maximum_fusion.5), channel_id=1, source_target_pairs={{0,128},{1,129},{2,130},{3,131},{4,132},{5,133},{6,134},{7,135},{8... | collective-permute-start | bytes 786440 | tf_op jit(solution)/shard_map/ppermute | solution.py:52
  35.6 6.7 %collective-permute-start.1 = (bf16[2,256,256]{1,2,0:T(8,128)(2,1)S(1)}, bf16[2,256,256]{1,2,0:T(8,128)(2,1)S(1)}, u32[]{:S(2)}, u32[]{:S(2)}) collective-permute-start(bf16[2,256,256]{1,2,0:T(8,128)(2,1)S(1)} %pad_maximum_fusion.5), channel_id=1, source_target_pairs={{0,256},{1,257},{2,258},{3,259},{4,260},{5,261},{6,262},{7,263},{8... | collective-permute-start | bytes 786440 | tf_op jit(solution)/shard_map/ppermute | solution.py:52
  37.9 5.2 %collective-permute-start = (bf16[2,256,256]{1,2,0:T(8,128)(2,1)S(1)}, bf16[2,256,256]{1,2,0:T(8,128)(2,1)S(1)}, u32[]{:S(2)}, u32[]{:S(2)}) collective-permute-start(bf16[2,256,256]{1,2,0:T(8,128)(2,1)S(1)} %pad_maximum_fusion.5), channel_id=1, source_target_pairs={{0,384},{1,385},{2,386},{3,387},{4,388},{5,389},{6,390},{7,391},{8... | collective-permute-start | bytes 786440 | tf_op jit(solution)/shard_map/ppermute | solution.py:52
  43.1 5.2 %collective-permute-start.5 = (bf16[2,256,256]{1,2,0:T(8,128)(2,1)S(1)}, bf16[2,256,256]{1,2,0:T(8,128)(2,1)S(1)}, u32[]{:S(2)}, u32[]{:S(2)}) collective-permute-start(bf16[2,256,256]{1,2,0:T(8,128)(2,1)S(1)} %select_select_fusion.1), channel_id=1, source_target_pairs={{0,32},{128,160},{256,288},{384,416},{1,33},{129,161},{257,289},{3... | collective-permute-start | bytes 786440 | tf_op jit(solution)/shard_map/ppermute | solution.py:52
  44.4 6.7 %collective-permute-start.4 = (bf16[2,256,256]{1,2,0:T(8,128)(2,1)S(1)}, bf16[2,256,256]{1,2,0:T(8,128)(2,1)S(1)}, u32[]{:S(2)}, u32[]{:S(2)}) collective-permute-start(bf16[2,256,256]{1,2,0:T(8,128)(2,1)S(1)} %select_select_fusion.1), channel_id=1, source_target_pairs={{0,64},{128,192},{256,320},{384,448},{1,65},{129,193},{257,321},{3... | collective-permute-start | bytes 786440 | tf_op jit(solution)/shard_map/ppermute | solution.py:52
  45.7 8.2 %collective-permute-start.3 = (bf16[2,256,256]{1,2,0:T(8,128)(2,1)S(1)}, bf16[2,256,256]{1,2,0:T(8,128)(2,1)S(1)}, u32[]{:S(2)}, u32[]{:S(2)}) collective-permute-start(bf16[2,256,256]{1,2,0:T(8,128)(2,1)S(1)} %select_select_fusion.1), channel_id=1, source_target_pairs={{0,96},{128,224},{256,352},{384,480},{1,97},{129,225},{257,353},{3... | collective-permute-start | bytes 786440 | tf_op jit(solution)/shard_map/ppermute | solution.py:52
  54.9 5.4 %collective-permute-start.6 = (bf16[2,768,256]{1,2,0:T(8,128)(2,1)}, bf16[2,768,256]{1,2,0:T(8,128)(2,1)S(1)}, u32[]{:S(2)}, u32[]{:S(2)}) collective-permute-start(bf16[2,768,256]{1,2,0:T(8,128)(2,1)} %pad_maximum_fusion.1), channel_id=1, source_target_pairs={{0,16},{16,32},{32,48},{48,64},{64,80},{80,96},{96,112},{112,128},... | collective-permute-start | bytes 2359304 | tf_op jit(solution)/shard_map/ppermute | solution.py:19
  70.1 5.0 %collective-permute-start.8 = (bf16[2,256,256]{1,2,0:T(8,128)(2,1)S(1)}, bf16[2,256,256]{1,2,0:T(8,128)(2,1)S(1)}, u32[]{:S(2)}, u32[]{:S(2)}) collective-permute-start(bf16[2,256,256]{1,2,0:T(8,128)(2,1)S(1)} %fusion.28), channel_id=1, source_target_pairs={{16,0},{48,32},{80,64},{112,96},{144,128},{176,160},{208,192},{240... | collective-permute-start | bytes 786440 | tf_op jit(solution)/shard_map/ppermute | solution.py:67
  72.5 20.7 %copy-start = (f32[4,256,256]{1,2,0:T(8,128)}, f32[4,256,256]{1,2,0:T(8,128)S(1)}, u32[]{:S(2)}) copy-start(f32[4,256,256]{1,2,0:T(8,128)S(1)} %pad_add_fusion) | copy-start | bytes 3145732
  72.6 24.8 %copy-start.10 = (bf16[2,256,2,128]{3,1,0,2:T(8,128)(2,1)S(1)}, bf16[2,256,2,128]{3,1,0,2:T(8,128)(2,1)}, u32[]{:S(2)}) copy-start(bf16[2,256,2,128]{3,1,0,2:T(8,128)(2,1)} %copy.146) | copy-start | bytes 786436
  72.6 24.8 %copy-start.12 = (bf16[2,256,2,128]{3,1,0,2:T(8,128)(2,1)S(1)}, bf16[2,256,2,128]{3,1,0,2:T(8,128)(2,1)}, u32[]{:S(2)}) copy-start(bf16[2,256,2,128]{3,1,0,2:T(8,128)(2,1)} %copy-done.11) | copy-start | bytes 786436
  75.1 16.6 %collective-permute-start.11 = (bf16[2,256,256]{1,2,0:T(8,128)(2,1)S(1)}, bf16[2,256,256]{1,2,0:T(8,128)(2,1)S(1)}, u32[]{:S(2)}, u32[]{:S(2)}) collective-permute-start(bf16[2,256,256]{1,2,0:T(8,128)(2,1)S(1)} %fusion.30), channel_id=1, source_target_pairs={{96,0},{224,128},{352,256},{480,384},{97,1},{225,129},{353,257},{4... | collective-permute-start | bytes 786440 | tf_op jit(solution)/shard_map/ppermute | solution.py:67
  76.4 15.9 %collective-permute-start.10 = (bf16[2,256,256]{1,2,0:T(8,128)(2,1)S(1)}, bf16[2,256,256]{1,2,0:T(8,128)(2,1)S(1)}, u32[]{:S(2)}, u32[]{:S(2)}) collective-permute-start(bf16[2,256,256]{1,2,0:T(8,128)(2,1)S(1)} %fusion.30), channel_id=1, source_target_pairs={{64,0},{192,128},{320,256},{448,384},{65,1},{193,129},{321,257},{4... | collective-permute-start | bytes 786440 | tf_op jit(solution)/shard_map/ppermute | solution.py:67
  77.7 14.6 %collective-permute-start.9 = (bf16[2,256,256]{1,2,0:T(8,128)(2,1)S(1)}, bf16[2,256,256]{1,2,0:T(8,128)(2,1)S(1)}, u32[]{:S(2)}, u32[]{:S(2)}) collective-permute-start(bf16[2,256,256]{1,2,0:T(8,128)(2,1)S(1)} %fusion.30), channel_id=1, source_target_pairs={{32,0},{160,128},{288,256},{416,384},{33,1},{161,129},{289,257},{4... | collective-permute-start | bytes 786440 | tf_op jit(solution)/shard_map/ppermute | solution.py:67
  80.1 35.0 %collective-permute-start.7 = (f32[2,2,256,256]{2,3,1,0:T(8,128)}, f32[2,2,256,256]{2,3,1,0:T(8,128)}, u32[]{:S(2)}, u32[]{:S(2)}) collective-permute-start(f32[2,2,256,256]{2,3,1,0:T(8,128)} %pad_maximum_fusion), channel_id=1, source_target_pairs={{16,0},{32,16},{48,32},{64,48},{80,64},{96,80},{112,96},{128,112},... | collective-permute-start | bytes 3145736 | tf_op jit(solution)/shard_map/ppermute | solution.py:19
  93.2 20.3 %collective-permute-start.14 = (bf16[2,256,256]{1,2,0:T(8,128)(2,1)}, bf16[2,256,256]{1,2,0:T(8,128)(2,1)}, u32[]{:S(2)}, u32[]{:S(2)}) collective-permute-start(bf16[2,256,256]{1,2,0:T(8,128)(2,1)} %fusion.79), channel_id=1, source_target_pairs={{384,0},{385,1},{386,2},{387,3},{388,4},{389,5},{390,6},{391,7},{3... | collective-permute-start | bytes 786440 | tf_op jit(solution)/shard_map/ppermute | solution.py:67
  94.6 18.9 %collective-permute-start.13 = (bf16[2,256,256]{1,2,0:T(8,128)(2,1)}, bf16[2,256,256]{1,2,0:T(8,128)(2,1)}, u32[]{:S(2)}, u32[]{:S(2)}) collective-permute-start(bf16[2,256,256]{1,2,0:T(8,128)(2,1)} %fusion.79), channel_id=1, source_target_pairs={{256,0},{257,1},{258,2},{259,3},{260,4},{261,5},{262,6},{263,7},{2... | collective-permute-start | bytes 786440 | tf_op jit(solution)/shard_map/ppermute | solution.py:67
  95.9 17.6 %collective-permute-start.12 = (bf16[2,256,256]{1,2,0:T(8,128)(2,1)}, bf16[2,256,256]{1,2,0:T(8,128)(2,1)}, u32[]{:S(2)}, u32[]{:S(2)}) collective-permute-start(bf16[2,256,256]{1,2,0:T(8,128)(2,1)} %fusion.79), channel_id=1, source_target_pairs={{128,0},{129,1},{130,2},{131,3},{132,4},{133,5},{134,6},{135,7},{1... | collective-permute-start | bytes 786440 | tf_op jit(solution)/shard_map/ppermute | solution.py:67
  117.5 16.5 %all-to-all-start.1 = ((f32[16,2,512]{2,1,0:T(2,128)}), f32[16,2,512]{2,1,0:T(2,128)S(1)}, u32[]{:S(2)}, u32[]{:S(2)}) async-start(f32[16,2,512]{2,1,0:T(2,128)} %broadcast_in_dim.103), calls=%async_computation.1 | async-start | bytes 131072 | tf_op jit(solution)/shard_map/all_to_all | solution.py:25
  (15 other events, 108.9 us)

commit v9 on v8

--- a/solution.py
+++ b/solution.py
@@ -192,7 +192,8 @@
     grad_v_near = fold_offsets(from_heads(grad_vh), F_DEV, F_DEV, CAP)
     grad_k_anchor = grad_ka.transpose(1, 0, 2).reshape(CAP, local_width)
     grad_v_anchor = grad_va.transpose(1, 0, 2).reshape(CAP, local_width)
-    back_k, back_v = shifted(jnp.stack([grad_k_near[:F_DEV], grad_v_near[:F_DEV]]), "seq", -1)
+    back = jnp.stack([grad_k_near[:F_DEV], grad_v_near[:F_DEV]]).astype(jnp.bfloat16)
+    back_k, back_v = shifted(back, "seq", -1).astype(jnp.float32)
     grad_k_own = grad_k_near[F_DEV:] + back_k
     grad_v_own = grad_v_near[F_DEV:] + back_v
     anchor_gk, anchor_gv = tree_reduce(jnp.stack([grad_k_anchor, grad_v_anchor]), "seq", jnp.bfloat16)

time: 137 us -> 141 us (1.029)
  waiting for transfers between devices: 53.4 us -> 57.6 us
  local copies, waits for them, and re-layouts: 14.9 us -> 17.9 us
  other arithmetic: 14.4 us -> 11.9 us
    ppermute x7, waiting for transfers between devices: 26.2 us -> 28.7 us  [tree_reduce(): arrived = lax.ppermute(sent, axis, route)]
    unnamed x51 -> x45, local copies, waits for them, and re-layouts: 5.89 us -> 7.71 us
  transfers between devices with their start and end apart: 17 -> 17, of which waited for: 11 -> 11; matrix products, arithmetic and copies ran while one was open for 14% -> 13% of each run, Pallas kernels for 0% -> 0%
where the time goes in v9:
time: 141 us
  waiting for transfers between devices  57.6 us (41%)
  starting transfers between devices  43.5 us (31%)
  local copies, waits for them, and re-layouts  17.9 us (13%)
  other arithmetic  11.9 us (8%)
  matrix products  8.22 us (6%)
  between operations  1.49 us (1%)
    ppermute x7, waiting for transfers between devices, tree_reduce(): arrived = lax.ppermute(sent, axis, route)  28.7 us
    all_to_all x2, starting transfers between devices, gather_sum(): return jnp.sum(lax.all_to_all(copies, axis, 0, 0, tiled=False), axis=0)  20.8 us
    all_to_all x2, waiting for transfers between devices, gather_sum(): return jnp.sum(lax.all_to_all(copies, axis, 0, 0, tiled=False), axis=0)  18.6 us
    ppermute x6, starting transfers between devices, tree_bcast(): arrived = lax.ppermute(values, axis, route)  10.8 us
    ppermute x6, waiting for transfers between devices, tree_bcast(): arrived = lax.ppermute(values, axis, route)  10.3 us
    ppermute x7, starting transfers between devices, tree_reduce(): arrived = lax.ppermute(sent, axis, route)  9.21 us
    unnamed x45, local copies, waits for them, and re-layouts  7.71 us
  transfers between devices with their start and end apart: 17, of which 11 were waited for; matrix products, arithmetic and copies ran while one was open for 13% of the time, Pallas kernels for 0%

profile of v9, /device:TPU:8, one launch (start us, length us, event | category | flops | bytes accessed | tf_op | source)
XLA Modules:
  0.0 140.5 jit_solution(5884114679470474048)
XLA Ops:
  3.7 16.0 %all-to-all-start = ((f32[16,2,512]{2,1,0:T(2,128)}), f32[16,2,512]{2,1,0:T(2,128)S(1)}, u32[]{:S(2)}, u32[]{:S(2)}) async-start(f32[16,2,512]{2,1,0:T(2,128)} %broadcast_in_dim.58), calls=%async_computation | async-start | bytes 131072 | tf_op jit(solution)/shard_map/all_to_all | solution.py:25
  22.4 8.9 %all-to-all-done = f32[16,2,512]{2,1,0:T(2,128)S(1)} async-done(((f32[16,2,512]{2,1,0:T(2,128)}), f32[16,2,512]{2,1,0:T(2,128)S(1)}, u32[]{:S(2)}, u32[]{:S(2)}) %all-to-all-start) | async-done | bytes 65568 | tf_op jit(solution)/shard_map/all_to_all | solution.py:25
  32.2 3.4 %collective-permute-start.2 = (bf16[2,256,256]{1,2,0:T(8,128)(2,1)S(1)}, bf16[2,256,256]{1,2,0:T(8,128)(2,1)S(1)}, u32[]{:S(2)}, u32[]{:S(2)}) collective-permute-start(bf16[2,256,256]{1,2,0:T(8,128)(2,1)S(1)} %pad_maximum_fusion.5), channel_id=1, source_target_pairs={{0,128},{1,129},{2,130},{3,131},{4,132},{5,133},{6,134},{7,135},{8... | collective-permute-start | bytes 786440 | tf_op jit(solution)/shard_map/ppermute | solution.py:52
  35.7 2.2 %collective-permute-start.1 = (bf16[2,256,256]{1,2,0:T(8,128)(2,1)S(1)}, bf16[2,256,256]{1,2,0:T(8,128)(2,1)S(1)}, u32[]{:S(2)}, u32[]{:S(2)}) collective-permute-start(bf16[2,256,256]{1,2,0:T(8,128)(2,1)S(1)} %pad_maximum_fusion.5), channel_id=1, source_target_pairs={{0,256},{1,257},{2,258},{3,259},{4,260},{5,261},{6,262},{7,263},{8... | collective-permute-start | bytes 786440 | tf_op jit(solution)/shard_map/ppermute | solution.py:52
  37.9 1.3 collective-permute-start
  39.5 2.8 %collective-permute-done.1 = bf16[2,256,256]{1,2,0:T(8,128)(2,1)S(1)} collective-permute-done((bf16[2,256,256]{1,2,0:T(8,128)(2,1)S(1)}, bf16[2,256,256]{1,2,0:T(8,128)(2,1)S(1)}, u32[]{:S(2)}, u32[]{:S(2)}) %collective-permute-start.1) | collective-permute-done | bytes 262176 | tf_op jit(solution)/shard_map/ppermute | solution.py:52
  43.1 1.3 collective-permute-start.5
  44.4 1.3 collective-permute-start.4
  45.7 1.3 collective-permute-start.3
  48.3 2.8 %collective-permute-done.4 = bf16[2,256,256]{1,2,0:T(8,128)(2,1)S(1)} collective-permute-done((bf16[2,256,256]{1,2,0:T(8,128)(2,1)S(1)}, bf16[2,256,256]{1,2,0:T(8,128)(2,1)S(1)}, u32[]{:S(2)}, u32[]{:S(2)}) %collective-permute-start.4) | collective-permute-done | bytes 262176 | tf_op jit(solution)/shard_map/ppermute | solution.py:52
  51.1 2.8 %collective-permute-done.3 = bf16[2,256,256]{1,2,0:T(8,128)(2,1)S(1)} collective-permute-done((bf16[2,256,256]{1,2,0:T(8,128)(2,1)S(1)}, bf16[2,256,256]{1,2,0:T(8,128)(2,1)S(1)}, u32[]{:S(2)}, u32[]{:S(2)}) %collective-permute-start.3) | collective-permute-done | bytes 262176 | tf_op jit(solution)/shard_map/ppermute | solution.py:52
  54.9 1.3 collective-permute-start.6
  69.8 1.3 collective-permute-start.8
  74.9 1.3 collective-permute-done.8
  78.2 1.3 collective-permute-start.10
  79.5 1.5 %collective-permute-start.9 = (bf16[2,256,256]{1,2,0:T(8,128)(2,1)}, bf16[2,256,256]{1,2,0:T(8,128)(2,1)}, u32[]{:S(2)}, u32[]{:S(2)}) collective-permute-start(bf16[2,256,256]{1,2,0:T(8,128)(2,1)} %fusion.30), channel_id=1, source_target_pairs={{32,0},{160,128},{288,256},{416,384},{33,1},{161,129},{289,257},{4... | collective-permute-start | bytes 786440 | tf_op jit(solution)/shard_map/ppermute | solution.py:67
  81.0 1.4 fusion.6
  82.4 2.0 %copy.204 = f32[2,256,2,128]{1,0,3,2:T(2,128)} copy(f32[2,256,2,128]{3,1,0,2:T(8,128)} %fusion.6) | data formatting | bytes 1048576 | tf_op jit(solution)/shard_map/reshape;reshape | solution.py:190
  85.8 13.4 %collective-permute-done.11 = bf16[2,256,256]{1,2,0:T(8,128)(2,1)} collective-permute-done((bf16[2,256,256]{1,2,0:T(8,128)(2,1)}, bf16[2,256,256]{1,2,0:T(8,128)(2,1)}, u32[]{:S(2)}, u32[]{:S(2)}) %collective-permute-start.11) | collective-permute-done | bytes 262176 | tf_op jit(solution)/shard_map/ppermute | solution.py:67
  100.4 1.3 collective-permute-start.14
  105.7 14.0 %collective-permute-done.14 = bf16[2,256,256]{1,2,0:T(8,128)(2,1)S(1)} collective-permute-done((bf16[2,256,256]{1,2,0:T(8,128)(2,1)S(1)}, bf16[2,256,256]{1,2,0:T(8,128)(2,1)S(1)}, u32[]{:S(2)}, u32[]{:S(2)}) %collective-permute-start.14) | collective-permute-done | bytes 262176 | tf_op jit(solution)/shard_map/ppermute | solution.py:67
  119.6 1.4 convert_add_fusion
  122.0 4.8 %all-to-all-start.1 = ((f32[16,2,512]{2,1,0:T(2,128)}), f32[16,2,512]{2,1,0:T(2,128)S(1)}, u32[]{:S(2)}, u32[]{:S(2)}) async-start(f32[16,2,512]{2,1,0:T(2,128)} %broadcast_in_dim.103), calls=%async_computation.1 | async-start | bytes 131072 | tf_op jit(solution)/shard_map/all_to_all | solution.py:25
  128.8 9.7 %all-to-all-done.1 = f32[16,2,512]{2,1,0:T(2,128)S(1)} async-done(((f32[16,2,512]{2,1,0:T(2,128)}), f32[16,2,512]{2,1,0:T(2,128)S(1)}, u32[]{:S(2)}, u32[]{:S(2)}) %all-to-all-start.1) | async-done | bytes 65568 | tf_op jit(solution)/shard_map/all_to_all | solution.py:25
  (150 shorter events, 40.2 us)
Async XLA Ops:
  0.6 46.4 %copy-start.18 = (s32[64]{0:T(128)S(1)}, s32[64]{0:T(128)}, u32[]{:S(2)}) copy-start(s32[64]{0:T(128)} %param.18) | copy-start | bytes 772
  0.6 38.5 %copy-start.17 = (s32[2]{0:T(128)S(1)}, s32[2]{0:T(128)}, u32[]{:S(2)}) copy-start(s32[2]{0:T(128)} %param.19) | copy-start | bytes 28
  0.7 46.5 %copy-start.14 = (f32[256]{0:T(256)S(1)}, f32[256]{0:T(256)}, u32[]{:S(2)}) copy-start(f32[256]{0:T(256)} %param.16) | copy-start | bytes 3076
  0.7 38.6 %copy-start.6 = (bf16[512,256]{1,0:T(8,128)(2,1)S(1)}, bf16[512,256]{1,0:T(8,128)(2,1)}, u32[]{:S(2)}) copy-start(bf16[512,256]{1,0:T(8,128)(2,1)} %param.17) | copy-start | bytes 786436
  3.7 27.6 %all-to-all-start = ((f32[16,2,512]{2,1,0:T(2,128)}), f32[16,2,512]{2,1,0:T(2,128)S(1)}, u32[]{:S(2)}, u32[]{:S(2)}) async-start(f32[16,2,512]{2,1,0:T(2,128)} %broadcast_in_dim.58), calls=%async_computation | async-start | bytes 131072 | tf_op jit(solution)/shard_map/all_to_all | solution.py:25
  32.2 24.1 %copy-start.2 = (bf16[512,256]{1,0:T(8,128)(2,1)S(1)}, bf16[512,256]{1,0:T(8,128)(2,1)}, u32[]{:S(2)}) copy-start(bf16[512,256]{1,0:T(8,128)(2,1)} %param.14) | copy-start | bytes 786436
  32.2 7.3 %collective-permute-start.2 = (bf16[2,256,256]{1,2,0:T(8,128)(2,1)S(1)}, bf16[2,256,256]{1,2,0:T(8,128)(2,1)S(1)}, u32[]{:S(2)}, u32[]{:S(2)}) collective-permute-start(bf16[2,256,256]{1,2,0:T(8,128)(2,1)S(1)} %pad_maximum_fusion.5), channel_id=1, source_target_pairs={{0,128},{1,129},{2,130},{3,131},{4,132},{5,133},{6,134},{7,135},{8... | collective-permute-start | bytes 786440 | tf_op jit(solution)/shard_map/ppermute | solution.py:52
  35.7 6.7 %collective-permute-start.1 = (bf16[2,256,256]{1,2,0:T(8,128)(2,1)S(1)}, bf16[2,256,256]{1,2,0:T(8,128)(2,1)S(1)}, u32[]{:S(2)}, u32[]{:S(2)}) collective-permute-start(bf16[2,256,256]{1,2,0:T(8,128)(2,1)S(1)} %pad_maximum_fusion.5), channel_id=1, source_target_pairs={{0,256},{1,257},{2,258},{3,259},{4,260},{5,261},{6,262},{7,263},{8... | collective-permute-start | bytes 786440 | tf_op jit(solution)/shard_map/ppermute | solution.py:52
  37.9 5.2 %collective-permute-start = (bf16[2,256,256]{1,2,0:T(8,128)(2,1)S(1)}, bf16[2,256,256]{1,2,0:T(8,128)(2,1)S(1)}, u32[]{:S(2)}, u32[]{:S(2)}) collective-permute-start(bf16[2,256,256]{1,2,0:T(8,128)(2,1)S(1)} %pad_maximum_fusion.5), channel_id=1, source_target_pairs={{0,384},{1,385},{2,386},{3,387},{4,388},{5,389},{6,390},{7,391},{8... | collective-permute-start | bytes 786440 | tf_op jit(solution)/shard_map/ppermute | solution.py:52
  43.1 5.2 %collective-permute-start.5 = (bf16[2,256,256]{1,2,0:T(8,128)(2,1)S(1)}, bf16[2,256,256]{1,2,0:T(8,128)(2,1)S(1)}, u32[]{:S(2)}, u32[]{:S(2)}) collective-permute-start(bf16[2,256,256]{1,2,0:T(8,128)(2,1)S(1)} %select_select_fusion.1), channel_id=1, source_target_pairs={{0,32},{128,160},{256,288},{384,416},{1,33},{129,161},{257,289},{3... | collective-permute-start | bytes 786440 | tf_op jit(solution)/shard_map/ppermute | solution.py:52
  44.4 6.7 %collective-permute-start.4 = (bf16[2,256,256]{1,2,0:T(8,128)(2,1)S(1)}, bf16[2,256,256]{1,2,0:T(8,128)(2,1)S(1)}, u32[]{:S(2)}, u32[]{:S(2)}) collective-permute-start(bf16[2,256,256]{1,2,0:T(8,128)(2,1)S(1)} %select_select_fusion.1), channel_id=1, source_target_pairs={{0,64},{128,192},{256,320},{384,448},{1,65},{129,193},{257,321},{3... | collective-permute-start | bytes 786440 | tf_op jit(solution)/shard_map/ppermute | solution.py:52
  45.7 8.2 %collective-permute-start.3 = (bf16[2,256,256]{1,2,0:T(8,128)(2,1)S(1)}, bf16[2,256,256]{1,2,0:T(8,128)(2,1)S(1)}, u32[]{:S(2)}, u32[]{:S(2)}) collective-permute-start(bf16[2,256,256]{1,2,0:T(8,128)(2,1)S(1)} %select_select_fusion.1), channel_id=1, source_target_pairs={{0,96},{128,224},{256,352},{384,480},{1,97},{129,225},{257,353},{3... | collective-permute-start | bytes 786440 | tf_op jit(solution)/shard_map/ppermute | solution.py:52
  54.9 4.0 %collective-permute-start.6 = (bf16[2,768,256]{1,2,0:T(8,128)(2,1)}, bf16[2,768,256]{1,2,0:T(8,128)(2,1)S(1)}, u32[]{:S(2)}, u32[]{:S(2)}) collective-permute-start(bf16[2,768,256]{1,2,0:T(8,128)(2,1)} %pad_maximum_fusion), channel_id=1, source_target_pairs={{0,16},{16,32},{32,48},{48,64},{64,80},{80,96},{96,112},{112,128},... | collective-permute-start | bytes 2359304 | tf_op jit(solution)/shard_map/ppermute | solution.py:19
  69.8 6.4 %collective-permute-start.8 = (bf16[2,256,256]{1,2,0:T(8,128)(2,1)S(1)}, bf16[2,256,256]{1,2,0:T(8,128)(2,1)S(1)}, u32[]{:S(2)}, u32[]{:S(2)}) collective-permute-start(bf16[2,256,256]{1,2,0:T(8,128)(2,1)S(1)} %fusion.28), channel_id=1, source_target_pairs={{16,0},{48,32},{80,64},{112,96},{144,128},{176,160},{208,192},{240... | collective-permute-start | bytes 786440 | tf_op jit(solution)/shard_map/ppermute | solution.py:67
  73.2 31.1 %collective-permute-start.7 = (bf16[2,2,256,256]{2,3,1,0:T(8,128)(2,1)}, bf16[2,2,256,256]{2,3,1,0:T(8,128)(2,1)}, u32[]{:S(2)}, u32[]{:S(2)}) collective-permute-start(bf16[2,2,256,256]{2,3,1,0:T(8,128)(2,1)} %pad_maximum_fusion.1), channel_id=1, source_target_pairs={{16,0},{32,16},{48,32},{64,48},{80,64},{96,80},{112,96},{128,112},... | collective-permute-start | bytes 1572872 | tf_op jit(solution)/shard_map/ppermute | solution.py:19
  76.9 22.2 %collective-permute-start.11 = (bf16[2,256,256]{1,2,0:T(8,128)(2,1)}, bf16[2,256,256]{1,2,0:T(8,128)(2,1)}, u32[]{:S(2)}, u32[]{:S(2)}) collective-permute-start(bf16[2,256,256]{1,2,0:T(8,128)(2,1)} %fusion.30), channel_id=1, source_target_pairs={{96,0},{224,128},{352,256},{480,384},{97,1},{225,129},{353,257},{4... | collective-permute-start | bytes 786440 | tf_op jit(solution)/shard_map/ppermute | solution.py:67
  78.2 21.0 %collective-permute-start.10 = (bf16[2,256,256]{1,2,0:T(8,128)(2,1)}, bf16[2,256,256]{1,2,0:T(8,128)(2,1)}, u32[]{:S(2)}, u32[]{:S(2)}) collective-permute-start(bf16[2,256,256]{1,2,0:T(8,128)(2,1)} %fusion.30), channel_id=1, source_target_pairs={{64,0},{192,128},{320,256},{448,384},{65,1},{193,129},{321,257},{4... | collective-permute-start | bytes 786440 | tf_op jit(solution)/shard_map/ppermute | solution.py:67
  79.5 19.7 %collective-permute-start.9 = (bf16[2,256,256]{1,2,0:T(8,128)(2,1)}, bf16[2,256,256]{1,2,0:T(8,128)(2,1)}, u32[]{:S(2)}, u32[]{:S(2)}) collective-permute-start(bf16[2,256,256]{1,2,0:T(8,128)(2,1)} %fusion.30), channel_id=1, source_target_pairs={{32,0},{160,128},{288,256},{416,384},{33,1},{161,129},{289,257},{4... | collective-permute-start | bytes 786440 | tf_op jit(solution)/shard_map/ppermute | solution.py:67
  84.5 21.0 %copy-start.1 = (f32[4,256,256]{1,2,0:T(8,128)S(1)}, f32[4,256,256]{1,2,0:T(8,128)}, u32[]{:S(2)}) copy-start(f32[4,256,256]{1,2,0:T(8,128)} %copy-done) | copy-start | bytes 3145732
  100.4 19.2 %collective-permute-start.14 = (bf16[2,256,256]{1,2,0:T(8,128)(2,1)S(1)}, bf16[2,256,256]{1,2,0:T(8,128)(2,1)S(1)}, u32[]{:S(2)}, u32[]{:S(2)}) collective-permute-start(bf16[2,256,256]{1,2,0:T(8,128)(2,1)S(1)} %fusion.81), channel_id=1, source_target_pairs={{384,0},{385,1},{386,2},{387,3},{388,4},{389,5},{390,6},{391,7},{3... | collective-permute-start | bytes 786440 | tf_op jit(solution)/shard_map/ppermute | solution.py:67
  101.7 17.9 %collective-permute-start.13 = (bf16[2,256,256]{1,2,0:T(8,128)(2,1)S(1)}, bf16[2,256,256]{1,2,0:T(8,128)(2,1)S(1)}, u32[]{:S(2)}, u32[]{:S(2)}) collective-permute-start(bf16[2,256,256]{1,2,0:T(8,128)(2,1)S(1)} %fusion.81), channel_id=1, source_target_pairs={{256,0},{257,1},{258,2},{259,3},{260,4},{261,5},{262,6},{263,7},{2... | collective-permute-start | bytes 786440 | tf_op jit(solution)/shard_map/ppermute | solution.py:67
  103.0 16.6 %collective-permute-start.12 = (bf16[2,256,256]{1,2,0:T(8,128)(2,1)S(1)}, bf16[2,256,256]{1,2,0:T(8,128)(2,1)S(1)}, u32[]{:S(2)}, u32[]{:S(2)}) collective-permute-start(bf16[2,256,256]{1,2,0:T(8,128)(2,1)S(1)} %fusion.81), channel_id=1, source_target_pairs={{128,0},{129,1},{130,2},{131,3},{132,4},{133,5},{134,6},{135,7},{1... | collective-permute-start | bytes 786440 | tf_op jit(solution)/shard_map/ppermute | solution.py:67
  105.6 21.2 %copy-start.4 = (bf16[2,2,256,128]{3,2,1,0:T(8,128)(2,1)S(1)}, bf16[2,2,256,128]{3,2,1,0:T(8,128)(2,1)}, u32[]{:S(2)}) copy-start(bf16[2,2,256,128]{3,2,1,0:T(8,128)(2,1)} %copy-done.3) | copy-start | bytes 786436
  122.0 16.5 %all-to-all-start.1 = ((f32[16,2,512]{2,1,0:T(2,128)}), f32[16,2,512]{2,1,0:T(2,128)S(1)}, u32[]{:S(2)}, u32[]{:S(2)}) async-start(f32[16,2,512]{2,1,0:T(2,128)} %broadcast_in_dim.103), calls=%async_computation.1 | async-start | bytes 131072 | tf_op jit(solution)/shard_map/all_to_all | solution.py:25
  (12 other events, 79.5 us)

commit v10 on v8

--- a/solution.py
+++ b/solution.py
@@ -127,9 +127,10 @@
     local_heads = local_width // HD
     device = lax.axis_index("seq")
     q_float = q_in.astype(jnp.float32)
+    q_raw, k_raw = (x.astype(jnp.float32) for x in lax.optimization_barrier((q_in, k_in)))
     k_float = k_in.astype(jnp.float32)
     q_power, k_power = gather_sum(
-        jnp.stack([jnp.sum(q_float * q_float, axis=1), jnp.sum(k_float * k_float, axis=1)]), "tp"
+        jnp.stack([jnp.sum(q_raw * q_raw, axis=1), jnp.sum(k_raw * k_raw, axis=1)]), "tp"
     )
     q_rinv = lax.rsqrt(q_power / WIDTH + EPS)[:, None]
     k_rinv = lax.rsqrt(k_power / WIDTH + EPS)[:, None]

time: 137 us -> 135 us (0.985)
  other arithmetic: 14.4 us -> 12.5 us
  waiting for transfers between devices: 53.4 us -> 55.2 us
  local copies, waits for them, and re-layouts: 14.9 us -> 13.2 us
    unnamed x51 -> x47, local copies, waits for them, and re-layouts: 5.89 us -> 4.89 us
  transfers between devices with their start and end apart: 17 -> 17, of which waited for: 11 -> 12; matrix products, arithmetic and copies ran while one was open for 14% -> 12% of each run, Pallas kernels for 0% -> 0%
where the time goes in v10:
time: 135 us; the launch traced here: 134 us
  waiting for transfers between devices  55.2 us (41%)
  starting transfers between devices  43.6 us (32%)
  local copies, waits for them, and re-layouts  13.2 us (10%)
  other arithmetic  12.5 us (9%)
  matrix products  8.2 us (6%)
  between operations  1.53 us (1%)
    ppermute x7, waiting for transfers between devices, tree_reduce(): arrived = lax.ppermute(sent, axis, route)  27.4 us
    all_to_all x2, starting transfers between devices, gather_sum(): return jnp.sum(lax.all_to_all(copies, axis, 0, 0, tiled=False), axis=0)  20.8 us
    all_to_all x2, waiting for transfers between devices, gather_sum(): return jnp.sum(lax.all_to_all(copies, axis, 0, 0, tiled=False), axis=0)  17.5 us
    ppermute x6, starting transfers between devices, tree_bcast(): arrived = lax.ppermute(values, axis, route)  11 us
    ppermute x6, waiting for transfers between devices, tree_bcast(): arrived = lax.ppermute(values, axis, route)  10.3 us
    ppermute x7, starting transfers between devices, tree_reduce(): arrived = lax.ppermute(sent, axis, route)  9.21 us
    unnamed x47, local copies, waits for them, and re-layouts  4.89 us
    concatenate x12, local copies, waits for them, and re-layouts, stack_offsets(): return jnp.concatenate(blocks, axis=1)  2.77 us
  transfers between devices with their start and end apart: 17, of which 12 were waited for; matrix products, arithmetic and copies ran while one was open for 12% of the time, Pallas kernels for 0%

profile of v10, /device:TPU:8, one launch (start us, length us, event | category | flops | bytes accessed | tf_op | source)
XLA Modules:
  0.0 134.2 jit_solution(14250409840196132326)
XLA Ops:
  2.6 16.0 %all-to-all-start = ((f32[16,2,512]{2,1,0:T(2,128)}), f32[16,2,512]{2,1,0:T(2,128)S(1)}, u32[]{:S(2)}, u32[]{:S(2)}) async-start(f32[16,2,512]{2,1,0:T(2,128)} %broadcast_in_dim.58), calls=%async_computation | async-start | bytes 131072 | tf_op jit(solution)/shard_map/all_to_all | solution.py:25
  22.4 7.8 %all-to-all-done = f32[16,2,512]{2,1,0:T(2,128)S(1)} async-done(((f32[16,2,512]{2,1,0:T(2,128)}), f32[16,2,512]{2,1,0:T(2,128)S(1)}, u32[]{:S(2)}, u32[]{:S(2)}) %all-to-all-start) | async-done | bytes 65568 | tf_op jit(solution)/shard_map/all_to_all | solution.py:25
  31.1 3.5 %collective-permute-start.2 = (bf16[2,256,256]{1,2,0:T(8,128)(2,1)S(1)}, bf16[2,256,256]{1,2,0:T(8,128)(2,1)S(1)}, u32[]{:S(2)}, u32[]{:S(2)}) collective-permute-start(bf16[2,256,256]{1,2,0:T(8,128)(2,1)S(1)} %pad_maximum_fusion.5), channel_id=1, source_target_pairs={{0,128},{1,129},{2,130},{3,131},{4,132},{5,133},{6,134},{7,135},{8... | collective-permute-start | bytes 786440 | tf_op jit(solution)/shard_map/ppermute | solution.py:52
  34.7 2.2 %collective-permute-start.1 = (bf16[2,256,256]{1,2,0:T(8,128)(2,1)S(1)}, bf16[2,256,256]{1,2,0:T(8,128)(2,1)S(1)}, u32[]{:S(2)}, u32[]{:S(2)}) collective-permute-start(bf16[2,256,256]{1,2,0:T(8,128)(2,1)S(1)} %pad_maximum_fusion.5), channel_id=1, source_target_pairs={{0,256},{1,257},{2,258},{3,259},{4,260},{5,261},{6,262},{7,263},{8... | collective-permute-start | bytes 786440 | tf_op jit(solution)/shard_map/ppermute | solution.py:52
  36.9 1.3 collective-permute-start
  38.5 2.8 %collective-permute-done.1 = bf16[2,256,256]{1,2,0:T(8,128)(2,1)S(1)} collective-permute-done((bf16[2,256,256]{1,2,0:T(8,128)(2,1)S(1)}, bf16[2,256,256]{1,2,0:T(8,128)(2,1)S(1)}, u32[]{:S(2)}, u32[]{:S(2)}) %collective-permute-start.1) | collective-permute-done | bytes 262176 | tf_op jit(solution)/shard_map/ppermute | solution.py:52
  42.1 1.3 collective-permute-start.5
  43.5 1.3 collective-permute-start.4
  44.8 1.3 collective-permute-start.3
  47.3 2.8 %collective-permute-done.4 = bf16[2,256,256]{1,2,0:T(8,128)(2,1)S(1)} collective-permute-done((bf16[2,256,256]{1,2,0:T(8,128)(2,1)S(1)}, bf16[2,256,256]{1,2,0:T(8,128)(2,1)S(1)}, u32[]{:S(2)}, u32[]{:S(2)}) %collective-permute-start.4) | collective-permute-done | bytes 262176 | tf_op jit(solution)/shard_map/ppermute | solution.py:52
  50.1 2.8 %collective-permute-done.3 = bf16[2,256,256]{1,2,0:T(8,128)(2,1)S(1)} collective-permute-done((bf16[2,256,256]{1,2,0:T(8,128)(2,1)S(1)}, bf16[2,256,256]{1,2,0:T(8,128)(2,1)S(1)}, u32[]{:S(2)}, u32[]{:S(2)}) %collective-permute-start.3) | collective-permute-done | bytes 262176 | tf_op jit(solution)/shard_map/ppermute | solution.py:52
  53.9 1.3 collective-permute-start.6
  67.2 1.3 collective-permute-start.8
  69.8 3.7 %collective-permute-done.8 = bf16[2,256,256]{1,2,0:T(8,128)(2,1)S(1)} collective-permute-done((bf16[2,256,256]{1,2,0:T(8,128)(2,1)S(1)}, bf16[2,256,256]{1,2,0:T(8,128)(2,1)S(1)}, u32[]{:S(2)}, u32[]{:S(2)}) %collective-permute-start.8) | collective-permute-done | bytes 262176 | tf_op jit(solution)/shard_map/ppermute | solution.py:67
  73.5 1.3 collective-permute-start.11
  74.8 1.3 collective-permute-start.10
  80.1 10.0 %collective-permute-done.11 = bf16[2,256,256]{1,2,0:T(8,128)(2,1)S(1)} collective-permute-done((bf16[2,256,256]{1,2,0:T(8,128)(2,1)S(1)}, bf16[2,256,256]{1,2,0:T(8,128)(2,1)S(1)}, u32[]{:S(2)}, u32[]{:S(2)}) %collective-permute-start.11) | collective-permute-done | bytes 262176 | tf_op jit(solution)/shard_map/ppermute | solution.py:67
  92.9 1.5 %collective-permute-start.13 = (bf16[2,256,256]{1,2,0:T(8,128)(2,1)}, bf16[2,256,256]{1,2,0:T(8,128)(2,1)}, u32[]{:S(2)}, u32[]{:S(2)}) collective-permute-start(bf16[2,256,256]{1,2,0:T(8,128)(2,1)} %fusion.77), channel_id=1, source_target_pairs={{256,0},{257,1},{258,2},{259,3},{260,4},{261,5},{262,6},{263,7},{2... | collective-permute-start | bytes 786440 | tf_op jit(solution)/shard_map/ppermute | solution.py:67
  95.7 1.4 %fusion.6 = f32[2,256,2,128]{3,1,0,2:T(8,128)} fusion(f32[2,2,256,128]{3,2,1,0:T(8,128)S(1)} %fusion.54, bf16[2,2,256,768]{3,2,1,0:T(8,128)(2,1)S(1)} %multiply_convert_fusion, bf16[2,256,2,128]{3,1,0,2:T(8,128)(2,1)S(1)} %copy-done.13, bf16[2,256,2,128]{3,1,0,2:T(8,128)(2,1)S(1)} %copy.147, bf16[2,256,2,128]{3,1,0,2:T(8,128)(2,1)S(1)} %copy-done.11), kind=kOutput, calls=%fused_computation.15 | convolution fusion | flops 203816960 | bytes 3407872 | tf_op jit(solution)/shard_map/hfqk,hfkd->hfqd/dot_general | solution.py:117
  98.6 13.1 %collective-permute-done.14 = bf16[2,256,256]{1,2,0:T(8,128)(2,1)} collective-permute-done((bf16[2,256,256]{1,2,0:T(8,128)(2,1)}, bf16[2,256,256]{1,2,0:T(8,128)(2,1)}, u32[]{:S(2)}, u32[]{:S(2)}) %collective-permute-start.14) | collective-permute-done | bytes 262176 | tf_op jit(solution)/shard_map/ppermute | solution.py:67
  111.7 1.6 %convert_add_fusion = f32[2,256,256]{1,2,0:T(8,128)S(1)} fusion(bf16[2,256,256]{1,2,0:T(8,128)(2,1)} %collective-permute-done.14, bf16[2,256,256]{1,2,0:T(8,128)(2,1)} %collective-permute-done.13, bf16[2,256,256]{1,2,0:T(8,128)(2,1)} %collective-permute-done.12, bf16[2,256,256]{1,2,0:T(8,128)(2,1)} %copy-done.6, bf16[2,256,256]{1,2,0:T(8,128)(2,1)} %copy-done.7, ...), kind=kLoop, calls=%fused_computation.55 | loop fusion | flops 1966080 | bytes 2883584 | tf_op jit(solution)/shard_map/add | solution.py:68
  113.3 1.4 %fusion.24 = (f32[2,256,256]{1,2,0:T(8,128)S(1)}, f32[2,256,256]{1,2,0:T(8,128)S(1)}) fusion(f32[2,2,256,256]{2,3,1,0:T(8,128)} %collective-permute-done.7, f32[4,256,256]{1,2,0:T(8,128)S(1)} %copy-done.1, f32[4,256,256]{1,2,0:T(8,128)S(1)} %pad_add_fusion.1), kind=kLoop, calls=%fused_computation.49 | loop fusion | flops 262144 | bytes 3145728 | tf_op jit(solution)/shard_map/add | solution.py:198
  115.8 4.8 %all-to-all-start.1 = ((f32[16,2,512]{2,1,0:T(2,128)}), f32[16,2,512]{2,1,0:T(2,128)S(1)}, u32[]{:S(2)}, u32[]{:S(2)}) async-start(f32[16,2,512]{2,1,0:T(2,128)} %broadcast_in_dim.103), calls=%async_computation.1 | async-start | bytes 131072 | tf_op jit(solution)/shard_map/all_to_all | solution.py:25
  122.5 9.7 %all-to-all-done.1 = f32[16,2,512]{2,1,0:T(2,128)S(1)} async-done(((f32[16,2,512]{2,1,0:T(2,128)}), f32[16,2,512]{2,1,0:T(2,128)S(1)}, u32[]{:S(2)}, u32[]{:S(2)}) %all-to-all-start.1) | async-done | bytes 65568 | tf_op jit(solution)/shard_map/all_to_all | solution.py:25
  (151 shorter events, 37.2 us)
Async XLA Ops:
  0.6 45.5 %copy-start.19 = (s32[64]{0:T(128)S(1)}, s32[64]{0:T(128)}, u32[]{:S(2)}) copy-start(s32[64]{0:T(128)} %param.18) | copy-start | bytes 772
  0.6 37.6 %copy-start.18 = (s32[2]{0:T(128)S(1)}, s32[2]{0:T(128)}, u32[]{:S(2)}) copy-start(s32[2]{0:T(128)} %param.19) | copy-start | bytes 28
  0.7 45.5 %copy-start.15 = (f32[256]{0:T(256)S(1)}, f32[256]{0:T(256)}, u32[]{:S(2)}) copy-start(f32[256]{0:T(256)} %param.16) | copy-start | bytes 3076
  0.7 37.7 %copy-start.9 = (bf16[512,256]{1,0:T(8,128)(2,1)S(1)}, bf16[512,256]{1,0:T(8,128)(2,1)}, u32[]{:S(2)}) copy-start(bf16[512,256]{1,0:T(8,128)(2,1)} %param.17) | copy-start | bytes 786436
  2.6 27.6 %all-to-all-start = ((f32[16,2,512]{2,1,0:T(2,128)}), f32[16,2,512]{2,1,0:T(2,128)S(1)}, u32[]{:S(2)}, u32[]{:S(2)}) async-start(f32[16,2,512]{2,1,0:T(2,128)} %broadcast_in_dim.58), calls=%async_computation | async-start | bytes 131072 | tf_op jit(solution)/shard_map/all_to_all | solution.py:25
  31.1 24.4 %copy-start.3 = (bf16[512,256]{1,0:T(8,128)(2,1)S(1)}, bf16[512,256]{1,0:T(8,128)(2,1)}, u32[]{:S(2)}) copy-start(bf16[512,256]{1,0:T(8,128)(2,1)} %param.14) | copy-start | bytes 786436
  31.1 7.4 %collective-permute-start.2 = (bf16[2,256,256]{1,2,0:T(8,128)(2,1)S(1)}, bf16[2,256,256]{1,2,0:T(8,128)(2,1)S(1)}, u32[]{:S(2)}, u32[]{:S(2)}) collective-permute-start(bf16[2,256,256]{1,2,0:T(8,128)(2,1)S(1)} %pad_maximum_fusion.5), channel_id=1, source_target_pairs={{0,128},{1,129},{2,130},{3,131},{4,132},{5,133},{6,134},{7,135},{8... | collective-permute-start | bytes 786440 | tf_op jit(solution)/shard_map/ppermute | solution.py:52
  34.7 6.7 %collective-permute-start.1 = (bf16[2,256,256]{1,2,0:T(8,128)(2,1)S(1)}, bf16[2,256,256]{1,2,0:T(8,128)(2,1)S(1)}, u32[]{:S(2)}, u32[]{:S(2)}) collective-permute-start(bf16[2,256,256]{1,2,0:T(8,128)(2,1)S(1)} %pad_maximum_fusion.5), channel_id=1, source_target_pairs={{0,256},{1,257},{2,258},{3,259},{4,260},{5,261},{6,262},{7,263},{8... | collective-permute-start | bytes 786440 | tf_op jit(solution)/shard_map/ppermute | solution.py:52
  36.9 5.2 %collective-permute-start = (bf16[2,256,256]{1,2,0:T(8,128)(2,1)S(1)}, bf16[2,256,256]{1,2,0:T(8,128)(2,1)S(1)}, u32[]{:S(2)}, u32[]{:S(2)}) collective-permute-start(bf16[2,256,256]{1,2,0:T(8,128)(2,1)S(1)} %pad_maximum_fusion.5), channel_id=1, source_target_pairs={{0,384},{1,385},{2,386},{3,387},{4,388},{5,389},{6,390},{7,391},{8... | collective-permute-start | bytes 786440 | tf_op jit(solution)/shard_map/ppermute | solution.py:52
  42.1 5.2 %collective-permute-start.5 = (bf16[2,256,256]{1,2,0:T(8,128)(2,1)S(1)}, bf16[2,256,256]{1,2,0:T(8,128)(2,1)S(1)}, u32[]{:S(2)}, u32[]{:S(2)}) collective-permute-start(bf16[2,256,256]{1,2,0:T(8,128)(2,1)S(1)} %select_select_fusion.1), channel_id=1, source_target_pairs={{0,32},{128,160},{256,288},{384,416},{1,33},{129,161},{257,289},{3... | collective-permute-start | bytes 786440 | tf_op jit(solution)/shard_map/ppermute | solution.py:52
  43.5 6.7 %collective-permute-start.4 = (bf16[2,256,256]{1,2,0:T(8,128)(2,1)S(1)}, bf16[2,256,256]{1,2,0:T(8,128)(2,1)S(1)}, u32[]{:S(2)}, u32[]{:S(2)}) collective-permute-start(bf16[2,256,256]{1,2,0:T(8,128)(2,1)S(1)} %select_select_fusion.1), channel_id=1, source_target_pairs={{0,64},{128,192},{256,320},{384,448},{1,65},{129,193},{257,321},{3... | collective-permute-start | bytes 786440 | tf_op jit(solution)/shard_map/ppermute | solution.py:52
  44.8 8.2 %collective-permute-start.3 = (bf16[2,256,256]{1,2,0:T(8,128)(2,1)S(1)}, bf16[2,256,256]{1,2,0:T(8,128)(2,1)S(1)}, u32[]{:S(2)}, u32[]{:S(2)}) collective-permute-start(bf16[2,256,256]{1,2,0:T(8,128)(2,1)S(1)} %select_select_fusion.1), channel_id=1, source_target_pairs={{0,96},{128,224},{256,352},{384,480},{1,97},{129,225},{257,353},{3... | collective-permute-start | bytes 786440 | tf_op jit(solution)/shard_map/ppermute | solution.py:52
  53.9 4.2 %collective-permute-start.6 = (bf16[2,768,256]{1,2,0:T(8,128)(2,1)}, bf16[2,768,256]{1,2,0:T(8,128)(2,1)S(1)}, u32[]{:S(2)}, u32[]{:S(2)}) collective-permute-start(bf16[2,768,256]{1,2,0:T(8,128)(2,1)} %pad_maximum_fusion.1), channel_id=1, source_target_pairs={{0,16},{16,32},{32,48},{48,64},{64,80},{80,96},{96,112},{112,128},... | collective-permute-start | bytes 2359304 | tf_op jit(solution)/shard_map/ppermute | solution.py:19
  67.2 6.2 %collective-permute-start.8 = (bf16[2,256,256]{1,2,0:T(8,128)(2,1)S(1)}, bf16[2,256,256]{1,2,0:T(8,128)(2,1)S(1)}, u32[]{:S(2)}, u32[]{:S(2)}) collective-permute-start(bf16[2,256,256]{1,2,0:T(8,128)(2,1)S(1)} %fusion.26), channel_id=1, source_target_pairs={{16,0},{48,32},{80,64},{112,96},{144,128},{176,160},{208,192},{240... | collective-permute-start | bytes 786440 | tf_op jit(solution)/shard_map/ppermute | solution.py:67
  69.8 25.9 %copy-start.11 = (bf16[2,256,2,128]{3,1,0,2:T(8,128)(2,1)S(1)}, bf16[2,256,2,128]{3,1,0,2:T(8,128)(2,1)}, u32[]{:S(2)}) copy-start(bf16[2,256,2,128]{3,1,0,2:T(8,128)(2,1)} %copy.146) | copy-start | bytes 786436
  69.8 25.9 %copy-start.13 = (bf16[2,256,2,128]{3,1,0,2:T(8,128)(2,1)S(1)}, bf16[2,256,2,128]{3,1,0,2:T(8,128)(2,1)}, u32[]{:S(2)}) copy-start(bf16[2,256,2,128]{3,1,0,2:T(8,128)(2,1)} %copy-done.12) | copy-start | bytes 786436
  73.5 16.6 %collective-permute-start.11 = (bf16[2,256,256]{1,2,0:T(8,128)(2,1)S(1)}, bf16[2,256,256]{1,2,0:T(8,128)(2,1)S(1)}, u32[]{:S(2)}, u32[]{:S(2)}) collective-permute-start(bf16[2,256,256]{1,2,0:T(8,128)(2,1)S(1)} %fusion.28), channel_id=1, source_target_pairs={{96,0},{224,128},{352,256},{480,384},{97,1},{225,129},{353,257},{4... | collective-permute-start | bytes 786440 | tf_op jit(solution)/shard_map/ppermute | solution.py:67
  74.8 15.9 %collective-permute-start.10 = (bf16[2,256,256]{1,2,0:T(8,128)(2,1)S(1)}, bf16[2,256,256]{1,2,0:T(8,128)(2,1)S(1)}, u32[]{:S(2)}, u32[]{:S(2)}) collective-permute-start(bf16[2,256,256]{1,2,0:T(8,128)(2,1)S(1)} %fusion.28), channel_id=1, source_target_pairs={{64,0},{192,128},{320,256},{448,384},{65,1},{193,129},{321,257},{4... | collective-permute-start | bytes 786440 | tf_op jit(solution)/shard_map/ppermute | solution.py:67
  76.1 14.6 %collective-permute-start.9 = (bf16[2,256,256]{1,2,0:T(8,128)(2,1)S(1)}, bf16[2,256,256]{1,2,0:T(8,128)(2,1)S(1)}, u32[]{:S(2)}, u32[]{:S(2)}) collective-permute-start(bf16[2,256,256]{1,2,0:T(8,128)(2,1)S(1)} %fusion.28), channel_id=1, source_target_pairs={{32,0},{160,128},{288,256},{416,384},{33,1},{161,129},{289,257},{4... | collective-permute-start | bytes 786440 | tf_op jit(solution)/shard_map/ppermute | solution.py:67
  78.4 34.9 %collective-permute-start.7 = (f32[2,2,256,256]{2,3,1,0:T(8,128)}, f32[2,2,256,256]{2,3,1,0:T(8,128)}, u32[]{:S(2)}, u32[]{:S(2)}) collective-permute-start(f32[2,2,256,256]{2,3,1,0:T(8,128)} %pad_maximum_fusion), channel_id=1, source_target_pairs={{16,0},{32,16},{48,32},{64,48},{80,64},{96,80},{112,96},{128,112},... | collective-permute-start | bytes 3145736 | tf_op jit(solution)/shard_map/ppermute | solution.py:19
  91.6 20.1 %collective-permute-start.14 = (bf16[2,256,256]{1,2,0:T(8,128)(2,1)}, bf16[2,256,256]{1,2,0:T(8,128)(2,1)}, u32[]{:S(2)}, u32[]{:S(2)}) collective-permute-start(bf16[2,256,256]{1,2,0:T(8,128)(2,1)} %fusion.77), channel_id=1, source_target_pairs={{384,0},{385,1},{386,2},{387,3},{388,4},{389,5},{390,6},{391,7},{3... | collective-permute-start | bytes 786440 | tf_op jit(solution)/shard_map/ppermute | solution.py:67
  92.9 18.8 %collective-permute-start.13 = (bf16[2,256,256]{1,2,0:T(8,128)(2,1)}, bf16[2,256,256]{1,2,0:T(8,128)(2,1)}, u32[]{:S(2)}, u32[]{:S(2)}) collective-permute-start(bf16[2,256,256]{1,2,0:T(8,128)(2,1)} %fusion.77), channel_id=1, source_target_pairs={{256,0},{257,1},{258,2},{259,3},{260,4},{261,5},{262,6},{263,7},{2... | collective-permute-start | bytes 786440 | tf_op jit(solution)/shard_map/ppermute | solution.py:67
  94.4 17.4 %collective-permute-start.12 = (bf16[2,256,256]{1,2,0:T(8,128)(2,1)}, bf16[2,256,256]{1,2,0:T(8,128)(2,1)}, u32[]{:S(2)}, u32[]{:S(2)}) collective-permute-start(bf16[2,256,256]{1,2,0:T(8,128)(2,1)} %fusion.77), channel_id=1, source_target_pairs={{128,0},{129,1},{130,2},{131,3},{132,4},{133,5},{134,6},{135,7},{1... | collective-permute-start | bytes 786440 | tf_op jit(solution)/shard_map/ppermute | solution.py:67
  115.8 16.5 %all-to-all-start.1 = ((f32[16,2,512]{2,1,0:T(2,128)}), f32[16,2,512]{2,1,0:T(2,128)S(1)}, u32[]{:S(2)}, u32[]{:S(2)}) async-start(f32[16,2,512]{2,1,0:T(2,128)} %broadcast_in_dim.103), calls=%async_computation.1 | async-start | bytes 131072 | tf_op jit(solution)/shard_map/all_to_all | solution.py:25
  (13 other events, 125.8 us)

commit v11 on v10

--- a/solution.py
+++ b/solution.py
@@ -202,9 +202,8 @@
     grad_v_own = grad_v_own.at[0].add(jnp.where(first_device, anchor_gv, 0.0))
     q_scaled = grad_qn * q_gain
     k_scaled = grad_k_own.reshape(row_count, local_width) * k_gain
-    q_dot, k_dot = gather_sum(
-        jnp.stack([jnp.sum(q_float * q_scaled, axis=1), jnp.sum(k_float * k_scaled, axis=1)]), "tp"
-    )
+    q_dot = gather_sum(jnp.sum(q_float * q_scaled, axis=1)[None], "tp")[0]
+    k_dot = gather_sum(jnp.sum(k_float * k_scaled, axis=1)[None], "tp")[0]
     grad_q = (q_rinv * q_scaled - q_float * q_rinv**3 * q_dot[:, None] / WIDTH).astype(jnp.bfloat16)
     grad_k = (k_rinv * k_scaled - k_float * k_rinv**3 * k_dot[:, None] / WIDTH).astype(jnp.bfloat16)
     grad_v = grad_v_own.reshape(row_count, local_width).astype(jnp.bfloat16)

time: 135 us -> 156 us (1.16)
  the two profiles are of different devices: /device:TPU:8 before, /device:TPU:6 now
where the time goes in v11:
time: 156 us; the launch traced here: 155 us
  waiting for transfers between devices  72.8 us (47%)
  starting transfers between devices  44.5 us (29%)
  other arithmetic  14.7 us (9%)
  local copies, waits for them, and re-layouts  13.8 us (9%)
  matrix products  7.41 us (5%)
  between operations  1.59 us (1%)
    all_to_all x3, waiting for transfers between devices, gather_sum(): return jnp.sum(lax.all_to_all(copies, axis, 0, 0, tiled=False), axis=0)  30 us
    all_to_all x3, starting transfers between devices, gather_sum(): return jnp.sum(lax.all_to_all(copies, axis, 0, 0, tiled=False), axis=0)  22.6 us
    ppermute x7, waiting for transfers between devices, tree_reduce(): arrived = lax.ppermute(sent, axis, route)  16.5 us
    ppermute x6, waiting for transfers between devices, tree_bcast(): arrived = lax.ppermute(values, axis, route)  15.5 us
    ppermute x2, waiting for transfers between devices, shifted(): return lax.ppermute(block, axis, route)  10.9 us
    ppermute x7, starting transfers between devices, tree_reduce(): arrived = lax.ppermute(sent, axis, route)  9.5 us
    ppermute x6, starting transfers between devices, tree_bcast(): arrived = lax.ppermute(values, axis, route)  6.7 us
    ppermute x2, starting transfers between devices, shifted(): return lax.ppermute(block, axis, route)  5.7 us
  transfers between devices with their start and end apart: 18, of which 10 were waited for; matrix products, arithmetic and copies ran while one was open for 13% of the time, Pallas kernels for 0%

profile of v11, /device:TPU:6, one launch (start us, length us, event | category | flops | bytes accessed | tf_op | source)
XLA Modules:
  0.0 154.9 jit_solution(10706473944032466966)
XLA Ops:
  2.6 15.6 %all-to-all-start = ((f32[16,2,512]{2,1,0:T(2,128)}), f32[16,2,512]{2,1,0:T(2,128)S(1)}, u32[]{:S(2)}, u32[]{:S(2)}) async-start(f32[16,2,512]{2,1,0:T(2,128)} %broadcast_in_dim.61), calls=%async_computation | async-start | bytes 131072 | tf_op jit(solution)/shard_map/all_to_all | solution.py:25
  22.1 9.1 %all-to-all-done = f32[16,2,512]{2,1,0:T(2,128)S(1)} async-done(((f32[16,2,512]{2,1,0:T(2,128)}), f32[16,2,512]{2,1,0:T(2,128)S(1)}, u32[]{:S(2)}, u32[]{:S(2)}) %all-to-all-start) | async-done | bytes 65568 | tf_op jit(solution)/shard_map/all_to_all | solution.py:25
  35.3 8.8 %collective-permute-done = bf16[2,256,256]{1,2,0:T(8,128)(2,1)S(1)} collective-permute-done((bf16[2,256,256]{1,2,0:T(8,128)(2,1)S(1)}, bf16[2,256,256]{1,2,0:T(8,128)(2,1)S(1)}, u32[]{:S(2)}, u32[]{:S(2)}) %collective-permute-start) | collective-permute-done | bytes 262176 | tf_op jit(solution)/shard_map/ppermute | solution.py:52
  44.1 1.3 collective-permute-start.5
  45.4 1.3 collective-permute-start.4
  46.8 1.3 collective-permute-start.3
  49.3 2.8 %collective-permute-done.4 = bf16[2,256,256]{1,2,0:T(8,128)(2,1)S(1)} collective-permute-done((bf16[2,256,256]{1,2,0:T(8,128)(2,1)S(1)}, bf16[2,256,256]{1,2,0:T(8,128)(2,1)S(1)}, u32[]{:S(2)}, u32[]{:S(2)}) %collective-permute-start.4) | collective-permute-done | bytes 262176 | tf_op jit(solution)/shard_map/ppermute | solution.py:52
  52.1 2.8 %collective-permute-done.3 = bf16[2,256,256]{1,2,0:T(8,128)(2,1)S(1)} collective-permute-done((bf16[2,256,256]{1,2,0:T(8,128)(2,1)S(1)}, bf16[2,256,256]{1,2,0:T(8,128)(2,1)S(1)}, u32[]{:S(2)}, u32[]{:S(2)}) %collective-permute-start.3) | collective-permute-done | bytes 262176 | tf_op jit(solution)/shard_map/ppermute | solution.py:52
  55.9 1.9 %collective-permute-start.6 = (bf16[2,768,256]{1,2,0:T(8,128)(2,1)}, bf16[2,768,256]{1,2,0:T(8,128)(2,1)S(1)}, u32[]{:S(2)}, u32[]{:S(2)}) collective-permute-start(bf16[2,768,256]{1,2,0:T(8,128)(2,1)} %pad_maximum_fusion.1), channel_id=1, source_target_pairs={{0,16},{16,32},{32,48},{48,64},{64,80},{80,96},{96,112},{112,128},... | collective-permute-start | bytes 2359304 | tf_op jit(solution)/shard_map/ppermute | solution.py:19
  61.3 10.9 %collective-permute-done.6 = bf16[2,768,256]{1,2,0:T(8,128)(2,1)S(1)} collective-permute-done((bf16[2,768,256]{1,2,0:T(8,128)(2,1)}, bf16[2,768,256]{1,2,0:T(8,128)(2,1)S(1)}, u32[]{:S(2)}, u32[]{:S(2)}) %collective-permute-start.6) | collective-permute-done | bytes 786464 | tf_op jit(solution)/shard_map/ppermute | solution.py:19
  84.9 3.8 %collective-permute-start.7 = (f32[2,2,256,256]{2,3,1,0:T(8,128)}, f32[2,2,256,256]{2,3,1,0:T(8,128)}, u32[]{:S(2)}, u32[]{:S(2)}) collective-permute-start(f32[2,2,256,256]{2,3,1,0:T(8,128)} %pad_maximum_fusion), channel_id=1, source_target_pairs={{16,0},{32,16},{48,32},{64,48},{80,64},{96,80},{112,96},{128,112},... | collective-permute-start | bytes 3145736 | tf_op jit(solution)/shard_map/ppermute | solution.py:19
  89.8 1.4 collective-permute-start.11
  92.6 1.5 collective-permute-start.9
  94.9 9.5 %collective-permute-done.11 = bf16[2,256,256]{1,2,0:T(8,128)(2,1)} collective-permute-done((bf16[2,256,256]{1,2,0:T(8,128)(2,1)}, bf16[2,256,256]{1,2,0:T(8,128)(2,1)}, u32[]{:S(2)}, u32[]{:S(2)}) %collective-permute-start.11) | collective-permute-done | bytes 262176 | tf_op jit(solution)/shard_map/ppermute | solution.py:67
  104.4 7.0 %collective-permute-done.9 = bf16[2,256,256]{1,2,0:T(8,128)(2,1)} collective-permute-done((bf16[2,256,256]{1,2,0:T(8,128)(2,1)}, bf16[2,256,256]{1,2,0:T(8,128)(2,1)}, u32[]{:S(2)}, u32[]{:S(2)}) %collective-permute-start.9) | collective-permute-done | bytes 262176 | tf_op jit(solution)/shard_map/ppermute | solution.py:67
  112.7 1.3 collective-permute-start.14
  114.0 1.4 collective-permute-start.13
  115.3 1.4 collective-permute-start.12
  117.5 3.5 %all-to-all-start.1 = ((f32[16,1,512]{2,1,0:T(1,128)}), f32[16,1,512]{2,1,0:T(1,128)S(1)}, u32[]{:S(2)}, u32[]{:S(2)}) async-start(f32[16,1,512]{2,1,0:T(1,128)} %broadcast_in_dim.106), calls=%async_computation.1 | async-start | bytes 65536 | tf_op jit(solution)/shard_map/all_to_all | solution.py:25
  123.5 10.1 %all-to-all-done.1 = f32[16,1,512]{2,1,0:T(1,128)S(1)} async-done(((f32[16,1,512]{2,1,0:T(1,128)}), f32[16,1,512]{2,1,0:T(1,128)S(1)}, u32[]{:S(2)}, u32[]{:S(2)}) %all-to-all-start.1) | async-done | bytes 32800 | tf_op jit(solution)/shard_map/all_to_all | solution.py:25
  133.7 1.6 %convert_add_fusion = f32[2,256,256]{1,2,0:T(8,128)S(1)} fusion(bf16[2,256,256]{1,2,0:T(8,128)(2,1)S(1)} %collective-permute-done.14, bf16[2,256,256]{1,2,0:T(8,128)(2,1)} %collective-permute-done.13, bf16[2,256,256]{1,2,0:T(8,128)(2,1)} %collective-permute-done.12, bf16[2,256,256]{1,2,0:T(8,128)(2,1)} %collective-permute-done.11, ...), kind=kLoop, calls=%fused_computation.55 | loop fusion | flops 1966080 | bytes 2883584 | tf_op jit(solution)/shard_map/add | solution.py:68
  135.3 1.3 fusion.24
  137.7 3.5 %all-to-all-start.2 = ((f32[16,1,512]{2,1,0:T(1,128)}), f32[16,1,512]{2,1,0:T(1,128)S(1)}, u32[]{:S(2)}, u32[]{:S(2)}) async-start(f32[16,1,512]{2,1,0:T(1,128)} %broadcast_in_dim.108), calls=%async_computation.2 | async-start | bytes 65536 | tf_op jit(solution)/shard_map/all_to_all | solution.py:25
  143.1 10.8 %all-to-all-done.2 = f32[16,1,512]{2,1,0:T(1,128)S(1)} async-done(((f32[16,1,512]{2,1,0:T(1,128)}), f32[16,1,512]{2,1,0:T(1,128)S(1)}, u32[]{:S(2)}, u32[]{:S(2)}) %all-to-all-start.2) | async-done | bytes 32800 | tf_op jit(solution)/shard_map/all_to_all | solution.py:25
  (155 shorter events, 39.4 us)
Async XLA Ops:
  0.6 47.4 %copy-start.20 = (s32[64]{0:T(128)S(1)}, s32[64]{0:T(128)}, u32[]{:S(2)}) copy-start(s32[64]{0:T(128)} %param.18) | copy-start | bytes 772
  0.6 34.4 %copy-start.19 = (s32[2]{0:T(128)S(1)}, s32[2]{0:T(128)}, u32[]{:S(2)}) copy-start(s32[2]{0:T(128)} %param.19) | copy-start | bytes 28
  0.7 47.5 %copy-start.10 = (f32[256]{0:T(256)S(1)}, f32[256]{0:T(256)}, u32[]{:S(2)}) copy-start(f32[256]{0:T(256)} %param.16) | copy-start | bytes 3076
  0.7 34.4 %copy-start.5 = (bf16[512,256]{1,0:T(8,128)(2,1)S(1)}, bf16[512,256]{1,0:T(8,128)(2,1)}, u32[]{:S(2)}) copy-start(bf16[512,256]{1,0:T(8,128)(2,1)} %param.17) | copy-start | bytes 786436
  2.6 28.6 %all-to-all-start = ((f32[16,2,512]{2,1,0:T(2,128)}), f32[16,2,512]{2,1,0:T(2,128)S(1)}, u32[]{:S(2)}, u32[]{:S(2)}) async-start(f32[16,2,512]{2,1,0:T(2,128)} %broadcast_in_dim.61), calls=%async_computation | async-start | bytes 131072 | tf_op jit(solution)/shard_map/all_to_all | solution.py:25
  32.1 26.5 %copy-start.3 = (bf16[512,256]{1,0:T(8,128)(2,1)S(1)}, bf16[512,256]{1,0:T(8,128)(2,1)}, u32[]{:S(2)}) copy-start(bf16[512,256]{1,0:T(8,128)(2,1)} %param.14) | copy-start | bytes 786436
  32.2 3.1 %collective-permute-start.2 = (bf16[2,256,256]{1,2,0:T(8,128)(2,1)S(1)}, bf16[2,256,256]{1,2,0:T(8,128)(2,1)S(1)}, u32[]{:S(2)}, u32[]{:S(2)}) collective-permute-start(bf16[2,256,256]{1,2,0:T(8,128)(2,1)S(1)} %pad_maximum_fusion.5), channel_id=1, source_target_pairs={{0,128},{1,129},{2,130},{3,131},{4,132},{5,133},{6,134},{7,135},{8... | collective-permute-start | bytes 786440 | tf_op jit(solution)/shard_map/ppermute | solution.py:52
  33.0 2.2 %collective-permute-start.1 = (bf16[2,256,256]{1,2,0:T(8,128)(2,1)S(1)}, bf16[2,256,256]{1,2,0:T(8,128)(2,1)S(1)}, u32[]{:S(2)}, u32[]{:S(2)}) collective-permute-start(bf16[2,256,256]{1,2,0:T(8,128)(2,1)S(1)} %pad_maximum_fusion.5), channel_id=1, source_target_pairs={{0,256},{1,257},{2,258},{3,259},{4,260},{5,261},{6,262},{7,263},{8... | collective-permute-start | bytes 786440 | tf_op jit(solution)/shard_map/ppermute | solution.py:52
  33.7 10.4 %collective-permute-start = (bf16[2,256,256]{1,2,0:T(8,128)(2,1)S(1)}, bf16[2,256,256]{1,2,0:T(8,128)(2,1)S(1)}, u32[]{:S(2)}, u32[]{:S(2)}) collective-permute-start(bf16[2,256,256]{1,2,0:T(8,128)(2,1)S(1)} %pad_maximum_fusion.5), channel_id=1, source_target_pairs={{0,384},{1,385},{2,386},{3,387},{4,388},{5,389},{6,390},{7,391},{8... | collective-permute-start | bytes 786440 | tf_op jit(solution)/shard_map/ppermute | solution.py:52
  44.1 5.2 %collective-permute-start.5 = (bf16[2,256,256]{1,2,0:T(8,128)(2,1)S(1)}, bf16[2,256,256]{1,2,0:T(8,128)(2,1)S(1)}, u32[]{:S(2)}, u32[]{:S(2)}) collective-permute-start(bf16[2,256,256]{1,2,0:T(8,128)(2,1)S(1)} %select_select_fusion.1), channel_id=1, source_target_pairs={{0,32},{128,160},{256,288},{384,416},{1,33},{129,161},{257,289},{3... | collective-permute-start | bytes 786440 | tf_op jit(solution)/shard_map/ppermute | solution.py:52
  45.4 6.7 %collective-permute-start.4 = (bf16[2,256,256]{1,2,0:T(8,128)(2,1)S(1)}, bf16[2,256,256]{1,2,0:T(8,128)(2,1)S(1)}, u32[]{:S(2)}, u32[]{:S(2)}) collective-permute-start(bf16[2,256,256]{1,2,0:T(8,128)(2,1)S(1)} %select_select_fusion.1), channel_id=1, source_target_pairs={{0,64},{128,192},{256,320},{384,448},{1,65},{129,193},{257,321},{3... | collective-permute-start | bytes 786440 | tf_op jit(solution)/shard_map/ppermute | solution.py:52
  46.8 8.2 %collective-permute-start.3 = (bf16[2,256,256]{1,2,0:T(8,128)(2,1)S(1)}, bf16[2,256,256]{1,2,0:T(8,128)(2,1)S(1)}, u32[]{:S(2)}, u32[]{:S(2)}) collective-permute-start(bf16[2,256,256]{1,2,0:T(8,128)(2,1)S(1)} %select_select_fusion.1), channel_id=1, source_target_pairs={{0,96},{128,224},{256,352},{384,480},{1,97},{129,225},{257,353},{3... | collective-permute-start | bytes 786440 | tf_op jit(solution)/shard_map/ppermute | solution.py:52
  55.9 16.2 %collective-permute-start.6 = (bf16[2,768,256]{1,2,0:T(8,128)(2,1)}, bf16[2,768,256]{1,2,0:T(8,128)(2,1)S(1)}, u32[]{:S(2)}, u32[]{:S(2)}) collective-permute-start(bf16[2,768,256]{1,2,0:T(8,128)(2,1)} %pad_maximum_fusion.1), channel_id=1, source_target_pairs={{0,16},{16,32},{32,48},{48,64},{64,80},{80,96},{96,112},{112,128},... | collective-permute-start | bytes 2359304 | tf_op jit(solution)/shard_map/ppermute | solution.py:19
  81.3 7.8 %collective-permute-start.8 = (bf16[2,256,256]{1,2,0:T(8,128)(2,1)S(1)}, bf16[2,256,256]{1,2,0:T(8,128)(2,1)S(1)}, u32[]{:S(2)}, u32[]{:S(2)}) collective-permute-start(bf16[2,256,256]{1,2,0:T(8,128)(2,1)S(1)} %fusion.26), channel_id=1, source_target_pairs={{16,0},{48,32},{80,64},{112,96},{144,128},{176,160},{208,192},{240... | collective-permute-start | bytes 786440 | tf_op jit(solution)/shard_map/ppermute | solution.py:67
  84.9 50.4 %collective-permute-start.7 = (f32[2,2,256,256]{2,3,1,0:T(8,128)}, f32[2,2,256,256]{2,3,1,0:T(8,128)}, u32[]{:S(2)}, u32[]{:S(2)}) collective-permute-start(f32[2,2,256,256]{2,3,1,0:T(8,128)} %pad_maximum_fusion), channel_id=1, source_target_pairs={{16,0},{32,16},{48,32},{64,48},{80,64},{96,80},{112,96},{128,112},... | collective-permute-start | bytes 3145736 | tf_op jit(solution)/shard_map/ppermute | solution.py:19
  89.8 26.9 %copy-start.13 = (f32[256]{0:T(256)S(1)}, f32[256]{0:T(256)}, u32[]{:S(2)}) copy-start(f32[256]{0:T(256)} %param.15) | copy-start | bytes 3076
  89.8 14.6 %collective-permute-start.11 = (bf16[2,256,256]{1,2,0:T(8,128)(2,1)}, bf16[2,256,256]{1,2,0:T(8,128)(2,1)}, u32[]{:S(2)}, u32[]{:S(2)}) collective-permute-start(bf16[2,256,256]{1,2,0:T(8,128)(2,1)} %fusion.28), channel_id=1, source_target_pairs={{96,0},{224,128},{352,256},{480,384},{97,1},{225,129},{353,257},{4... | collective-permute-start | bytes 786440 | tf_op jit(solution)/shard_map/ppermute | solution.py:67
  91.3 13.2 %collective-permute-start.10 = (bf16[2,256,256]{1,2,0:T(8,128)(2,1)}, bf16[2,256,256]{1,2,0:T(8,128)(2,1)}, u32[]{:S(2)}, u32[]{:S(2)}) collective-permute-start(bf16[2,256,256]{1,2,0:T(8,128)(2,1)} %fusion.28), channel_id=1, source_target_pairs={{64,0},{192,128},{320,256},{448,384},{65,1},{193,129},{321,257},{4... | collective-permute-start | bytes 786440 | tf_op jit(solution)/shard_map/ppermute | solution.py:67
  92.6 18.8 %collective-permute-start.9 = (bf16[2,256,256]{1,2,0:T(8,128)(2,1)}, bf16[2,256,256]{1,2,0:T(8,128)(2,1)}, u32[]{:S(2)}, u32[]{:S(2)}) collective-permute-start(bf16[2,256,256]{1,2,0:T(8,128)(2,1)} %fusion.28), channel_id=1, source_target_pairs={{32,0},{160,128},{288,256},{416,384},{33,1},{161,129},{289,257},{4... | collective-permute-start | bytes 786440 | tf_op jit(solution)/shard_map/ppermute | solution.py:67
  112.7 21.0 %collective-permute-start.14 = (bf16[2,256,256]{1,2,0:T(8,128)(2,1)S(1)}, bf16[2,256,256]{1,2,0:T(8,128)(2,1)S(1)}, u32[]{:S(2)}, u32[]{:S(2)}) collective-permute-start(bf16[2,256,256]{1,2,0:T(8,128)(2,1)S(1)} %fusion.77), channel_id=1, source_target_pairs={{384,0},{385,1},{386,2},{387,3},{388,4},{389,5},{390,6},{391,7},{3... | collective-permute-start | bytes 786440 | tf_op jit(solution)/shard_map/ppermute | solution.py:67
  114.0 19.7 %collective-permute-start.13 = (bf16[2,256,256]{1,2,0:T(8,128)(2,1)S(1)}, bf16[2,256,256]{1,2,0:T(8,128)(2,1)}, u32[]{:S(2)}, u32[]{:S(2)}) collective-permute-start(bf16[2,256,256]{1,2,0:T(8,128)(2,1)S(1)} %fusion.77), channel_id=1, source_target_pairs={{256,0},{257,1},{258,2},{259,3},{260,4},{261,5},{262,6},{263,7},{2... | collective-permute-start | bytes 786440 | tf_op jit(solution)/shard_map/ppermute | solution.py:67
  115.3 18.4 %collective-permute-start.12 = (bf16[2,256,256]{1,2,0:T(8,128)(2,1)S(1)}, bf16[2,256,256]{1,2,0:T(8,128)(2,1)}, u32[]{:S(2)}, u32[]{:S(2)}) collective-permute-start(bf16[2,256,256]{1,2,0:T(8,128)(2,1)S(1)} %fusion.77), channel_id=1, source_target_pairs={{128,0},{129,1},{130,2},{131,3},{132,4},{133,5},{134,6},{135,7},{1... | collective-permute-start | bytes 786440 | tf_op jit(solution)/shard_map/ppermute | solution.py:67
  117.5 16.1 %all-to-all-start.1 = ((f32[16,1,512]{2,1,0:T(1,128)}), f32[16,1,512]{2,1,0:T(1,128)S(1)}, u32[]{:S(2)}, u32[]{:S(2)}) async-start(f32[16,1,512]{2,1,0:T(1,128)} %broadcast_in_dim.106), calls=%async_computation.1 | async-start | bytes 65536 | tf_op jit(solution)/shard_map/all_to_all | solution.py:25
  137.7 16.1 %all-to-all-start.2 = ((f32[16,1,512]{2,1,0:T(1,128)}), f32[16,1,512]{2,1,0:T(1,128)S(1)}, u32[]{:S(2)}, u32[]{:S(2)}) async-start(f32[16,1,512]{2,1,0:T(1,128)} %broadcast_in_dim.108), calls=%async_computation.2 | async-start | bytes 65536 | tf_op jit(solution)/shard_map/all_to_all | solution.py:25
  (15 other events, 116.9 us)

commit v12 on v10

--- a/solution.py
+++ b/solution.py
@@ -56,9 +56,9 @@
     return values
 
 
-def tree_reduce(values, axis, wire, first=0):
+def tree_reduce(values, axis, wire, first=0, last=None):
     n = lax.axis_size(axis)
-    for step, fan in tree_plan(n)[first:]:
+    for step, fan in tree_plan(n)[first:last]:
         span = step * fan
         total = values
         for j in range(1, fan):
@@ -193,10 +193,16 @@
     grad_v_near = fold_offsets(from_heads(grad_vh), F_DEV, F_DEV, CAP)
     grad_k_anchor = grad_ka.transpose(1, 0, 2).reshape(CAP, local_width)
     grad_v_anchor = grad_va.transpose(1, 0, 2).reshape(CAP, local_width)
-    back_k, back_v = shifted(jnp.stack([grad_k_near[:F_DEV], grad_v_near[:F_DEV]]), "seq", -1)
+    anchor_grads = tree_reduce(
+        jnp.stack([grad_k_anchor, grad_v_anchor]), "seq", jnp.bfloat16, last=2
+    )
+    back, anchor_grads = lax.optimization_barrier(
+        (jnp.stack([grad_k_near[:F_DEV], grad_v_near[:F_DEV]]), anchor_grads)
+    )
+    anchor_gk, anchor_gv = tree_reduce(anchor_grads, "seq", jnp.bfloat16, first=2)
+    back_k, back_v = shifted(back, "seq", -1)
     grad_k_own = grad_k_near[F_DEV:] + back_k
     grad_v_own = grad_v_near[F_DEV:] + back_v
-    anchor_gk, anchor_gv = tree_reduce(jnp.stack([grad_k_anchor, grad_v_anchor]), "seq", jnp.bfloat16)
     first_device = device == 0
     grad_k_own = grad_k_own.at[0].add(jnp.where(first_device, anchor_gk, 0.0))
     grad_v_own = grad_v_own.at[0].add(jnp.where(first_device, anchor_gv, 0.0))

time: 135 us -> 137 us (1.015)
  waiting for transfers between devices: 55.2 us -> 59.9 us
    ppermute x7, waiting for transfers between devices: 27.4 us -> 32.4 us  [tree_reduce(): arrived = lax.ppermute(sent, axis, route)]
    unnamed x47 -> x33, local copies, waits for them, and re-layouts: 4.89 us -> 4.85 us
  transfers between devices with their start and end apart: 17 -> 17, of which waited for: 12 -> 12; matrix products, arithmetic and copies ran while one was open for 12% -> 10% of each run, Pallas kernels for 0% -> 0%
where the time goes in v12:
time: 137 us; the launch traced here: 136 us
  waiting for transfers between devices  59.9 us (44%)
  starting transfers between devices  43.5 us (32%)
  local copies, waits for them, and re-layouts  12.2 us (9%)
  other arithmetic  11.5 us (8%)
  matrix products  7.42 us (5%)
  between operations  1.48 us (1%)
    ppermute x7, waiting for transfers between devices, tree_reduce(): arrived = lax.ppermute(sent, axis, route)  32.4 us
    all_to_all x2, starting transfers between devices, gather_sum(): return jnp.sum(lax.all_to_all(copies, axis, 0, 0, tiled=False), axis=0)  20.8 us
    all_to_all x2, waiting for transfers between devices, gather_sum(): return jnp.sum(lax.all_to_all(copies, axis, 0, 0, tiled=False), axis=0)  17.5 us
    ppermute x6, starting transfers between devices, tree_bcast(): arrived = lax.ppermute(values, axis, route)  10.8 us
    ppermute x7, starting transfers between devices, tree_reduce(): arrived = lax.ppermute(sent, axis, route)  9.21 us
    ppermute x6, waiting for transfers between devices, tree_bcast(): arrived = lax.ppermute(values, axis, route)  9.19 us
    unnamed x33, local copies, waits for them, and re-layouts  4.85 us
    concatenate x12, local copies, waits for them, and re-layouts, stack_offsets(): return jnp.concatenate(blocks, axis=1)  2.77 us
  transfers between devices with their start and end apart: 17, of which 12 were waited for; matrix products, arithmetic and copies ran while one was open for 10% of the time, Pallas kernels for 0%

profile of v12, /device:TPU:8, one launch (start us, length us, event | category | flops | bytes accessed | tf_op | source)
XLA Modules:
  0.0 136.0 jit_solution(5194523667800669204)
XLA Ops:
  0.7 1.3 multiply_reduce_fusion.1
  2.7 16.0 %all-to-all-start = ((f32[16,2,512]{2,1,0:T(2,128)}), f32[16,2,512]{2,1,0:T(2,128)S(1)}, u32[]{:S(2)}, u32[]{:S(2)}) async-start(f32[16,2,512]{2,1,0:T(2,128)} %broadcast_in_dim.58), calls=%async_computation | async-start | bytes 131072 | tf_op jit(solution)/shard_map/all_to_all | solution.py:25
  22.5 7.8 %all-to-all-done = f32[16,2,512]{2,1,0:T(2,128)S(1)} async-done(((f32[16,2,512]{2,1,0:T(2,128)}), f32[16,2,512]{2,1,0:T(2,128)S(1)}, u32[]{:S(2)}, u32[]{:S(2)}) %all-to-all-start) | async-done | bytes 65568 | tf_op jit(solution)/shard_map/all_to_all | solution.py:25
  31.1 3.4 %collective-permute-start.2 = (bf16[2,256,256]{1,2,0:T(8,128)(2,1)S(1)}, bf16[2,256,256]{1,2,0:T(8,128)(2,1)S(1)}, u32[]{:S(2)}, u32[]{:S(2)}) collective-permute-start(bf16[2,256,256]{1,2,0:T(8,128)(2,1)S(1)} %pad_maximum_fusion.5), channel_id=1, source_target_pairs={{0,128},{1,129},{2,130},{3,131},{4,132},{5,133},{6,134},{7,135},{8... | collective-permute-start | bytes 786440 | tf_op jit(solution)/shard_map/ppermute | solution.py:52
  34.6 2.2 %collective-permute-start.1 = (bf16[2,256,256]{1,2,0:T(8,128)(2,1)S(1)}, bf16[2,256,256]{1,2,0:T(8,128)(2,1)S(1)}, u32[]{:S(2)}, u32[]{:S(2)}) collective-permute-start(bf16[2,256,256]{1,2,0:T(8,128)(2,1)S(1)} %pad_maximum_fusion.5), channel_id=1, source_target_pairs={{0,256},{1,257},{2,258},{3,259},{4,260},{5,261},{6,262},{7,263},{8... | collective-permute-start | bytes 786440 | tf_op jit(solution)/shard_map/ppermute | solution.py:52
  36.8 1.3 collective-permute-start
  38.4 2.8 %collective-permute-done.1 = bf16[2,256,256]{1,2,0:T(8,128)(2,1)S(1)} collective-permute-done((bf16[2,256,256]{1,2,0:T(8,128)(2,1)S(1)}, bf16[2,256,256]{1,2,0:T(8,128)(2,1)S(1)}, u32[]{:S(2)}, u32[]{:S(2)}) %collective-permute-start.1) | collective-permute-done | bytes 262176 | tf_op jit(solution)/shard_map/ppermute | solution.py:52
  42.0 1.3 collective-permute-start.5
  43.3 1.3 collective-permute-start.4
  44.6 1.3 collective-permute-start.3
  47.2 2.8 %collective-permute-done.4 = bf16[2,256,256]{1,2,0:T(8,128)(2,1)S(1)} collective-permute-done((bf16[2,256,256]{1,2,0:T(8,128)(2,1)S(1)}, bf16[2,256,256]{1,2,0:T(8,128)(2,1)S(1)}, u32[]{:S(2)}, u32[]{:S(2)}) %collective-permute-start.4) | collective-permute-done | bytes 262176 | tf_op jit(solution)/shard_map/ppermute | solution.py:52
  50.0 2.8 %collective-permute-done.3 = bf16[2,256,256]{1,2,0:T(8,128)(2,1)S(1)} collective-permute-done((bf16[2,256,256]{1,2,0:T(8,128)(2,1)S(1)}, bf16[2,256,256]{1,2,0:T(8,128)(2,1)S(1)}, u32[]{:S(2)}, u32[]{:S(2)}) %collective-permute-start.3) | collective-permute-done | bytes 262176 | tf_op jit(solution)/shard_map/ppermute | solution.py:52
  53.8 1.3 collective-permute-start.6
  68.8 4.5 %collective-permute-done.7 = bf16[2,256,256]{1,2,0:T(8,128)(2,1)S(1)} collective-permute-done((bf16[2,256,256]{1,2,0:T(8,128)(2,1)S(1)}, bf16[2,256,256]{1,2,0:T(8,128)(2,1)S(1)}, u32[]{:S(2)}, u32[]{:S(2)}) %collective-permute-start.7) | collective-permute-done | bytes 262176 | tf_op jit(solution)/shard_map/ppermute | solution.py:67
  73.4 1.3 collective-permute-start.10
  74.7 1.3 collective-permute-start.9
  78.4 11.6 %collective-permute-done.10 = bf16[2,256,256]{1,2,0:T(8,128)(2,1)S(1)} collective-permute-done((bf16[2,256,256]{1,2,0:T(8,128)(2,1)S(1)}, bf16[2,256,256]{1,2,0:T(8,128)(2,1)S(1)}, u32[]{:S(2)}, u32[]{:S(2)}) %collective-permute-start.10) | collective-permute-done | bytes 262176 | tf_op jit(solution)/shard_map/ppermute | solution.py:67
  90.7 1.3 collective-permute-start.11
  94.4 1.5 %collective-permute-start.13 = (bf16[2,256,256]{1,2,0:T(8,128)(2,1)}, bf16[2,256,256]{1,2,0:T(8,128)(2,1)}, u32[]{:S(2)}, u32[]{:S(2)}) collective-permute-start(bf16[2,256,256]{1,2,0:T(8,128)(2,1)} %convert_element_type.113), channel_id=1, source_target_pairs={{256,0},{257,1},{258,2},{259,3},{260,4},{261,5},{262,6},{263,7},{2... | collective-permute-start | bytes 786440 | tf_op jit(solution)/shard_map/ppermute | solution.py:67
  95.9 1.3 collective-permute-start.12
  98.2 15.6 %collective-permute-done.14 = bf16[2,256,256]{1,2,0:T(8,128)(2,1)} collective-permute-done((bf16[2,256,256]{1,2,0:T(8,128)(2,1)}, bf16[2,256,256]{1,2,0:T(8,128)(2,1)}, u32[]{:S(2)}, u32[]{:S(2)}) %collective-permute-start.14) | collective-permute-done | bytes 262176 | tf_op jit(solution)/shard_map/ppermute | solution.py:67
  115.1 1.3 fusion.24
  117.5 4.8 %all-to-all-start.1 = ((f32[16,2,512]{2,1,0:T(2,128)}), f32[16,2,512]{2,1,0:T(2,128)S(1)}, u32[]{:S(2)}, u32[]{:S(2)}) async-start(f32[16,2,512]{2,1,0:T(2,128)} %broadcast_in_dim.103), calls=%async_computation.1 | async-start | bytes 131072 | tf_op jit(solution)/shard_map/all_to_all | solution.py:25
  124.2 9.8 %all-to-all-done.1 = f32[16,2,512]{2,1,0:T(2,128)S(1)} async-done(((f32[16,2,512]{2,1,0:T(2,128)}), f32[16,2,512]{2,1,0:T(2,128)S(1)}, u32[]{:S(2)}, u32[]{:S(2)}) %all-to-all-start.1) | async-done | bytes 65568 | tf_op jit(solution)/shard_map/all_to_all | solution.py:25
  (138 shorter events, 34.5 us)
Async XLA Ops:
  0.6 45.4 %copy-start.2 = (bf16[512,256]{1,0:T(8,128)(2,1)S(1)}, bf16[512,256]{1,0:T(8,128)(2,1)}, u32[]{:S(2)}) copy-start(bf16[512,256]{1,0:T(8,128)(2,1)} %param.12) | copy-start | bytes 786436
  0.6 37.4 %copy-start.12 = (s32[64]{0:T(128)S(1)}, s32[64]{0:T(128)}, u32[]{:S(2)}) copy-start(s32[64]{0:T(128)} %param.18) | copy-start | bytes 772
  0.7 45.5 %copy-start.3 = (bf16[512,256]{1,0:T(8,128)(2,1)S(1)}, bf16[512,256]{1,0:T(8,128)(2,1)}, u32[]{:S(2)}) copy-start(bf16[512,256]{1,0:T(8,128)(2,1)} %param.14) | copy-start | bytes 786436
  0.7 37.5 %copy-start.4 = (bf16[512,256]{1,0:T(8,128)(2,1)S(1)}, bf16[512,256]{1,0:T(8,128)(2,1)}, u32[]{:S(2)}) copy-start(bf16[512,256]{1,0:T(8,128)(2,1)} %param.17) | copy-start | bytes 786436
  2.7 27.6 %all-to-all-start = ((f32[16,2,512]{2,1,0:T(2,128)}), f32[16,2,512]{2,1,0:T(2,128)S(1)}, u32[]{:S(2)}, u32[]{:S(2)}) async-start(f32[16,2,512]{2,1,0:T(2,128)} %broadcast_in_dim.58), calls=%async_computation | async-start | bytes 131072 | tf_op jit(solution)/shard_map/all_to_all | solution.py:25
  19.8 27.3 %copy-start.9 = (f32[256]{0:T(256)S(1)}, f32[256]{0:T(256)}, u32[]{:S(2)}) copy-start(f32[256]{0:T(256)} %param.16) | copy-start | bytes 3076
  31.1 7.3 %collective-permute-start.2 = (bf16[2,256,256]{1,2,0:T(8,128)(2,1)S(1)}, bf16[2,256,256]{1,2,0:T(8,128)(2,1)S(1)}, u32[]{:S(2)}, u32[]{:S(2)}) collective-permute-start(bf16[2,256,256]{1,2,0:T(8,128)(2,1)S(1)} %pad_maximum_fusion.5), channel_id=1, source_target_pairs={{0,128},{1,129},{2,130},{3,131},{4,132},{5,133},{6,134},{7,135},{8... | collective-permute-start | bytes 786440 | tf_op jit(solution)/shard_map/ppermute | solution.py:52
  34.6 6.7 %collective-permute-start.1 = (bf16[2,256,256]{1,2,0:T(8,128)(2,1)S(1)}, bf16[2,256,256]{1,2,0:T(8,128)(2,1)S(1)}, u32[]{:S(2)}, u32[]{:S(2)}) collective-permute-start(bf16[2,256,256]{1,2,0:T(8,128)(2,1)S(1)} %pad_maximum_fusion.5), channel_id=1, source_target_pairs={{0,256},{1,257},{2,258},{3,259},{4,260},{5,261},{6,262},{7,263},{8... | collective-permute-start | bytes 786440 | tf_op jit(solution)/shard_map/ppermute | solution.py:52
  36.8 5.2 %collective-permute-start = (bf16[2,256,256]{1,2,0:T(8,128)(2,1)S(1)}, bf16[2,256,256]{1,2,0:T(8,128)(2,1)S(1)}, u32[]{:S(2)}, u32[]{:S(2)}) collective-permute-start(bf16[2,256,256]{1,2,0:T(8,128)(2,1)S(1)} %pad_maximum_fusion.5), channel_id=1, source_target_pairs={{0,384},{1,385},{2,386},{3,387},{4,388},{5,389},{6,390},{7,391},{8... | collective-permute-start | bytes 786440 | tf_op jit(solution)/shard_map/ppermute | solution.py:52
  42.0 5.2 %collective-permute-start.5 = (bf16[2,256,256]{1,2,0:T(8,128)(2,1)S(1)}, bf16[2,256,256]{1,2,0:T(8,128)(2,1)S(1)}, u32[]{:S(2)}, u32[]{:S(2)}) collective-permute-start(bf16[2,256,256]{1,2,0:T(8,128)(2,1)S(1)} %select_select_fusion.1), channel_id=1, source_target_pairs={{0,32},{128,160},{256,288},{384,416},{1,33},{129,161},{257,289},{3... | collective-permute-start | bytes 786440 | tf_op jit(solution)/shard_map/ppermute | solution.py:52
  43.3 6.7 %collective-permute-start.4 = (bf16[2,256,256]{1,2,0:T(8,128)(2,1)S(1)}, bf16[2,256,256]{1,2,0:T(8,128)(2,1)S(1)}, u32[]{:S(2)}, u32[]{:S(2)}) collective-permute-start(bf16[2,256,256]{1,2,0:T(8,128)(2,1)S(1)} %select_select_fusion.1), channel_id=1, source_target_pairs={{0,64},{128,192},{256,320},{384,448},{1,65},{129,193},{257,321},{3... | collective-permute-start | bytes 786440 | tf_op jit(solution)/shard_map/ppermute | solution.py:52
  44.6 8.2 %collective-permute-start.3 = (bf16[2,256,256]{1,2,0:T(8,128)(2,1)S(1)}, bf16[2,256,256]{1,2,0:T(8,128)(2,1)S(1)}, u32[]{:S(2)}, u32[]{:S(2)}) collective-permute-start(bf16[2,256,256]{1,2,0:T(8,128)(2,1)S(1)} %select_select_fusion.1), channel_id=1, source_target_pairs={{0,96},{128,224},{256,352},{384,480},{1,97},{129,225},{257,353},{3... | collective-permute-start | bytes 786440 | tf_op jit(solution)/shard_map/ppermute | solution.py:52
  53.8 3.4 %collective-permute-start.6 = (bf16[2,768,256]{1,2,0:T(8,128)(2,1)}, bf16[2,768,256]{1,2,0:T(8,128)(2,1)S(1)}, u32[]{:S(2)}, u32[]{:S(2)}) collective-permute-start(bf16[2,768,256]{1,2,0:T(8,128)(2,1)} %pad_maximum_fusion.1), channel_id=1, source_target_pairs={{0,16},{16,32},{32,48},{48,64},{64,80},{80,96},{96,112},{112,128},... | collective-permute-start | bytes 2359304 | tf_op jit(solution)/shard_map/ppermute | solution.py:19
  66.3 7.0 %collective-permute-start.7 = (bf16[2,256,256]{1,2,0:T(8,128)(2,1)S(1)}, bf16[2,256,256]{1,2,0:T(8,128)(2,1)S(1)}, u32[]{:S(2)}, u32[]{:S(2)}) collective-permute-start(bf16[2,256,256]{1,2,0:T(8,128)(2,1)S(1)} %fusion.26), channel_id=1, source_target_pairs={{16,0},{48,32},{80,64},{112,96},{144,128},{176,160},{208,192},{240... | collective-permute-start | bytes 786440 | tf_op jit(solution)/shard_map/ppermute | solution.py:67
  68.7 21.8 %copy-start = (f32[4,256,256]{1,2,0:T(8,128)}, f32[4,256,256]{1,2,0:T(8,128)S(1)}, u32[]{:S(2)}) copy-start(f32[4,256,256]{1,2,0:T(8,128)S(1)} %pad_add_fusion.1) | copy-start | bytes 3145732
  73.4 16.6 %collective-permute-start.10 = (bf16[2,256,256]{1,2,0:T(8,128)(2,1)S(1)}, bf16[2,256,256]{1,2,0:T(8,128)(2,1)S(1)}, u32[]{:S(2)}, u32[]{:S(2)}) collective-permute-start(bf16[2,256,256]{1,2,0:T(8,128)(2,1)S(1)} %fusion.28), channel_id=1, source_target_pairs={{96,0},{224,128},{352,256},{480,384},{97,1},{225,129},{353,257},{4... | collective-permute-start | bytes 786440 | tf_op jit(solution)/shard_map/ppermute | solution.py:67
  74.7 15.9 %collective-permute-start.9 = (bf16[2,256,256]{1,2,0:T(8,128)(2,1)S(1)}, bf16[2,256,256]{1,2,0:T(8,128)(2,1)S(1)}, u32[]{:S(2)}, u32[]{:S(2)}) collective-permute-start(bf16[2,256,256]{1,2,0:T(8,128)(2,1)S(1)} %fusion.28), channel_id=1, source_target_pairs={{64,0},{192,128},{320,256},{448,384},{65,1},{193,129},{321,257},{4... | collective-permute-start | bytes 786440 | tf_op jit(solution)/shard_map/ppermute | solution.py:67
  76.0 14.6 %collective-permute-start.8 = (bf16[2,256,256]{1,2,0:T(8,128)(2,1)S(1)}, bf16[2,256,256]{1,2,0:T(8,128)(2,1)S(1)}, u32[]{:S(2)}, u32[]{:S(2)}) collective-permute-start(bf16[2,256,256]{1,2,0:T(8,128)(2,1)S(1)} %fusion.28), channel_id=1, source_target_pairs={{32,0},{160,128},{288,256},{416,384},{33,1},{161,129},{289,257},{4... | collective-permute-start | bytes 786440 | tf_op jit(solution)/shard_map/ppermute | solution.py:67
  77.3 19.9 %copy-start.7 = (bf16[2,256,2,128]{3,1,0,2:T(8,128)(2,1)S(1)}, bf16[2,256,2,128]{3,1,0,2:T(8,128)(2,1)}, u32[]{:S(2)}) copy-start(bf16[2,256,2,128]{3,1,0,2:T(8,128)(2,1)} %copy-done.6) | copy-start | bytes 786436
  90.7 24.4 %collective-permute-start.11 = (f32[2,2,256,256]{2,3,1,0:T(8,128)}, f32[2,2,256,256]{2,3,1,0:T(8,128)}, u32[]{:S(2)}, u32[]{:S(2)}) collective-permute-start(f32[2,2,256,256]{2,3,1,0:T(8,128)} %pad_maximum_fusion), channel_id=1, source_target_pairs={{16,0},{32,16},{48,32},{64,48},{80,64},{96,80},{112,96},{128,112},... | collective-permute-start | bytes 3145736 | tf_op jit(solution)/shard_map/ppermute | solution.py:19
  93.1 20.8 %collective-permute-start.14 = (bf16[2,256,256]{1,2,0:T(8,128)(2,1)}, bf16[2,256,256]{1,2,0:T(8,128)(2,1)}, u32[]{:S(2)}, u32[]{:S(2)}) collective-permute-start(bf16[2,256,256]{1,2,0:T(8,128)(2,1)} %convert_element_type.113), channel_id=1, source_target_pairs={{384,0},{385,1},{386,2},{387,3},{388,4},{389,5},{390,6},{391,7},{3... | collective-permute-start | bytes 786440 | tf_op jit(solution)/shard_map/ppermute | solution.py:67
  94.4 19.5 %collective-permute-start.13 = (bf16[2,256,256]{1,2,0:T(8,128)(2,1)}, bf16[2,256,256]{1,2,0:T(8,128)(2,1)}, u32[]{:S(2)}, u32[]{:S(2)}) collective-permute-start(bf16[2,256,256]{1,2,0:T(8,128)(2,1)} %convert_element_type.113), channel_id=1, source_target_pairs={{256,0},{257,1},{258,2},{259,3},{260,4},{261,5},{262,6},{263,7},{2... | collective-permute-start | bytes 786440 | tf_op jit(solution)/shard_map/ppermute | solution.py:67
  95.9 18.0 %collective-permute-start.12 = (bf16[2,256,256]{1,2,0:T(8,128)(2,1)}, bf16[2,256,256]{1,2,0:T(8,128)(2,1)}, u32[]{:S(2)}, u32[]{:S(2)}) collective-permute-start(bf16[2,256,256]{1,2,0:T(8,128)(2,1)} %convert_element_type.113), channel_id=1, source_target_pairs={{128,0},{129,1},{130,2},{131,3},{132,4},{133,5},{134,6},{135,7},{1... | collective-permute-start | bytes 786440 | tf_op jit(solution)/shard_map/ppermute | solution.py:67
  117.5 16.5 %all-to-all-start.1 = ((f32[16,2,512]{2,1,0:T(2,128)}), f32[16,2,512]{2,1,0:T(2,128)S(1)}, u32[]{:S(2)}, u32[]{:S(2)}) async-start(f32[16,2,512]{2,1,0:T(2,128)} %broadcast_in_dim.103), calls=%async_computation.1 | async-start | bytes 131072 | tf_op jit(solution)/shard_map/all_to_all | solution.py:25
  (6 other events, 51.9 us)
